TPU v7x, 32 devices: a whole 2x2x4 slice. The times are simulated.
32 devices in a mesh: tok: 4 (over y, x), ka: 4 (over z), out: 2 (over core).
Axes of the slice: x: 2, y: 2, z: 4, core: 2. Of those that a mesh axis runs over, the one named last changes fastest.
Arguments:
- features: bfloat16 [1024, 12288], P('tok', ('ka', 'out')), may hold values from -12 to 12, as said below
- lengths: int32 [4], P('tok'), may hold values from 1 to 256, 768 in all
- w_qkv: bfloat16 [12288, 24576], P(('ka', 'tok'), 'out'), may hold values from -0.0546875 to 0.0546875
- b_qkv: bfloat16 [24576], P(('out', 'ka')), may hold values from -2 to 2
- w_out: bfloat16 [8192, 12288], P(('out', 'tok'), 'ka'), may hold values from -0.0625 to 0.0625
- b_out: bfloat16 [12288], P(('ka', 'out')), may hold values from -3 to 3
Outputs:
- result: float32 [1024, 12288], P('tok', ('ka', 'out'))
Inputs may be any that keep to these rules, and one draw needn't show every extreme that they name: features: activations of order one; rows may differ in scale. `lengths`: live tokens of each prompt; some prompt is full.
All inputs are finite; a program needn't handle non-finite values. No bound on the sum of `lengths` on one device may be relied on, other than what follows from the above.
Results may differ from a plain program's by a relative error of at most 0.008.
Values may be sent and summed in bfloat16 or wider, within the bound.
No kernel may reach another device: no remote copies, remote signals or barrier semaphores. Data moves between devices by JAX's collectives and lax.ppermute only.
A program may use at most 192 MiB of HBM per device.

v0:
```python
import jax
import jax.numpy as jnp
from jax import lax
from jax.sharding import PartitionSpec as P

HD = 128
SEQ = 256


def softmax_rows(scores, allowed):
    scores = jnp.where(allowed, scores, -1e30)
    row_max = jnp.max(scores, axis=-1, keepdims=True)
    weights = jnp.exp(scores - row_max)
    row_sum = jnp.sum(weights, axis=-1, keepdims=True)
    return (weights / row_sum).astype(jnp.bfloat16)


def shards(features, lengths, w_qkv, b_qkv, w_out, b_out):
    row_count = features.shape[0]
    prompts = row_count // SEQ
    score_scale = 1.0 / HD**0.5
    panel = lax.all_gather(features, "out", axis=1, tiled=True)
    w_block = lax.all_gather(w_qkv, "tok", axis=0, tiled=True)
    partial_value = jnp.dot(panel, w_block, preferred_element_type=jnp.float32)
    qkv_sum = lax.psum_scatter(
        partial_value.astype(jnp.bfloat16), "ka", scatter_dimension=1, tiled=True
    ).astype(jnp.float32)
    qkv_held = (qkv_sum + b_qkv.astype(jnp.float32)).astype(jnp.bfloat16)
    heads_dev = qkv_held.shape[1] // (3 * HD)
    table = qkv_held.reshape(prompts, SEQ, heads_dev, 3, HD)
    positions = jnp.arange(SEQ)
    causal = positions[None, :] <= positions[:, None]
    live = positions[None, :] < lengths[:, None]
    allowed = causal[None, None] & live[:, None, None, :]
    scores = (
        jnp.einsum(
            "pshd,pthd->phst",
            table[:, :, :, 0],
            table[:, :, :, 1],
            preferred_element_type=jnp.float32,
        )
        * score_scale
    )
    prob_rows = softmax_rows(scores, allowed)
    context = jnp.einsum(
        "phst,pthd->pshd", prob_rows, table[:, :, :, 2], preferred_element_type=jnp.float32
    )
    context = context.astype(jnp.bfloat16).reshape(row_count, heads_dev * HD)
    head_group = lax.all_gather(context, "ka", axis=1, tiled=True)
    terms = jnp.dot(
        head_group,
        lax.all_gather(w_out, "tok", axis=0, tiled=True),
        preferred_element_type=jnp.float32,
    )
    summed = lax.psum_scatter(terms, "out", scatter_dimension=1, tiled=True)
    return summed + b_out.astype(jnp.float32)


def solution(mesh):
    placed = (
        P("tok", ("ka", "out")),
        P("tok"),
        P(("ka", "tok"), "out"),
        P(("out", "ka")),
        P(("out", "tok"), "ka"),
        P(("ka", "out")),
    )
    return jax.shard_map(
        shards, mesh=mesh, in_specs=placed, out_specs=P("tok", ("ka", "out")), check_vma=False
    )
```

profile of v0, /device:TPU:0, one launch (start us, length us, event | category | flops | bytes accessed | tf_op | source)
XLA Modules:
  0.0 1123.8 jit_solution(12351789201548837394)
XLA Ops:
  6.5 0.0 all-gather.5.cloned.1.call-start
  6.5 0.7 all-gather.5.cloned.1.call-update
  7.3 0.0 all-gather.7.cloned.1.call-start
  7.3 0.7 all-gather.7.cloned.1.call-update
  8.0 0.0 reduce-scatter.3.cloned.1.call-start
  8.1 13.4 %all-gather.5.cloned.1.call-done = bf16[256,3072]{1,0:T(8,128)(2,1)} async-done(((bf16[256,1536]{1,0:T(8,128)(2,1)}), bf16[256,3072]{1,0:T(8,128)(2,1)}) %all-gather.5.cloned.1.call-update) | async-done | bytes 1572880 | tf_op jit(solution)/shard_map/all_gather | solution.py:22
  21.4 650.2 %all-gather.7.cloned.1.call-done = bf16[3072,12288]{1,0:T(8,128)(2,1)} async-done(((bf16[768,12288]{1,0:T(8,128)(2,1)}), bf16[3072,12288]{1,0:T(8,128)(2,1)}) %all-gather.7.cloned.1.call-update) | async-done | bytes 75497488 | tf_op jit(solution)/shard_map/all_gather | solution.py:23
  671.6 31.1 %convolution_convert_fusion = bf16[256,12288]{1,0:T(8,128)(2,1)} fusion(bf16[256,3072]{1,0:T(8,128)(2,1)} %all-gather.5.cloned.1.call-done, bf16[3072,12288]{1,0:T(8,128)(2,1)} %all-gather.7.cloned.1.call-done), kind=kOutput, calls=%fused_computation.1 | convolution fusion | flops 19330498560 | bytes 83361792 | tf_op jit(solution)/shard_map/dot_general | solution.py:24
  702.7 0.0 reduce-scatter.3.cloned.1.call-update
  702.8 0.0 copy-start
  702.8 0.0 all-gather.11.cloned.1.call-start
  702.8 0.5 all-gather.11.cloned.1.call-update
  703.4 0.0 all-gather.9.cloned.1.call-start
  703.4 0.1 copy-done
  704.1 0.1 fusion.6
  704.2 109.4 %reduce-scatter.3.cloned.1.call-done = bf16[256,3072]{1,0:T(8,128)(2,1)} async-done(((bf16[256,12288]{1,0:T(8,128)(2,1)}), bf16[256,3072]{1,0:T(8,128)(2,1)}) %reduce-scatter.3.cloned.1.call-update) | async-done | bytes 1572880 | tf_op jit(solution)/shard_map/reduce_scatter | solution.py:25
  813.7 1.7 add_convert_fusion
  815.4 0.7 copy.11
  816.1 0.9 fusion.14
  817.0 2.0 convolution_convert_fusion.1
  819.0 0.0 all-gather.9.cloned.1.call-update
  819.0 0.0 reduce-scatter.5.cloned.1.call-start
  819.0 224.6 %all-gather.11.cloned.1.call-done = bf16[4096,3072]{1,0:T(8,128)(2,1)} async-done(((bf16[1024,3072]{1,0:T(8,128)(2,1)}), bf16[4096,3072]{1,0:T(8,128)(2,1)}) %all-gather.11.cloned.1.call-update) | async-done | bytes 25165840 | tf_op jit(solution)/shard_map/all_gather | solution.py:52
  1043.7 47.4 %all-gather.9.cloned.1.call-done = bf16[256,4096]{0,1:T(8,128)(2,1)} async-done(((bf16[256,1024]{0,1:T(8,128)(2,1)}), bf16[256,4096]{0,1:T(8,128)(2,1)}) %all-gather.9.cloned.1.call-update) | async-done | bytes 2097168 | tf_op jit(solution)/shard_map/all_gather | solution.py:49
  1091.1 13.3 %fusion.15 = f32[256,3072]{1,0:T(8,128)} fusion(bf16[256,4096]{0,1:T(8,128)(2,1)} %all-gather.9.cloned.1.call-done, bf16[4096,3072]{1,0:T(8,128)(2,1)} %all-gather.11.cloned.1.call-done), kind=kOutput, calls=%fused_computation.25 | convolution fusion | flops 6442450944 | bytes 30408704 | tf_op jit(solution)/shard_map/dot_general | solution.py:50
  1104.4 0.0 copy-start.1
  1104.4 0.0 reduce-scatter.5.cloned.1.call-update
  1104.4 0.7 copy-done.1
  1105.1 9.1 reduce-scatter.5.cloned.1.call-done
  1114.2 2.7 broadcast_add_fusion
  (3 shorter events, 0.0 us)
Async XLA Ops:
  6.5 14.9 %all-gather.5.cloned.1.call-start = ((), (), s32[]{:S(2)}) async-start(), calls=%async_computation.2 | async-start | bytes 2359296 | tf_op jit(solution)/shard_map/all_gather | solution.py:22
  7.3 664.4 %all-gather.7.cloned.1.call-start = ((), (), s32[]{:S(2)}) async-start(), calls=%async_computation.3 | async-start | bytes 94371840 | tf_op jit(solution)/shard_map/all_gather | solution.py:23
  8.0 805.7 %reduce-scatter.3.cloned.1.call-start = ((), (), s32[]{:S(2)}) async-start(), calls=%async_computation.4 | async-start | bytes 7864320 | tf_op jit(solution)/shard_map/reduce_scatter | solution.py:25
  702.8 0.7 copy-start
  702.8 340.9 %all-gather.11.cloned.1.call-start = ((), (), s32[]{:S(2)}) async-start(), calls=%async_computation.6 | async-start | bytes 31457280 | tf_op jit(solution)/shard_map/all_gather | solution.py:52
  703.4 387.7 %all-gather.9.cloned.1.call-start = ((), (), s32[]{:S(2)}) async-start(), calls=%async_computation.5 | async-start | bytes 2621440 | tf_op jit(solution)/shard_map/all_gather | solution.py:49
  819.0 295.2 %reduce-scatter.5.cloned.1.call-start = ((), (), s32[]{:S(2)}) async-start(), calls=%async_computation.7 | async-start | bytes 4718592 | tf_op jit(solution)/shard_map/reduce_scatter | solution.py:55
  1104.4 0.7 copy-start.1
Sparse Core Ops, SparseCore 0:
  8.9 12.4 all-gather.4
  23.3 648.2 all-gather.6
  702.9 110.7 reduce-scatter.2
  815.4 228.2 all-gather.10
  1045.1 45.9 all-gather.8
  1104.5 9.5 reduce-scatter.4
where the time goes:
time: 1120 us
  waiting for transfers between devices  1060 us (95%)
  matrix products  47.3 us (4%)
  between operations  14.2 us (1%)
    all_gather x1, waiting for transfers between devices, shards(): w_block = lax.all_gather(w_qkv, 'tok', axis=0, tiled=True)  650 us
    all_gather x1, waiting for transfers between devices, shards(): lax.all_gather(w_out, 'tok', axis=0, tiled=True)  225 us
    reduce_scatter x1, waiting for transfers between devices, shards(): lax.psum_scatter(partial_value.astype(jnp.bfloat16), 'ka', scatter_dimens...  109 us
    all_gather x1, waiting for transfers between devices, shards(): head_group = lax.all_gather(context, 'ka', axis=1, tiled=True)  47.4 us
    dot_general x1, matrix products, shards(): partial_value = jnp.dot(panel, w_block, preferred_element_type=jnp.float32)  31.1 us
  transfers between devices with their start and end apart: 6, of which 6 were waited for; matrix products, arithmetic and copies ran while one was open for 0% of the time, Pallas kernels for 0%

commit v1 on v0

v1 whole, which is shorter than its diff:
```python
import jax
import jax.numpy as jnp
from jax import lax
from jax.sharding import PartitionSpec as P

HD = 128
SEQ = 256


def softmax_rows(scores, allowed):
    scores = jnp.where(allowed, scores, -1e30)
    row_max = jnp.max(scores, axis=-1, keepdims=True)
    weights = jnp.exp(scores - row_max)
    row_sum = jnp.sum(weights, axis=-1, keepdims=True)
    return (weights / row_sum).astype(jnp.bfloat16)


def attention(qkv_held, length):
    heads_dev = qkv_held.shape[1] // (3 * HD)
    table = qkv_held.reshape(SEQ, heads_dev, 3, HD)
    positions = jnp.arange(SEQ)
    allowed = (positions[None, :] <= positions[:, None]) & (positions[None, :] < length)
    scores = (
        jnp.einsum(
            "shd,thd->hst",
            table[:, :, 0],
            table[:, :, 1],
            preferred_element_type=jnp.float32,
        )
        * (1.0 / HD**0.5)
    )
    prob_rows = softmax_rows(scores, allowed[None])
    context = jnp.einsum(
        "hst,thd->shd", prob_rows, table[:, :, 2], preferred_element_type=jnp.float32
    )
    return context.astype(jnp.bfloat16).reshape(SEQ, heads_dev * HD)


def shards(features, lengths, w_qkv, b_qkv, w_out, b_out):
    n_tok = lax.axis_size("tok")
    t = lax.axis_index("tok")
    k = lax.axis_index("ka")
    slab = lax.all_gather(features, "out", axis=1, tiled=True)
    panel = lax.all_to_all(slab, "tok", split_axis=1, concat_axis=0, tiled=True)
    partial_value = jnp.dot(panel, w_qkv, preferred_element_type=jnp.float32)
    part = lax.psum_scatter(
        partial_value.astype(jnp.bfloat16), "tok", scatter_dimension=1, tiled=True
    )
    qkv_sum = lax.psum_scatter(part, "ka", scatter_dimension=0, tiled=True)
    bias_half = lax.all_gather(b_qkv, "ka", axis=0, tiled=True)
    width = qkv_sum.shape[1]
    bias = lax.dynamic_slice_in_dim(bias_half, t * width, width)
    qkv_held = (qkv_sum.astype(jnp.float32) + bias.astype(jnp.float32)).astype(jnp.bfloat16)
    all_lengths = lax.all_gather(lengths, "tok", axis=0, tiled=True)
    length = lax.dynamic_index_in_dim(all_lengths, k, keepdims=False)
    context = attention(qkv_held, length)
    head_group = lax.all_gather(context, "ka", axis=0, tiled=True)
    terms = jnp.dot(head_group, w_out, preferred_element_type=jnp.float32)
    summed = lax.psum_scatter(terms, "out", scatter_dimension=1, tiled=True)
    summed = lax.psum_scatter(summed, "tok", scatter_dimension=0, tiled=True)
    del n_tok
    return summed + b_out.astype(jnp.float32)


def solution(mesh):
    placed = (
        P("tok", ("ka", "out")),
        P("tok"),
        P(("ka", "tok"), "out"),
        P(("out", "ka")),
        P(("out", "tok"), "ka"),
        P(("ka", "out")),
    )
    return jax.shard_map(
        shards, mesh=mesh, in_specs=placed, out_specs=P("tok", ("ka", "out")), check_vma=False
    )
```

time: 1120 us -> 580 us (0.52)
  waiting for transfers between devices: 1060 us -> 462 us
  blocking collectives: 0 us -> 46.6 us
    all_gather x4 -> x2, waiting for transfers between devices: 936 us -> 59.4 us  [the longest x1 46.8 us: shards(): head_group = lax.all_gather(context, 'ka', axis=0, tiled=True)]
    reduce_scatter x1 -> x3, waiting for transfers between devices: 109 us -> 383 us  [the longest x1 222 us: shards(): lax.psum_scatter(partial_value.astype(jnp.bfloat16), 'tok', scatter_dimen...]
    all_to_all x0 -> x1, blocking collectives: none -> 24.1 us  [shards(): panel = lax.all_to_all(slab, 'tok', split_axis=1, concat_axis=0, tiled=True)]
    all_gather x0 -> x1, blocking collectives: none -> 15.3 us  [shards(): bias_half = lax.all_gather(b_qkv, 'ka', axis=0, tiled=True)]
where the time goes in v1:
time: 580 us; the launch traced here: 579 us
  waiting for transfers between devices  462 us (80%)
  blocking collectives  46.6 us (8%)
  matrix products  44.2 us (8%)
  between operations  14.2 us (2%)
  local copies, waits for them, and re-layouts  6.27 us (1%)
    reduce_scatter x1, waiting for transfers between devices, shards(): lax.psum_scatter(partial_value.astype(jnp.bfloat16), 'tok', scatter_dimen...  222 us
    reduce_scatter x1, waiting for transfers between devices, shards(): qkv_sum = lax.psum_scatter(part, 'ka', scatter_dimension=0, tiled=True)  87.6 us
    reduce_scatter x1, waiting for transfers between devices, shards(): summed = lax.psum_scatter(summed, 'tok', scatter_dimension=0, tiled=True)  73.8 us
    all_gather x1, waiting for transfers between devices, shards(): head_group = lax.all_gather(context, 'ka', axis=0, tiled=True)  46.8 us
    dot_general x1, matrix products, shards(): partial_value = jnp.dot(panel, w_qkv, preferred_element_type=jnp.float32)  29.2 us
    all_to_all x1, blocking collectives, shards(): panel = lax.all_to_all(slab, 'tok', split_axis=1, concat_axis=0, tiled=True)  24.1 us
    reduce_scatter x1, waiting for transfers between devices, shards(): summed = lax.psum_scatter(terms, 'out', scatter_dimension=1, tiled=True)  19.8 us
    all_gather x1, blocking collectives, shards(): bias_half = lax.all_gather(b_qkv, 'ka', axis=0, tiled=True)  15.3 us
  transfers between devices with their start and end apart: 6, of which 6 were waited for; matrix products, arithmetic and copies ran while one was open for 0% of the time, Pallas kernels for 0%

profile of v1, /device:TPU:0, one launch (start us, length us, event | category | flops | bytes accessed | tf_op | source)
XLA Modules:
  0.0 579.1 jit_solution(7870896389509634013)
XLA Ops:
  6.5 2.3 copy.23
  8.8 0.0 all-gather.3.cloned.1.call-update
  8.8 0.0 reduce-scatter.5.cloned.1.call-start
  8.9 12.6 %all-gather.3.cloned.1.call-done = bf16[256,3072]{0,1:T(8,128)(2,1)} async-done(((bf16[256,1536]{0,1:T(8,128)(2,1)}), bf16[256,3072]{0,1:T(8,128)(2,1)}) %all-gather.3.cloned.1.call-update) | async-done | bytes 1572880 | tf_op jit(solution)/shard_map/all_gather | solution.py:43
  21.5 24.1 %all_to_all.19 = bf16[256,4,768]{0,2,1:T(8,128)(2,1)S(1)} all-to-all(bf16[256,4,768]{0,2,1:T(8,128)(2,1)} %bitcast.51), channel_id=1, replica_groups=mesh['tok'=4,'ka'=4,'out'=2] {'tok'}, dimensions={1} | all-to-all | bytes 3145728 | tf_op jit(solution)/shard_map/all_to_all | solution.py:44
  45.6 0.7 copy.24
  46.3 29.2 %convolution_convert_fusion = bf16[1024,12288]{1,0:T(8,128)(2,1)} fusion(bf16[1024,768]{1,0:T(8,128)(2,1)S(1)} %bitcast.54, bf16[768,12288]{1,0:T(8,128)(2,1)} %param.8), kind=kOutput, calls=%fused_computation.1 | convolution fusion | flops 19339935744 | bytes 45613056 | tf_op jit(solution)/shard_map/dot_general | solution.py:45
  75.6 0.0 reduce-scatter.5.cloned.1.call-update
  75.6 0.0 reduce-scatter.7.cloned.1.call-start
  75.7 221.6 %reduce-scatter.5.cloned.1.call-done = bf16[1024,3072]{1,0:T(8,128)(2,1)} async-done(((bf16[1024,12288]{1,0:T(8,128)(2,1)}), bf16[1024,3072]{1,0:T(8,128)(2,1)}) %reduce-scatter.5.cloned.1.call-update) | async-done | bytes 6291472 | tf_op jit(solution)/shard_map/reduce_scatter | solution.py:46
  297.2 0.0 reduce-scatter.7.cloned.1.call-update
  297.2 0.0 all-gather.5.cloned.1.call-start
  298.0 0.6 dynamic-slice
  298.5 0.8 dynamic-update-slice
  299.3 7.2 %all-reduce = s32[4]{0:T(128)S(1)} all-reduce(s32[4]{0:T(128)S(1)} %dynamic-update-slice), channel_id=1, replica_groups=mesh['tok'=4,'ka'=4,'out'=2] {'tok'}, use_global_device_ids=true, to_apply=%add | all-reduce | flops 4 | bytes 32
  306.5 0.6 dynamic_slice.8
  307.1 15.3 %all_gather.13 = bf16[12288]{0:T(1024)(128)(2,1)S(1)} all-gather(bf16[3072]{0:T(1024)(128)(2,1)S(1)} %copy-done), channel_id=1, replica_groups=mesh['tok'=4,'ka'=4,'out'=2] {'ka'}, dimensions={0}, use_global_device_ids=true | all-gather | bytes 30720 | tf_op jit(solution)/shard_map/all_gather | solution.py:50
  322.4 0.6 iota_compare_fusion.1
  323.1 0.1 fusion.6
  323.2 87.6 %reduce-scatter.7.cloned.1.call-done = bf16[256,3072]{1,0:T(8,128)(2,1)} async-done(((bf16[1024,3072]{1,0:T(8,128)(2,1)}), bf16[256,3072]{1,0:T(8,128)(2,1)}) %reduce-scatter.7.cloned.1.call-update) | async-done | bytes 1572880 | tf_op jit(solution)/shard_map/reduce_scatter | solution.py:49
  410.8 1.7 add_convert_fusion
  412.6 0.7 copy.25
  413.3 0.9 fusion.14
  414.1 2.0 convolution_convert_fusion.1
  416.1 0.0 reduce-scatter.9.cloned.1.call-start
  416.2 46.8 %all-gather.5.cloned.1.call-done = bf16[1024,1024]{0,1:T(8,128)(2,1)} async-done(((bf16[256,1024]{0,1:T(8,128)(2,1)}), bf16[1024,1024]{0,1:T(8,128)(2,1)}) %all-gather.5.cloned.1.call-update) | async-done | bytes 2097168 | tf_op jit(solution)/shard_map/all_gather | solution.py:57
  462.9 12.2 %fusion.15 = f32[1024,3072]{1,0:T(8,128)} fusion(bf16[1024,1024]{0,1:T(8,128)(2,1)} %all-gather.5.cloned.1.call-done, bf16[1024,3072]{1,0:T(8,128)(2,1)} %param.10), kind=kOutput, calls=%fused_computation.26 | convolution fusion | flops 6442450944 | bytes 20971520 | tf_op jit(solution)/shard_map/dot_general | solution.py:58
  475.1 0.0 reduce-scatter.11.cloned.1.call-start
  475.2 19.8 %reduce-scatter.9.cloned.1.call-done = f32[1024,1536]{1,0:T(8,128)} async-done(((f32[1024,3072]{1,0:T(8,128)}), f32[1024,1536]{1,0:T(8,128)}) %reduce-scatter.9.cloned.1.call-update) | async-done | bytes 6291472 | tf_op jit(solution)/shard_map/reduce_scatter | solution.py:59
  495.0 0.7 copy-done.1
  495.7 73.8 %reduce-scatter.11.cloned.1.call-done = f32[256,1536]{1,0:T(8,128)} async-done(((f32[1024,1536]{1,0:T(8,128)}), f32[256,1536]{1,0:T(8,128)}) %reduce-scatter.11.cloned.1.call-update) | async-done | bytes 1572880 | tf_op jit(solution)/shard_map/reduce_scatter | solution.py:60
  569.5 2.7 broadcast_add_fusion
  (12 shorter events, 0.1 us)
Async XLA Ops:
  6.5 15.0 %all-gather.3.cloned.1.call-start = ((), (), s32[]{:S(2)}) async-start(), calls=%async_computation.5 | async-start | bytes 2359296 | tf_op jit(solution)/shard_map/all_gather | solution.py:43
  8.8 288.4 %reduce-scatter.5.cloned.1.call-start = ((), (), s32[]{:S(2)}) async-start(), calls=%async_computation.6 | async-start | bytes 31457280 | tf_op jit(solution)/shard_map/reduce_scatter | solution.py:46
  75.6 335.2 %reduce-scatter.7.cloned.1.call-start = ((), (), s32[]{:S(2)}) async-start(), calls=%async_computation.7 | async-start | bytes 7864320 | tf_op jit(solution)/shard_map/reduce_scatter | solution.py:49
  297.2 0.7 copy-start.2
  297.2 9.9 %copy-start = (bf16[3072]{0:T(1024)(128)(2,1)S(1)}, bf16[3072]{0:T(1024)(128)(2,1)}, u32[]{:S(2)}) copy-start(bf16[3072]{0:T(1024)(128)(2,1)} %param.9) | copy-start | bytes 18436
  297.2 165.7 %all-gather.5.cloned.1.call-start = ((), (), s32[]{:S(2)}) async-start(), calls=%async_computation.8 | async-start | bytes 2621440 | tf_op jit(solution)/shard_map/all_gather | solution.py:57
  416.1 78.9 %reduce-scatter.9.cloned.1.call-start = ((), (), s32[]{:S(2)}) async-start(), calls=%async_computation.9 | async-start | bytes 18874368 | tf_op jit(solution)/shard_map/reduce_scatter | solution.py:59
  475.1 94.4 %reduce-scatter.11.cloned.1.call-start = ((), (), s32[]{:S(2)}) async-start(), calls=%async_computation.10 | async-start | bytes 7864320 | tf_op jit(solution)/shard_map/reduce_scatter | solution.py:60
  495.0 0.7 copy-start.1
Sparse Core Ops, SparseCore 0:
  9.0 12.4 all-gather.2
  75.7 221.4 reduce-scatter.4
  299.6 111.1 reduce-scatter.6
  416.2 46.6 all-gather.4
  475.2 19.7 reduce-scatter.8
  498.1 71.3 reduce-scatter.10

commit v2 on v0

v2 whole, which is shorter than its diff:
```python
import jax
import jax.numpy as jnp
from jax import lax
from jax.sharding import PartitionSpec as P

HD = 128
SEQ = 256


def softmax_rows(scores, allowed):
    scores = jnp.where(allowed, scores, -1e30)
    row_max = jnp.max(scores, axis=-1, keepdims=True)
    weights = jnp.exp(scores - row_max)
    row_sum = jnp.sum(weights, axis=-1, keepdims=True)
    return (weights / row_sum).astype(jnp.bfloat16)


def attention(qkv_held, lengths):
    prompts = qkv_held.shape[0] // SEQ
    heads_dev = qkv_held.shape[1] // (3 * HD)
    table = qkv_held.reshape(prompts, SEQ, heads_dev, 3, HD)
    positions = jnp.arange(SEQ)
    causal = positions[None, :] <= positions[:, None]
    live = positions[None, :] < lengths[:, None]
    allowed = causal[None, None] & live[:, None, None, :]
    scores = (
        jnp.einsum(
            "pshd,pthd->phst",
            table[:, :, :, 0],
            table[:, :, :, 1],
            preferred_element_type=jnp.float32,
        )
        * (1.0 / HD**0.5)
    )
    prob_rows = softmax_rows(scores, allowed)
    context = jnp.einsum(
        "phst,pthd->pshd", prob_rows, table[:, :, :, 2], preferred_element_type=jnp.float32
    )
    return context.astype(jnp.bfloat16).reshape(prompts * SEQ, heads_dev * HD)


def pick(x, i, axis):
    return lax.dynamic_index_in_dim(x, i, axis=axis, keepdims=False)


def rs_tok_2d(part, t, x_first):
    rows, _, w = part.shape
    grid = part.reshape(rows, 2, 2, w)
    xb, yb = t % 2, t // 2
    x_pairs = [(i, i ^ 1) for i in range(4)]
    y_pairs = [(i, i ^ 2) for i in range(4)]
    if x_first:
        first_axis, first_bit, first_pairs = 2, xb, x_pairs
        second_bit, second_pairs = yb, y_pairs
    else:
        first_axis, first_bit, first_pairs = 1, yb, y_pairs
        second_bit, second_pairs = xb, x_pairs
    keep = pick(grid, first_bit, first_axis).astype(jnp.float32)
    sent = lax.ppermute(pick(grid, 1 - first_bit, first_axis), "tok", first_pairs)
    step = keep + sent.astype(jnp.float32)
    keep = pick(step, second_bit, 1)
    sent = lax.ppermute(pick(step, 1 - second_bit, 1).astype(jnp.bfloat16), "tok", second_pairs)
    return keep + sent.astype(jnp.float32)


def shards(features, lengths, w_qkv, b_qkv, w_out, b_out, n_tok, n_ka):
    t = lax.axis_index("tok")
    k = lax.axis_index("ka")
    rows_dev = features.shape[0]
    slab = lax.all_gather(features, "out", axis=1, tiled=True)
    panel = lax.all_to_all(slab, "tok", split_axis=1, concat_axis=0, tiled=True)
    partial_value = jnp.dot(panel, w_qkv, preferred_element_type=jnp.float32)
    tokens, cols = partial_value.shape
    width = cols // n_tok
    row_of = lax.broadcasted_iota(jnp.int32, (tokens, n_tok, 1), 0) // rows_dev
    block_of = lax.broadcasted_iota(jnp.int32, (tokens, n_tok, 1), 1)
    here = (row_of == t) & (block_of == k)
    bias = b_qkv.astype(jnp.float32).reshape(1, 1, width)
    part = partial_value.reshape(tokens, n_tok, width)
    part = (part + jnp.where(here, bias, 0.0)).astype(jnp.bfloat16)
    if n_tok == n_ka:
        transpose = [(a * n_ka + b, b * n_ka + a) for a in range(n_tok) for b in range(n_ka)]
        own_lengths = lax.ppermute(lengths, ("tok", "ka"), transpose)
    else:
        all_lengths = lax.all_gather(lengths, "tok", axis=0, tiled=True)
        per = all_lengths.shape[0] // n_ka
        own_lengths = lax.dynamic_slice_in_dim(all_lengths, k * per, per)
    heads_block = width // (3 * HD)
    if n_tok == 4 and heads_block % 2 == 0:
        half = width // 2
        streams = [
            rs_tok_2d(part[:, :, :half], t, True),
            rs_tok_2d(part[:, :, half:], t, False),
        ]
    else:
        streams = [
            lax.psum_scatter(part.reshape(tokens, cols), "tok", scatter_dimension=1, tiled=True)
        ]
    w_rows = w_out.shape[0] // len(streams)
    terms = None
    for i, slab_sum in enumerate(streams):
        qkv_held = lax.psum_scatter(
            slab_sum.astype(jnp.bfloat16), "ka", scatter_dimension=0, tiled=True
        )
        context = attention(qkv_held, own_lengths)
        head_group = lax.all_gather(context, "ka", axis=0, tiled=True)
        term = jnp.dot(
            head_group, w_out[i * w_rows:(i + 1) * w_rows], preferred_element_type=jnp.float32
        )
        terms = term if terms is None else terms + term
    summed = lax.psum_scatter(terms, "out", scatter_dimension=1, tiled=True)
    summed = lax.psum_scatter(summed, "tok", scatter_dimension=0, tiled=True)
    return summed + b_out.astype(jnp.float32)


def solution(mesh):
    n_tok, n_ka = mesh.shape["tok"], mesh.shape["ka"]
    placed = (
        P("tok", ("ka", "out")),
        P("tok"),
        P(("ka", "tok"), "out"),
        P(("out", "ka")),
        P(("out", "tok"), "ka"),
        P(("ka", "out")),
    )

    def body(*args):
        return shards(*args, n_tok=n_tok, n_ka=n_ka)

    return jax.shard_map(
        body, mesh=mesh, in_specs=placed, out_specs=P("tok", ("ka", "out")), check_vma=False
    )
```

time: 1120 us -> 690 us (0.62)
  waiting for transfers between devices: 1060 us -> 454 us
  local copies, waits for them, and re-layouts: 1.42 us -> 106 us
  other arithmetic: 4.6 us -> 39.2 us
  matrix products: 47.3 us -> 64.1 us
  starting transfers between devices: 0.2 us -> 12 us
    all_gather x4 -> x3, waiting for transfers between devices: 936 us -> 60.3 us  [the longest x2 46.1 us: shards(): head_group = lax.all_gather(context, 'ka', axis=0, tiled=True)]
    ppermute x0 -> x5, waiting for transfers between devices: none -> 245 us  [the longest x2 138 us: rs_tok_2d(): lax.ppermute(pick(step, 1 - second_bit, 1).astype(jnp.bfloat16), 'tok', s...]
    dynamic_slice x0 -> x4, local copies, waits for them, and re-layouts: none -> 37.1 us  [pick(): return lax.dynamic_index_in_dim(x, i, axis=axis, keepdims=False)]
    dot_general x0 -> x1, local copies, waits for them, and re-layouts: none -> 24.6 us  [shards(): partial_value = jnp.dot(panel, w_qkv, preferred_element_type=jnp.float32)]
    add x0 -> x2, other arithmetic: none -> 24.4 us  [rs_tok_2d(): step = keep + sent.astype(jnp.float32)]
    reduce_scatter x1 -> x3, waiting for transfers between devices: 109 us -> 127 us  [the longest x1 74.3 us: shards(): summed = lax.psum_scatter(summed, 'tok', scatter_dimension=0, tiled=True)]
    slice x0 -> x1, local copies, waits for them, and re-layouts: none -> 17.3 us  [shards(): part[:, :, half:]]
    unnamed x4 -> x6, local copies, waits for them, and re-layouts: 0.72 us -> 17.4 us
  transfers between devices with their start and end apart: 6 -> 13, of which waited for: 6 -> 9; matrix products, arithmetic and copies ran while one was open for 0% -> 18% of each run, Pallas kernels for 0% -> 0%
where the time goes in v2:
time: 690 us; the launch traced here: 688 us
  waiting for transfers between devices  454 us (66%)
  local copies, waits for them, and re-layouts  106 us (15%)
  matrix products  64.1 us (9%)
  other arithmetic  39.2 us (6%)
  between operations  13.6 us (2%)
  starting transfers between devices  12 us (2%)
    ppermute x2, waiting for transfers between devices, rs_tok_2d(): lax.ppermute(pick(step, 1 - second_bit, 1).astype(jnp.bfloat16), 'tok', s...  138 us
    ppermute x2, waiting for transfers between devices, rs_tok_2d(): lax.ppermute(pick(grid, 1 - first_bit, first_axis), 'tok', first_pairs)  107 us
    reduce_scatter x1, waiting for transfers between devices, shards(): summed = lax.psum_scatter(summed, 'tok', scatter_dimension=0, tiled=True)  74.3 us
    reduce_scatter x2, waiting for transfers between devices, shards(): lax.psum_scatter(slab_sum.astype(jnp.bfloat16), 'ka', scatter_dimension=0...  53.1 us
    all_gather x2, waiting for transfers between devices, shards(): head_group = lax.all_gather(context, 'ka', axis=0, tiled=True)  46.1 us
    dynamic_slice x4, local copies, waits for them, and re-layouts, pick(): return lax.dynamic_index_in_dim(x, i, axis=axis, keepdims=False)  37.1 us
    dot_general x1, matrix products, shards(): partial_value = jnp.dot(panel, w_qkv, preferred_element_type=jnp.float32)  29.9 us
    dot_general x1, local copies, waits for them, and re-layouts, shards(): partial_value = jnp.dot(panel, w_qkv, preferred_element_type=jnp.float32)  24.6 us
  transfers between devices with their start and end apart: 13, of which 9 were waited for; matrix products, arithmetic and copies ran while one was open for 18% of the time, Pallas kernels for 0%

profile of v2, /device:TPU:0, one launch (start us, length us, event | category | flops | bytes accessed | tf_op | source)
XLA Modules:
  0.0 688.2 jit_solution(322174294168595411)
XLA Ops:
  7.3 14.2 %all-gather.4.cloned.1.call-done = bf16[256,3072]{1,0:T(8,128)(2,1)} async-done(((bf16[256,1536]{1,0:T(8,128)(2,1)}), bf16[256,3072]{1,0:T(8,128)(2,1)}) %all-gather.4.cloned.1.call-update) | async-done | bytes 1572880 | tf_op jit(solution)/shard_map/all_gather | solution.py:70
  21.4 2.7 copy.40
  24.1 3.9 all-to-all-start
  28.0 24.6 %copy.29 = bf16[12288,768]{1,0:T(8,128)(2,1)} copy(bf16[12288,768]{0,1:T(8,128)(2,1)} %bitcast.96) | data formatting | bytes 37748736 | tf_op jit(solution)/shard_map/dot_general | solution.py:72
  52.7 29.9 %add_convert_fusion = bf16[1024,4,3072]{2,0,1:T(8,128)(2,1)} fusion(bf16[1024,768,1]{1,0,2:T(8,128)(2,1)S(1)} %bitcast.100, bf16[4,3072,768]{2,1,0:T(8,128)(2,1)} %bitcast.97, f32[3072]{0:T(1024)S(1)} %convert_element_type.77, pred[1024,4]{0,1:T(4,128)(4,1)S(1)} %fusion.16), kind=kOutput, calls=%fused_computation.2 | convolution fusion | flops 19365101568 | bytes 45629440 | tf_op jit(solution)/shard_map/dot_general | solution.py:72
  82.7 17.3 %fusion.26 = (bf16[1024,4,1536]{2,0,1:T(8,128)(2,1)}, bf16[1024,4,1536]{2,0,1:T(8,128)(2,1)}) fusion(bf16[1024,4,3072]{2,0,1:T(8,128)(2,1)} %add_convert_fusion), kind=kLoop, calls=%fused_computation.60 | loop fusion | bytes 50331648 | tf_op jit(solution)/shard_map/slice | solution.py:93
  99.9 9.9 %constant_dynamic-slice_fusion.3 = (bf16[1024,2,1,1536]{3,0,2,1:T(8,128)(2,1)}, bf16[1024,2,1,1536]{3,0,2,1:T(8,128)(2,1)}) fusion(bf16[1024,2,2,1536]{3,0,2,1:T(8,128)(2,1)} %bitcast.95, s32[]{:T(128)S(6)} %select_n.59, s32[]{:T(128)S(6)} %select_n.60), kind=kLoop, calls=%fused_computation.51 | loop fusion | bytes 25165832 | tf_op jit(solution)/shard_map/jit(dynamic_index_in_dim)/dynamic_slice | solution.py:43
  109.8 8.6 %copy.16 = bf16[1024,2,1,1536]{0,3,1,2:T(8,128)(2,1)} copy(bf16[1024,2,1,1536]{3,0,2,1:T(8,128)(2,1)} %get-tuple-element.10) | data formatting | bytes 12582912 | tf_op jit(solution)/shard_map/jit(dynamic_index_in_dim)/dynamic_slice | solution.py:43
  118.4 2.0 collective-permute-start
  120.5 9.9 %constant_dynamic-slice_fusion.1 = (bf16[1024,1,2,1536]{3,0,2,1:T(8,128)(2,1)}, bf16[1024,1,2,1536]{3,0,2,1:T(8,128)(2,1)}) fusion(bf16[1024,2,2,1536]{3,0,2,1:T(8,128)(2,1)} %bitcast.94, s32[]{:T(128)S(6)} %select_n.62, s32[]{:T(128)S(6)} %select_n.63), kind=kLoop, calls=%fused_computation.49 | loop fusion | bytes 25165832 | tf_op jit(solution)/shard_map/jit(dynamic_index_in_dim)/dynamic_slice | solution.py:43
  130.3 8.7 %copy.22 = bf16[1024,1,2,1536]{0,3,2,1:T(8,128)(2,1)} copy(bf16[1024,1,2,1536]{3,0,2,1:T(8,128)(2,1)} %get-tuple-element.8) | data formatting | bytes 12582912 | tf_op jit(solution)/shard_map/jit(dynamic_index_in_dim)/dynamic_slice | solution.py:43
  140.5 8.7 %copy.30 = bf16[1024,2,1,1536]{0,3,1,2:T(8,128)(2,1)} copy(bf16[1024,2,1,1536]{3,0,2,1:T(8,128)(2,1)} %get-tuple-element.9) | data formatting | bytes 12582912
  149.2 107.0 %collective-permute-done = bf16[1024,2,1536]{0,2,1:T(8,128)(2,1)} collective-permute-done((bf16[1024,2,1536]{0,2,1:T(8,128)(2,1)}, bf16[1024,2,1536]{0,2,1:T(8,128)(2,1)}, u32[]{:S(2)}, u32[]{:S(2)}) %collective-permute-start) | collective-permute-done | bytes 6291488 | tf_op jit(solution)/shard_map/ppermute | solution.py:59
  256.2 12.2 %convert_add_fusion.1 = f32[1024,2,1536]{0,2,1:T(8,128)} fusion(bf16[1024,2,1536]{0,2,1:T(8,128)(2,1)} %collective-permute-done, bf16[1024,2,1,1536]{0,3,1,2:T(8,128)(2,1)} %copy.30), kind=kLoop, calls=%fused_computation.4 | loop fusion | flops 9437184 | bytes 25165824 | tf_op jit(solution)/shard_map/add | solution.py:60
  268.4 3.3 fusion.4
  273.5 70.1 %collective-permute-done.1 = bf16[1024,1536]{0,1:T(8,128)(2,1)S(1)} collective-permute-done((bf16[1024,1536]{0,1:T(8,128)(2,1)S(1)}, bf16[1024,1536]{0,1:T(8,128)(2,1)S(1)}, u32[]{:S(2)}, u32[]{:S(2)}) %collective-permute-start.1) | collective-permute-done | bytes 3145760 | tf_op jit(solution)/shard_map/ppermute | solution.py:62
  343.5 5.6 fusion.3
  349.4 8.7 %copy.34 = bf16[1024,1,2,1536]{0,3,2,1:T(8,128)(2,1)} copy(bf16[1024,1,2,1536]{3,0,2,1:T(8,128)(2,1)} %get-tuple-element.7) | data formatting | bytes 12582912
  358.1 12.2 %convert_add_fusion = f32[1024,2,1536]{0,2,1:T(8,128)} fusion(bf16[1024,2,1536]{0,2,1:T(8,128)(2,1)} %collective-permute-done.3, bf16[1024,1,2,1536]{0,3,2,1:T(8,128)(2,1)} %copy.34), kind=kLoop, calls=%fused_computation.3 | loop fusion | flops 9437184 | bytes 25165824 | tf_op jit(solution)/shard_map/add | solution.py:60
  370.3 3.3 fusion.5
  373.9 68.3 %collective-permute-done.4 = bf16[1024,1536]{0,1:T(8,128)(2,1)S(1)} collective-permute-done((bf16[1024,1536]{0,1:T(8,128)(2,1)S(1)}, bf16[1024,1536]{0,1:T(8,128)(2,1)S(1)}, u32[]{:S(2)}, u32[]{:S(2)}) %collective-permute-start.4) | collective-permute-done | bytes 3145760 | tf_op jit(solution)/shard_map/ppermute | solution.py:62
  442.2 5.6 fusion.2
  453.5 2.1 convolution_convert_fusion.1
  455.7 53.0 %reduce-scatter.7.cloned.1.call-done = bf16[256,1536]{0,1:T(8,128)(2,1)} async-done(((bf16[1024,1536]{0,1:T(8,128)(2,1)}), bf16[256,1536]{0,1:T(8,128)(2,1)}) %reduce-scatter.7.cloned.1.call-update) | async-done | bytes 786448 | tf_op jit(solution)/shard_map/reduce_scatter | solution.py:102
  511.7 2.1 convolution_convert_fusion
  514.0 26.4 %all-gather.6.cloned.1.call-done = bf16[1024,512]{0,1:T(8,128)(2,1)} async-done(((bf16[256,512]{0,1:T(8,128)(2,1)}), bf16[1024,512]{0,1:T(8,128)(2,1)}) %all-gather.6.cloned.1.call-update) | async-done | bytes 1048592 | tf_op jit(solution)/shard_map/all_gather | solution.py:106
  540.4 10.2 %fusion.7 = f32[1024,3072]{1,0:T(8,128)} fusion(bf16[1024,512]{0,1:T(8,128)(2,1)} %all-gather.6.cloned.1.call-done, bf16[1024,3072]{1,0:T(8,128)(2,1)} %param.10), kind=kOutput, calls=%fused_computation.15 | convolution fusion | flops 3221225472 | bytes 16777216 | tf_op jit(solution)/shard_map/dot_general | solution.py:107
  550.6 19.7 %all-gather.8.cloned.1.call-done = bf16[1024,512]{0,1:T(8,128)(2,1)} async-done(((bf16[256,512]{0,1:T(8,128)(2,1)}), bf16[1024,512]{0,1:T(8,128)(2,1)}) %all-gather.8.cloned.1.call-update) | async-done | bytes 1048592 | tf_op jit(solution)/shard_map/all_gather | solution.py:106
  570.3 13.9 %convolution_add_fusion = f32[1024,3072]{1,0:T(8,128)} fusion(f32[1024,3072]{1,0:T(8,128)} %fusion.7, bf16[1024,512]{0,1:T(8,128)(2,1)} %all-gather.8.cloned.1.call-done, bf16[1024,3072]{1,0:T(8,128)(2,1)} %param.10), kind=kOutput, calls=%fused_computation.11 | convolution fusion | flops 3224371200 | bytes 29360128 | tf_op jit(solution)/shard_map/dot_general | solution.py:107
  584.3 19.9 %reduce-scatter.9.cloned.1.call-done = f32[1024,1536]{1,0:T(8,128)} async-done(((f32[1024,3072]{1,0:T(8,128)}), f32[1024,1536]{1,0:T(8,128)}) %reduce-scatter.9.cloned.1.call-update) | async-done | bytes 6291472 | tf_op jit(solution)/shard_map/reduce_scatter | solution.py:111
  604.3 74.3 %reduce-scatter.11.cloned.1.call-done = f32[256,1536]{1,0:T(8,128)} async-done(((f32[1024,1536]{1,0:T(8,128)}), f32[256,1536]{1,0:T(8,128)}) %reduce-scatter.11.cloned.1.call-update) | async-done | bytes 1572880 | tf_op jit(solution)/shard_map/reduce_scatter | solution.py:112
  678.6 2.7 broadcast_add_fusion
  (38 shorter events, 13.6 us)
Async XLA Ops:
  6.5 14.9 %all-gather.4.cloned.1.call-start = ((), (), s32[]{:S(2)}) async-start(), calls=%async_computation.5 | async-start | bytes 2359296 | tf_op jit(solution)/shard_map/all_gather | solution.py:70
  24.1 28.6 %all-to-all-start = ((bf16[256,4,768]{2,0,1:T(8,128)(2,1)}), bf16[256,4,768]{2,0,1:T(8,128)(2,1)S(1)}, u32[]{:S(2)}, u32[]{:S(2)}) async-start(bf16[256,4,768]{2,0,1:T(8,128)(2,1)} %bitcast.93), calls=%async_computation | async-start | bytes 3145728 | tf_op jit(solution)/shard_map/all_to_all | solution.py:71
  28.0 422.5 %reduce-scatter.5.cloned.1.call-start = ((), (), s32[]{:S(2)}) async-start(), calls=%async_computation.6 | async-start | bytes 3932160 | tf_op jit(solution)/shard_map/reduce_scatter | solution.py:102
  28.0 24.6 %copy-start = (bf16[3072]{0:T(1024)(128)(2,1)S(1)}, bf16[3072]{0:T(1024)(128)(2,1)}, u32[]{:S(2)}) copy-start(bf16[3072]{0:T(1024)(128)(2,1)} %param.9) | copy-start | bytes 18436
  118.4 137.7 %collective-permute-start = (bf16[1024,2,1536]{0,2,1:T(8,128)(2,1)}, bf16[1024,2,1536]{0,2,1:T(8,128)(2,1)}, u32[]{:S(2)}, u32[]{:S(2)}) collective-permute-start(bf16[1024,2,1536]{0,2,1:T(8,128)(2,1)} %bitcast.98), channel_id=1, source_target_pairs={{0,8},{8,0},{16,24},{24,16},{1,9},{9,1},{17,25},{25,17},{2,10},{10... | collective-permute-start | bytes 18874376 | tf_op jit(solution)/shard_map/ppermute | solution.py:59
  139.0 219.1 %collective-permute-start.3 = (bf16[1024,2,1536]{0,2,1:T(8,128)(2,1)}, bf16[1024,2,1536]{0,2,1:T(8,128)(2,1)}, u32[]{:S(2)}, u32[]{:S(2)}) collective-permute-start(bf16[1024,2,1536]{0,2,1:T(8,128)(2,1)} %bitcast.99), channel_id=1, source_target_pairs={{0,16},{8,24},{16,0},{24,8},{1,17},{9,25},{17,1},{25,9},{2,18},{10... | collective-permute-start | bytes 18874376 | tf_op jit(solution)/shard_map/ppermute | solution.py:59
  271.7 71.9 %collective-permute-start.1 = (bf16[1024,1536]{0,1:T(8,128)(2,1)S(1)}, bf16[1024,1536]{0,1:T(8,128)(2,1)S(1)}, u32[]{:S(2)}, u32[]{:S(2)}) collective-permute-start(bf16[1024,1536]{0,1:T(8,128)(2,1)S(1)} %fusion.4), channel_id=1, source_target_pairs={{0,16},{8,24},{16,0},{24,8},{1,17},{9,25},{17,1},{25,9},{2,18},{10... | collective-permute-start | bytes 9437192 | tf_op jit(solution)/shard_map/ppermute | solution.py:62
  349.1 159.6 %reduce-scatter.7.cloned.1.call-start = ((), (), s32[]{:S(2)}) async-start(), calls=%async_computation.8 | async-start | bytes 3932160 | tf_op jit(solution)/shard_map/reduce_scatter | solution.py:102
  373.7 68.5 %collective-permute-start.4 = (bf16[1024,1536]{0,1:T(8,128)(2,1)S(1)}, bf16[1024,1536]{0,1:T(8,128)(2,1)S(1)}, u32[]{:S(2)}, u32[]{:S(2)}) collective-permute-start(bf16[1024,1536]{0,1:T(8,128)(2,1)S(1)} %fusion.5), channel_id=1, source_target_pairs={{0,8},{8,0},{16,24},{24,16},{1,9},{9,1},{17,25},{25,17},{2,10},{10... | collective-permute-start | bytes 9437192 | tf_op jit(solution)/shard_map/ppermute | solution.py:62
  447.8 92.6 %all-gather.6.cloned.1.call-start = ((), (), s32[]{:S(2)}) async-start(), calls=%async_computation.7 | async-start | bytes 1310720 | tf_op jit(solution)/shard_map/all_gather | solution.py:106
  447.9 1.9 collective-permute-start.2
  455.6 114.7 %all-gather.8.cloned.1.call-start = ((), (), s32[]{:S(2)}) async-start(), calls=%async_computation.9 | async-start | bytes 1310720 | tf_op jit(solution)/shard_map/all_gather | solution.py:106
  513.8 90.4 %reduce-scatter.9.cloned.1.call-start = ((), (), s32[]{:S(2)}) async-start(), calls=%async_computation.10 | async-start | bytes 18874368 | tf_op jit(solution)/shard_map/reduce_scatter | solution.py:111
  584.2 20.0 %copy-start.1 = (bf16[1536]{0:T(1024)(128)(2,1)S(1)}, bf16[1536]{0:T(1024)(128)(2,1)}, u32[]{:S(2)}) copy-start(bf16[1536]{0:T(1024)(128)(2,1)} %param.11) | copy-start | bytes 9220
  584.3 94.3 %reduce-scatter.11.cloned.1.call-start = ((), (), s32[]{:S(2)}) async-start(), calls=%async_computation.11 | async-start | bytes 7864320 | tf_op jit(solution)/shard_map/reduce_scatter | solution.py:112
Sparse Core Ops, SparseCore 0:
  8.9 12.4 all-gather.3
  349.3 60.4 reduce-scatter.4
  447.9 60.7 reduce-scatter.6
  510.1 30.2 all-gather.5
  541.8 28.4 all-gather.7
  584.4 19.7 reduce-scatter.8
  607.2 71.3 reduce-scatter.10

commit v3 on v2

--- a/solution.py
+++ b/solution.py
@@ -39,28 +39,17 @@
     return context.astype(jnp.bfloat16).reshape(prompts * SEQ, heads_dev * HD)
 
 
-def pick(x, i, axis):
-    return lax.dynamic_index_in_dim(x, i, axis=axis, keepdims=False)
-
-
-def rs_tok_2d(part, t, x_first):
-    rows, _, w = part.shape
-    grid = part.reshape(rows, 2, 2, w)
-    xb, yb = t % 2, t // 2
+def rs_tok_2d(blocks, x_first):
     x_pairs = [(i, i ^ 1) for i in range(4)]
     y_pairs = [(i, i ^ 2) for i in range(4)]
     if x_first:
-        first_axis, first_bit, first_pairs = 2, xb, x_pairs
-        second_bit, second_pairs = yb, y_pairs
+        keep, away, pairs, last = (0, 2), (1, 3), (x_pairs, y_pairs), 1
     else:
-        first_axis, first_bit, first_pairs = 1, yb, y_pairs
-        second_bit, second_pairs = xb, x_pairs
-    keep = pick(grid, first_bit, first_axis).astype(jnp.float32)
-    sent = lax.ppermute(pick(grid, 1 - first_bit, first_axis), "tok", first_pairs)
-    step = keep + sent.astype(jnp.float32)
-    keep = pick(step, second_bit, 1)
-    sent = lax.ppermute(pick(step, 1 - second_bit, 1).astype(jnp.bfloat16), "tok", second_pairs)
-    return keep + sent.astype(jnp.float32)
+        keep, away, pairs, last = (0, 1), (2, 3), (y_pairs, x_pairs), 1
+    sent = lax.ppermute(jnp.stack([blocks[j] for j in away]), "tok", pairs[0])
+    step = [blocks[j].astype(jnp.float32) + sent[i].astype(jnp.float32) for i, j in enumerate(keep)]
+    sent = lax.ppermute(step[last].astype(jnp.bfloat16), "tok", pairs[1])
+    return step[0] + sent.astype(jnp.float32)
 
 
 def shards(features, lengths, w_qkv, b_qkv, w_out, b_out, n_tok, n_ka):
@@ -69,15 +58,9 @@
     rows_dev = features.shape[0]
     slab = lax.all_gather(features, "out", axis=1, tiled=True)
     panel = lax.all_to_all(slab, "tok", split_axis=1, concat_axis=0, tiled=True)
-    partial_value = jnp.dot(panel, w_qkv, preferred_element_type=jnp.float32)
-    tokens, cols = partial_value.shape
+    tokens = panel.shape[0]
+    cols = w_qkv.shape[1]
     width = cols // n_tok
-    row_of = lax.broadcasted_iota(jnp.int32, (tokens, n_tok, 1), 0) // rows_dev
-    block_of = lax.broadcasted_iota(jnp.int32, (tokens, n_tok, 1), 1)
-    here = (row_of == t) & (block_of == k)
-    bias = b_qkv.astype(jnp.float32).reshape(1, 1, width)
-    part = partial_value.reshape(tokens, n_tok, width)
-    part = (part + jnp.where(here, bias, 0.0)).astype(jnp.bfloat16)
     if n_tok == n_ka:
         transpose = [(a * n_ka + b, b * n_ka + a) for a in range(n_tok) for b in range(n_ka)]
         own_lengths = lax.ppermute(lengths, ("tok", "ka"), transpose)
@@ -85,17 +68,31 @@
         all_lengths = lax.all_gather(lengths, "tok", axis=0, tiled=True)
         per = all_lengths.shape[0] // n_ka
         own_lengths = lax.dynamic_slice_in_dim(all_lengths, k * per, per)
+    own_rows = (lax.broadcasted_iota(jnp.int32, (tokens, 1), 0) // rows_dev) == t
     heads_block = width // (3 * HD)
-    if n_tok == 4 and heads_block % 2 == 0:
-        half = width // 2
-        streams = [
-            rs_tok_2d(part[:, :, :half], t, True),
-            rs_tok_2d(part[:, :, half:], t, False),
-        ]
+    split = n_tok == 4 and heads_block % 2 == 0
+    n_streams = 2 if split else 1
+    piece = width // n_streams
+    bias = b_qkv.astype(jnp.float32)
+
+    def block(c, h):
+        w_cols = lax.dynamic_slice_in_dim(w_qkv, c * width + h * piece, piece, axis=1)
+        value = jnp.dot(panel, w_cols, preferred_element_type=jnp.float32)
+        here = own_rows & (c == k)
+        value = value + jnp.where(here, bias[h * piece:(h + 1) * piece][None, :], 0.0)
+        return value.astype(jnp.bfloat16)
+
+    if split:
+        order = [(1, 3, 0, 2), (2, 3, 0, 1)]
+        streams = []
+        for h in range(2):
+            blocks = {}
+            for j in order[h]:
+                blocks[j] = block(jnp.bitwise_xor(t, j), h)
+            streams.append(rs_tok_2d(blocks, x_first=(h == 0)))
     else:
-        streams = [
-            lax.psum_scatter(part.reshape(tokens, cols), "tok", scatter_dimension=1, tiled=True)
-        ]
+        full = jnp.concatenate([block(c, 0) for c in range(n_tok)], axis=1)
+        streams = [lax.psum_scatter(full, "tok", scatter_dimension=1, tiled=True)]
     w_rows = w_out.shape[0] // len(streams)
     terms = None
     for i, slab_sum in enumerate(streams):

time: 690 us -> 614 us (0.89)
  local copies, waits for them, and re-layouts: 106 us -> 3.76 us
  waiting for transfers between devices: 454 us -> 476 us
  other arithmetic: 39.2 us -> 21.6 us
  matrix products: 64.1 us -> 81.4 us
    dynamic_slice x4 -> x0, local copies, waits for them, and re-layouts: 37.1 us -> none  [pick(): return lax.dynamic_index_in_dim(x, i, axis=axis, keepdims=False)]
    dot_general x1 -> x0, local copies, waits for them, and re-layouts: 24.6 us -> none  [shards(): partial_value = jnp.dot(panel, w_qkv, preferred_element_type=jnp.float32)]
    add x2 -> x0, other arithmetic: 24.4 us -> none  [rs_tok_2d(): step = keep + sent.astype(jnp.float32)]
    all_to_all x1, waiting for transfers between devices: 0.01 us -> 18.9 us  [shards(): panel = lax.all_to_all(slab, 'tok', split_axis=1, concat_axis=0, tiled=True)]
    dot_general x1 -> x8, matrix products: 29.9 us -> 47.1 us  [block(): value = jnp.dot(panel, w_cols, preferred_element_type=jnp.float32)]
    slice x1, local copies, waits for them, and re-layouts: 17.3 us -> 0.77 us  [block(): bias[h * piece:(h + 1) * piece][None, :]]
    unnamed x6 -> x5, local copies, waits for them, and re-layouts: 17.4 us -> 2.3 us
  transfers between devices with their start and end apart: 13 -> 13, of which waited for: 9 -> 10; matrix products, arithmetic and copies ran while one was open for 18% -> 12% of each run, Pallas kernels for 0% -> 0%
where the time goes in v3:
time: 614 us; the launch traced here: 608 us
  waiting for transfers between devices  476 us (78%)
  matrix products  81.4 us (13%)
  other arithmetic  21.6 us (4%)
  between operations  14.1 us (2%)
  starting transfers between devices  10.5 us (2%)
    ppermute x2, waiting for transfers between devices, rs_tok_2d(): sent = lax.ppermute(step[last].astype(jnp.bfloat16), 'tok', pairs[1])  130 us
    ppermute x2, waiting for transfers between devices, rs_tok_2d(): sent = lax.ppermute(jnp.stack([blocks[j] for j in away]), 'tok', pairs[0])  122 us
    reduce_scatter x1, waiting for transfers between devices, shards(): summed = lax.psum_scatter(summed, 'tok', scatter_dimension=0, tiled=True)  74.3 us
    reduce_scatter x2, waiting for transfers between devices, shards(): lax.psum_scatter(slab_sum.astype(jnp.bfloat16), 'ka', scatter_dimension=0...  53.2 us
    dot_general x8, matrix products, block(): value = jnp.dot(panel, w_cols, preferred_element_type=jnp.float32)  47.1 us
    all_gather x2, waiting for transfers between devices, shards(): head_group = lax.all_gather(context, 'ka', axis=0, tiled=True)  46 us
    dot_general x2, matrix products, shards(): jnp.dot(head_group, w_out[i * w_rows:(i + 1) * w_rows], preferred_element...  24.1 us
    reduce_scatter x1, waiting for transfers between devices, shards(): summed = lax.psum_scatter(terms, 'out', scatter_dimension=1, tiled=True)  19.9 us
  transfers between devices with their start and end apart: 13, of which 10 were waited for; matrix products, arithmetic and copies ran while one was open for 12% of the time, Pallas kernels for 0%

profile of v3, /device:TPU:0, one launch (start us, length us, event | category | flops | bytes accessed | tf_op | source)
XLA Modules:
  0.0 607.7 jit_solution(12108226633629013840)
XLA Ops:
  6.5 2.3 copy.23
  8.8 12.7 %all-gather.4.cloned.1.call-done = bf16[256,3072]{0,1:T(8,128)(2,1)} async-done(((bf16[256,1536]{0,1:T(8,128)(2,1)}), bf16[256,3072]{0,1:T(8,128)(2,1)}) %all-gather.4.cloned.1.call-update) | async-done | bytes 1572880 | tf_op jit(solution)/shard_map/all_gather | solution.py:59
  21.5 3.9 all-to-all-start
  26.2 18.9 %all-to-all-done = bf16[256,4,768]{0,2,1:T(8,128)(2,1)S(1)} async-done(((bf16[256,4,768]{0,2,1:T(8,128)(2,1)}), bf16[256,4,768]{0,2,1:T(8,128)(2,1)S(1)}, u32[]{:S(2)}, u32[]{:S(2)}) %all-to-all-start) | async-done | bytes 1572896 | tf_op jit(solution)/shard_map/all_to_all | solution.py:60
  45.8 5.5 fusion.16
  51.4 5.0 fusion.17
  56.4 3.1 pad_maximum_fusion
  60.9 5.0 fusion.19
  65.9 5.1 fusion.18
  71.1 3.2 pad_maximum_fusion.1
  74.8 121.6 %collective-permute-done = bf16[2,1024,1536]{1,2,0:T(8,128)(2,1)} collective-permute-done((bf16[2,1024,1536]{1,2,0:T(8,128)(2,1)}, bf16[2,1024,1536]{1,2,0:T(8,128)(2,1)}, u32[]{:S(2)}, u32[]{:S(2)}) %collective-permute-start) | collective-permute-done | bytes 6291488 | tf_op jit(solution)/shard_map/ppermute | solution.py:49
  196.4 7.8 %fusion.5 = bf16[1024,1536]{0,1:T(8,128)(2,1)} fusion(bf16[2,1024,1536]{1,2,0:T(8,128)(2,1)} %collective-permute-done, f32[1536]{0:T(1024)S(1)} %get-tuple-element.6, pred[1024]{0:T(1024)(128)(4,1)S(1)} %fusion.42, bf16[1024,768]{1,0:T(8,128)(2,1)S(1)} %bitcast.147, bf16[768,12288]{1,0:T(8,128)(2,1)} %param.8, s32[]{:T(128)S(6)} %select_n.84), kind=kOutput, calls=%fused_computation.10 | convolution fusion | flops 2426929152 | bytes 10230788 | tf_op jit(solution)/shard_map/dot_general | solution.py:80
  205.7 5.2 fusion.15
  210.9 67.3 %collective-permute-done.1 = bf16[1024,1536]{0,1:T(8,128)(2,1)S(1)} collective-permute-done((bf16[1024,1536]{0,1:T(8,128)(2,1)}, bf16[1024,1536]{0,1:T(8,128)(2,1)S(1)}, u32[]{:S(2)}, u32[]{:S(2)}) %collective-permute-start.1) | collective-permute-done | bytes 3145760 | tf_op jit(solution)/shard_map/ppermute | solution.py:51
  278.2 5.9 fusion.7
  284.4 8.3 %fusion.2 = bf16[1024,1536]{0,1:T(8,128)(2,1)} fusion(bf16[2,1024,1536]{1,2,0:T(8,128)(2,1)} %collective-permute-done.3, f32[1536]{0:T(1024)S(1)} %get-tuple-element.5, pred[1024]{0:T(1024)(128)(4,1)S(1)} %fusion.44, bf16[1024,768]{1,0:T(8,128)(2,1)} %bitcast.149, bf16[768,12288]{1,0:T(8,128)(2,1)} %param.8, s32[]{:T(128)S(6)} %select_n.93), kind=kOutput, calls=%fused_computation.5 | convolution fusion | flops 2426929152 | bytes 10230788 | tf_op jit(solution)/shard_map/dot_general | solution.py:80
  293.3 5.2 fusion.11
  298.5 62.3 %collective-permute-done.4 = bf16[1024,1536]{0,1:T(8,128)(2,1)S(1)} collective-permute-done((bf16[1024,1536]{0,1:T(8,128)(2,1)}, bf16[1024,1536]{0,1:T(8,128)(2,1)S(1)}, u32[]{:S(2)}, u32[]{:S(2)}) %collective-permute-start.4) | collective-permute-done | bytes 3145760 | tf_op jit(solution)/shard_map/ppermute | solution.py:51
  360.8 5.9 fusion.4
  366.8 1.8 collective-permute-start.2
  369.4 1.6 fusion.61
  372.4 2.1 convolution_convert_fusion.1
  374.5 53.2 %reduce-scatter.7.cloned.1.call-done = bf16[256,1536]{0,1:T(8,128)(2,1)} async-done(((bf16[1024,1536]{0,1:T(8,128)(2,1)}), bf16[256,1536]{0,1:T(8,128)(2,1)}) %reduce-scatter.7.cloned.1.call-update) | async-done | bytes 786448 | tf_op jit(solution)/shard_map/reduce_scatter | solution.py:99
  427.8 1.6 fusion.62
  430.7 2.1 convolution_convert_fusion
  433.1 26.3 %all-gather.6.cloned.1.call-done = bf16[1024,512]{0,1:T(8,128)(2,1)} async-done(((bf16[256,512]{0,1:T(8,128)(2,1)}), bf16[1024,512]{0,1:T(8,128)(2,1)}) %all-gather.6.cloned.1.call-update) | async-done | bytes 1048592 | tf_op jit(solution)/shard_map/all_gather | solution.py:103
  459.4 10.2 %fusion.21 = f32[1024,3072]{1,0:T(8,128)} fusion(bf16[1024,512]{0,1:T(8,128)(2,1)} %all-gather.6.cloned.1.call-done, bf16[1024,3072]{1,0:T(8,128)(2,1)} %param.10), kind=kOutput, calls=%fused_computation.40 | convolution fusion | flops 3221225472 | bytes 16777216 | tf_op jit(solution)/shard_map/dot_general | solution.py:104
  469.7 19.7 %all-gather.8.cloned.1.call-done = bf16[1024,512]{0,1:T(8,128)(2,1)} async-done(((bf16[256,512]{0,1:T(8,128)(2,1)}), bf16[1024,512]{0,1:T(8,128)(2,1)}) %all-gather.8.cloned.1.call-update) | async-done | bytes 1048592 | tf_op jit(solution)/shard_map/all_gather | solution.py:103
  489.4 13.9 %convolution_add_fusion = f32[1024,3072]{1,0:T(8,128)} fusion(f32[1024,3072]{1,0:T(8,128)} %fusion.21, bf16[1024,512]{0,1:T(8,128)(2,1)} %all-gather.8.cloned.1.call-done, bf16[1024,3072]{1,0:T(8,128)(2,1)} %param.10), kind=kOutput, calls=%fused_computation.30 | convolution fusion | flops 3224371200 | bytes 29360128 | tf_op jit(solution)/shard_map/dot_general | solution.py:104
  503.4 19.9 %reduce-scatter.9.cloned.1.call-done = f32[1024,1536]{1,0:T(8,128)} async-done(((f32[1024,3072]{1,0:T(8,128)}), f32[1024,1536]{1,0:T(8,128)}) %reduce-scatter.9.cloned.1.call-update) | async-done | bytes 6291472 | tf_op jit(solution)/shard_map/reduce_scatter | solution.py:108
  523.3 74.3 %reduce-scatter.11.cloned.1.call-done = f32[256,1536]{1,0:T(8,128)} async-done(((f32[1024,1536]{1,0:T(8,128)}), f32[256,1536]{1,0:T(8,128)}) %reduce-scatter.11.cloned.1.call-update) | async-done | bytes 1572880 | tf_op jit(solution)/shard_map/reduce_scatter | solution.py:109
  597.6 2.7 broadcast_add_fusion
  (36 shorter events, 9.9 us)
Async XLA Ops:
  6.5 15.0 %all-gather.4.cloned.1.call-start = ((), (), s32[]{:S(2)}) async-start(), calls=%async_computation.5 | async-start | bytes 2359296 | tf_op jit(solution)/shard_map/all_gather | solution.py:59
  21.5 23.6 %all-to-all-start = ((bf16[256,4,768]{0,2,1:T(8,128)(2,1)}), bf16[256,4,768]{0,2,1:T(8,128)(2,1)S(1)}, u32[]{:S(2)}, u32[]{:S(2)}) async-start(bf16[256,4,768]{0,2,1:T(8,128)(2,1)} %bitcast.151), calls=%async_computation | async-start | bytes 3145728 | tf_op jit(solution)/shard_map/all_to_all | solution.py:60
  25.4 344.0 %reduce-scatter.5.cloned.1.call-start = ((), (), s32[]{:S(2)}) async-start(), calls=%async_computation.6 | async-start | bytes 3932160 | tf_op jit(solution)/shard_map/reduce_scatter | solution.py:99
  45.8 150.6 %copy-start = (bf16[4,256,768]{2,1,0:T(8,128)(2,1)}, bf16[4,256,768]{2,1,0:T(8,128)(2,1)S(1)}, u32[]{:S(2)}) copy-start(bf16[4,256,768]{2,1,0:T(8,128)(2,1)S(1)} %copy.24) | copy-start | bytes 4718596
  59.5 136.9 %collective-permute-start = (bf16[2,1024,1536]{1,2,0:T(8,128)(2,1)}, bf16[2,1024,1536]{1,2,0:T(8,128)(2,1)}, u32[]{:S(2)}, u32[]{:S(2)}) collective-permute-start(bf16[2,1024,1536]{1,2,0:T(8,128)(2,1)} %pad_maximum_fusion), channel_id=1, source_target_pairs={{0,8},{8,0},{16,24},{24,16},{1,9},{9,1},{17,25},{25,17},{2,10},{10... | collective-permute-start | bytes 18874376 | tf_op jit(solution)/shard_map/ppermute | solution.py:49
  74.3 210.1 %collective-permute-start.3 = (bf16[2,1024,1536]{1,2,0:T(8,128)(2,1)}, bf16[2,1024,1536]{1,2,0:T(8,128)(2,1)}, u32[]{:S(2)}, u32[]{:S(2)}) collective-permute-start(bf16[2,1024,1536]{1,2,0:T(8,128)(2,1)} %pad_maximum_fusion.1), channel_id=1, source_target_pairs={{0,16},{8,24},{16,0},{24,8},{1,17},{9,25},{17,1},{25,9},{2,18},{10... | collective-permute-start | bytes 18874376 | tf_op jit(solution)/shard_map/ppermute | solution.py:49
  204.2 74.0 %collective-permute-start.1 = (bf16[1024,1536]{0,1:T(8,128)(2,1)}, bf16[1024,1536]{0,1:T(8,128)(2,1)S(1)}, u32[]{:S(2)}, u32[]{:S(2)}) collective-permute-start(bf16[1024,1536]{0,1:T(8,128)(2,1)} %fusion.5), channel_id=1, source_target_pairs={{0,16},{8,24},{16,0},{24,8},{1,17},{9,25},{17,1},{25,9},{2,18},{10... | collective-permute-start | bytes 9437192 | tf_op jit(solution)/shard_map/ppermute | solution.py:51
  284.1 143.7 %reduce-scatter.7.cloned.1.call-start = ((), (), s32[]{:S(2)}) async-start(), calls=%async_computation.8 | async-start | bytes 3932160 | tf_op jit(solution)/shard_map/reduce_scatter | solution.py:99
  292.7 68.2 %collective-permute-start.4 = (bf16[1024,1536]{0,1:T(8,128)(2,1)}, bf16[1024,1536]{0,1:T(8,128)(2,1)S(1)}, u32[]{:S(2)}, u32[]{:S(2)}) collective-permute-start(bf16[1024,1536]{0,1:T(8,128)(2,1)} %fusion.2), channel_id=1, source_target_pairs={{0,8},{8,0},{16,24},{24,16},{1,9},{9,1},{17,25},{25,17},{2,10},{10... | collective-permute-start | bytes 9437192 | tf_op jit(solution)/shard_map/ppermute | solution.py:51
  366.7 92.7 %all-gather.6.cloned.1.call-start = ((), (), s32[]{:S(2)}) async-start(), calls=%async_computation.7 | async-start | bytes 1310720 | tf_op jit(solution)/shard_map/all_gather | solution.py:103
  366.8 1.8 collective-permute-start.2
  374.5 114.9 %all-gather.8.cloned.1.call-start = ((), (), s32[]{:S(2)}) async-start(), calls=%async_computation.9 | async-start | bytes 1310720 | tf_op jit(solution)/shard_map/all_gather | solution.py:103
  432.8 90.4 %reduce-scatter.9.cloned.1.call-start = ((), (), s32[]{:S(2)}) async-start(), calls=%async_computation.10 | async-start | bytes 18874368 | tf_op jit(solution)/shard_map/reduce_scatter | solution.py:108
  503.3 20.0 %copy-start.1 = (bf16[1536]{0:T(1024)(128)(2,1)S(1)}, bf16[1536]{0:T(1024)(128)(2,1)}, u32[]{:S(2)}) copy-start(bf16[1536]{0:T(1024)(128)(2,1)} %param.11) | copy-start | bytes 9220
  503.3 94.3 %reduce-scatter.11.cloned.1.call-start = ((), (), s32[]{:S(2)}) async-start(), calls=%async_computation.11 | async-start | bytes 7864320 | tf_op jit(solution)/shard_map/reduce_scatter | solution.py:109
Sparse Core Ops, SparseCore 0:
  9.0 12.4 all-gather.3
  284.2 60.6 reduce-scatter.4
  366.9 60.8 reduce-scatter.6
  429.2 30.1 all-gather.5
  460.8 28.4 all-gather.7
  503.4 19.7 reduce-scatter.8
  526.2 71.3 reduce-scatter.10

commit v4 on v3

v4 whole, which is shorter than its diff:
```python
import jax
import jax.numpy as jnp
from jax import lax
from jax.sharding import PartitionSpec as P

HD = 128
SEQ = 256


def softmax_rows(scores, allowed):
    scores = jnp.where(allowed, scores, -1e30)
    row_max = jnp.max(scores, axis=-1, keepdims=True)
    weights = jnp.exp(scores - row_max)
    row_sum = jnp.sum(weights, axis=-1, keepdims=True)
    return (weights / row_sum).astype(jnp.bfloat16)


def attention(qkv_held, lengths):
    prompts = qkv_held.shape[0] // SEQ
    heads_dev = qkv_held.shape[1] // (3 * HD)
    table = qkv_held.reshape(prompts, SEQ, heads_dev, 3, HD)
    positions = jnp.arange(SEQ)
    causal = positions[None, :] <= positions[:, None]
    live = positions[None, :] < lengths[:, None]
    allowed = causal[None, None] & live[:, None, None, :]
    scores = (
        jnp.einsum(
            "pshd,pthd->phst",
            table[:, :, :, 0],
            table[:, :, :, 1],
            preferred_element_type=jnp.float32,
        )
        * (1.0 / HD**0.5)
    )
    prob_rows = softmax_rows(scores, allowed)
    context = jnp.einsum(
        "phst,pthd->pshd", prob_rows, table[:, :, :, 2], preferred_element_type=jnp.float32
    )
    return context.astype(jnp.bfloat16).reshape(prompts * SEQ, heads_dev * HD)


def shards(features, lengths, w_qkv, b_qkv, w_out, b_out, n_tok, n_ka):
    t = lax.axis_index("tok")
    k = lax.axis_index("ka")
    rows_dev = features.shape[0]
    slab = lax.all_gather(features, "out", axis=1, tiled=True)
    panel = lax.all_to_all(slab, "tok", split_axis=1, concat_axis=0, tiled=True)
    tokens = panel.shape[0]
    n_blocks = tokens // rows_dev
    by_xor = n_blocks == n_ka and n_ka & (n_ka - 1) == 0
    if by_xor:
        order = jnp.bitwise_xor(k, jnp.arange(n_blocks))
        panel = jnp.take(panel.reshape(n_blocks, rows_dev, -1), order, axis=0)
        panel = panel.reshape(tokens, -1)
        prompt_of = jnp.bitwise_xor(k, lax.broadcasted_iota(jnp.int32, (tokens, 1), 0) // rows_dev)
    else:
        prompt_of = lax.broadcasted_iota(jnp.int32, (tokens, 1), 0) // rows_dev
    cols = w_qkv.shape[1]
    width = cols // n_tok
    if n_tok == n_ka:
        transpose = [(a * n_ka + b, b * n_ka + a) for a in range(n_tok) for b in range(n_ka)]
        own_lengths = lax.ppermute(lengths, ("tok", "ka"), transpose)
    else:
        all_lengths = lax.all_gather(lengths, "tok", axis=0, tiled=True)
        per = all_lengths.shape[0] // n_ka
        own_lengths = lax.dynamic_slice_in_dim(all_lengths, k * per, per)
    heads_block = width // (3 * HD)
    n_streams = 2 if heads_block % 2 == 0 else 1
    piece = width // n_streams
    own_rows = prompt_of == t
    block_of = lax.broadcasted_iota(jnp.int32, (1, n_tok, 1), 1)
    here = own_rows[:, :, None] & (block_of == k)
    bias = b_qkv.astype(jnp.float32).reshape(n_streams, piece)
    w_split = w_qkv.reshape(w_qkv.shape[0], n_tok, n_streams, piece)
    w_rows = w_out.shape[0] // n_streams
    terms = None
    for h in range(n_streams):
        w_h = w_split[:, :, h, :].reshape(w_qkv.shape[0], n_tok * piece)
        value = jnp.dot(panel, w_h, preferred_element_type=jnp.float32)
        value = value.reshape(tokens, n_tok, piece) + jnp.where(here, bias[h][None, None, :], 0.0)
        part = value.astype(jnp.bfloat16).reshape(tokens, n_tok * piece)
        slab_sum = lax.psum_scatter(part, "tok", scatter_dimension=1, tiled=True)
        if by_xor:
            blocks = slab_sum.reshape(n_blocks, rows_dev, piece)
            total = blocks[0].astype(jnp.float32)
            for s in range(1, n_ka):
                pairs = [(i, i ^ s) for i in range(n_ka)]
                total = total + lax.ppermute(blocks[s], "ka", pairs).astype(jnp.float32)
            qkv_held = total.astype(jnp.bfloat16)
        else:
            qkv_held = lax.psum_scatter(slab_sum, "ka", scatter_dimension=0, tiled=True)
        context = attention(qkv_held, own_lengths)
        head_group = lax.all_gather(context, "ka", axis=0, tiled=True)
        term = jnp.dot(
            head_group, w_out[h * w_rows:(h + 1) * w_rows], preferred_element_type=jnp.float32
        )
        terms = term if terms is None else terms + term
    summed = lax.psum_scatter(terms, "out", scatter_dimension=1, tiled=True)
    summed = lax.psum_scatter(summed, "tok", scatter_dimension=0, tiled=True)
    return summed + b_out.astype(jnp.float32)


def solution(mesh):
    n_tok, n_ka = mesh.shape["tok"], mesh.shape["ka"]
    placed = (
        P("tok", ("ka", "out")),
        P("tok"),
        P(("ka", "tok"), "out"),
        P(("out", "ka")),
        P(("out", "tok"), "ka"),
        P(("ka", "out")),
    )

    def body(*args):
        return shards(*args, n_tok=n_tok, n_ka=n_ka)

    return jax.shard_map(
        body, mesh=mesh, in_specs=placed, out_specs=P("tok", ("ka", "out")), check_vma=False
    )
```

time: 614 us -> 653 us (1.064)
  local copies, waits for them, and re-layouts: 3.76 us -> 198 us
  waiting for transfers between devices: 476 us -> 351 us
  matrix products: 81.4 us -> 61.1 us
  other arithmetic: 21.6 us -> 8.21 us
    ppermute x4 -> x6, waiting for transfers between devices: 251 us -> 56 us  [shards(): total = total + lax.ppermute(blocks[s], 'ka', pairs).astype(jnp.float32)]
    slice x1 -> x6, local copies, waits for them, and re-layouts: 0.77 us -> 129 us  [the longest x3 123 us: shards(): w_h = w_split[:, :, h, :].reshape(w_qkv.shape[0], n_tok * piece)]
    reduce_scatter x2, waiting for transfers between devices: 53.2 us -> 159 us  [shards(): slab_sum = lax.psum_scatter(part, 'tok', scatter_dimension=1, tiled=True)]
    convert_element_type x0 -> x2, local copies, waits for them, and re-layouts: none -> 33.5 us  [shards(): part = value.astype(jnp.bfloat16).reshape(tokens, n_tok * piece)]
    reshape x0 -> x1, local copies, waits for them, and re-layouts: none -> 29.3 us  [shards(): w_split = w_qkv.reshape(w_qkv.shape[0], n_tok, n_streams, piece)]
    all_to_all x1, waiting for transfers between devices: 18.9 us -> 0.01 us  [shards(): panel = lax.all_to_all(slab, 'tok', split_axis=1, concat_axis=0, tiled=True)]
    dot_general x10 -> x4, matrix products: 71.3 us -> 57 us  [the longest x2 32.9 us: shards(): value = jnp.dot(panel, w_h, preferred_element_type=jnp.float32)]
    all_gather x1, waiting for transfers between devices: 12.7 us -> 0.01 us  [shards(): slab = lax.all_gather(features, 'out', axis=1, tiled=True)]
  transfers between devices with their start and end apart: 13 -> 15, of which waited for: 10 -> 8; matrix products, arithmetic and copies ran while one was open for 12% -> 33% of each run, Pallas kernels for 0% -> 0%
where the time goes in v4:
time: 653 us; the launch traced here: 648 us
  waiting for transfers between devices  351 us (54%)
  local copies, waits for them, and re-layouts  198 us (30%)
  matrix products  61.1 us (9%)
  starting transfers between devices  16.3 us (2%)
  between operations  13.6 us (2%)
  other arithmetic  8.21 us (1%)
    reduce_scatter x2, waiting for transfers between devices, shards(): slab_sum = lax.psum_scatter(part, 'tok', scatter_dimension=1, tiled=True)  159 us
    slice x3, local copies, waits for them, and re-layouts, shards(): w_h = w_split[:, :, h, :].reshape(w_qkv.shape[0], n_tok * piece)  123 us
    reduce_scatter x1, waiting for transfers between devices, shards(): summed = lax.psum_scatter(summed, 'tok', scatter_dimension=0, tiled=True)  73.7 us
    ppermute x6, waiting for transfers between devices, shards(): total = total + lax.ppermute(blocks[s], 'ka', pairs).astype(jnp.float32)  56 us
    all_gather x2, waiting for transfers between devices, shards(): head_group = lax.all_gather(context, 'ka', axis=0, tiled=True)  42.3 us
    convert_element_type x2, local copies, waits for them, and re-layouts, shards(): part = value.astype(jnp.bfloat16).reshape(tokens, n_tok * piece)  33.5 us
    dot_general x2, matrix products, shards(): value = jnp.dot(panel, w_h, preferred_element_type=jnp.float32)  32.9 us
    reshape x1, local copies, waits for them, and re-layouts, shards(): w_split = w_qkv.reshape(w_qkv.shape[0], n_tok, n_streams, piece)  29.3 us
  transfers between devices with their start and end apart: 15, of which 8 were waited for; matrix products, arithmetic and copies ran while one was open for 33% of the time, Pallas kernels for 0%

profile of v4, /device:TPU:0, one launch (start us, length us, event | category | flops | bytes accessed | tf_op | source)
XLA Modules:
  0.0 648.3 jit_solution(1615701862953891190)
XLA Ops:
  6.5 2.3 copy.26
  8.8 29.3 %reshape.320 = bf16[768,4,2,1536]{3,2,1,0:T(2,128)(2,1)} reshape(bf16[768,12288]{1,0:T(8,128)(2,1)} %param.8) | data formatting | bytes 37748736 | tf_op jit(solution)/shard_map/reshape | solution.py:74
  38.2 2.6 copy.27
  40.8 5.3 all-to-all-start
  46.1 35.9 %fusion.26 = (bf16[768,4,1,1536]{3,2,1,0:T(2,128)(2,1)}, bf16[768,4,1,1536]{3,2,1,0:T(2,128)(2,1)}) fusion(bf16[768,4,2,1536]{3,2,1,0:T(2,128)(2,1)} %reshape.320), kind=kLoop, calls=%fused_computation.58 | loop fusion | bytes 37748736 | tf_op jit(solution)/shard_map/slice | solution.py:78
  82.0 43.6 %copy.28 = bf16[768,4,1,1536]{0,3,1,2:T(8,128)(2,1)} copy(bf16[768,4,1,1536]{3,2,1,0:T(2,128)(2,1)} %get-tuple-element.6) | data formatting | bytes 18874368 | tf_op jit(solution)/shard_map/slice | solution.py:78
  126.6 16.3 %add_convert_fusion.1 = bf16[1024,4,1536]{2,0,1:T(8,128)(2,1)} fusion(bf16[1024,768,1]{1,0,2:T(8,128)(2,1)S(1)} %bitcast.94, f32[1536]{0:T(1024)S(1)} %get-tuple-element.14, pred[1024,4]{0,1:T(4,128)(4,1)S(1)} %broadcast_and_fusion, bf16[768,4,1,1536]{0,3,1,2:T(8,128)(2,1)} %copy.28), kind=kOutput, calls=%fused_computation.4 | convolution fusion | flops 9682550784 | bytes 23603200 | tf_op jit(solution)/shard_map/dot_general | solution.py:79
  142.9 16.6 %copy.29 = bf16[1024,4,1536]{0,2,1:T(8,128)(2,1)} copy(bf16[1024,4,1536]{2,0,1:T(8,128)(2,1)} %add_convert_fusion.1) | data formatting | bytes 25165824 | tf_op jit(solution)/shard_map/convert_element_type | solution.py:81
  159.6 44.0 %copy.34 = bf16[768,4,1,1536]{0,3,1,2:T(8,128)(2,1)} copy(bf16[768,4,1,1536]{3,2,1,0:T(2,128)(2,1)} %get-tuple-element.5) | data formatting | bytes 18874368 | tf_op jit(solution)/shard_map/slice | solution.py:78
  203.6 16.6 %add_convert_fusion = bf16[1024,4,1536]{2,0,1:T(8,128)(2,1)} fusion(bf16[1024,768,1]{1,0,2:T(8,128)(2,1)S(1)} %bitcast.95, f32[1536]{0:T(1024)S(1)} %get-tuple-element.13, pred[1024,4]{0,1:T(4,128)(4,1)S(1)} %broadcast_and_fusion, bf16[768,4,1,1536]{0,3,1,2:T(8,128)(2,1)} %copy.34), kind=kOutput, calls=%fused_computation.3 | convolution fusion | flops 9682550784 | bytes 23603200 | tf_op jit(solution)/shard_map/dot_general | solution.py:79
  220.2 16.8 %copy.35 = bf16[1024,4,1536]{0,2,1:T(8,128)(2,1)} copy(bf16[1024,4,1536]{2,0,1:T(8,128)(2,1)} %add_convert_fusion) | data formatting | bytes 25165824 | tf_op jit(solution)/shard_map/convert_element_type | solution.py:81
  237.1 1.8 collective-permute-start.3
  238.9 43.3 %reduce-scatter.5.cloned.1.call-done = bf16[1024,1536]{0,1:T(8,128)(2,1)} async-done(((bf16[1024,6144]{0,1:T(8,128)(2,1)}), bf16[1024,1536]{0,1:T(8,128)(2,1)}) %reduce-scatter.5.cloned.1.call-update) | async-done | bytes 3145744 | tf_op jit(solution)/shard_map/reduce_scatter | solution.py:82
  282.2 2.7 fusion.28
  284.9 1.5 collective-permute-start
  286.3 2.4 collective-permute-start.1
  289.9 116.1 %reduce-scatter.7.cloned.1.call-done = bf16[1024,1536]{0,1:T(8,128)(2,1)} async-done(((bf16[1024,6144]{0,1:T(8,128)(2,1)}), bf16[1024,1536]{0,1:T(8,128)(2,1)}) %reduce-scatter.7.cloned.1.call-update) | async-done | bytes 3145744 | tf_op jit(solution)/shard_map/reduce_scatter | solution.py:82
  406.1 2.7 fusion.27
  408.7 1.5 collective-permute-start.4
  410.2 2.4 collective-permute-start.5
  413.1 2.2 add_convert_fusion.3
  416.3 1.1 convolution_convert_fusion.1
  417.6 38.5 %collective-permute-done.4 = bf16[256,1536]{0,1:T(8,128)(2,1)} collective-permute-done((bf16[256,1536]{0,1:T(8,128)(2,1)}, bf16[256,1536]{0,1:T(8,128)(2,1)}, u32[]{:S(2)}, u32[]{:S(2)}) %collective-permute-start.4) | collective-permute-done | bytes 786464 | tf_op jit(solution)/shard_map/ppermute | solution.py:88
  456.2 17.5 %collective-permute-done.5 = bf16[256,1536]{0,1:T(8,128)(2,1)} collective-permute-done((bf16[256,1536]{0,1:T(8,128)(2,1)S(1)}, bf16[256,1536]{0,1:T(8,128)(2,1)}, u32[]{:S(2)}, u32[]{:S(2)}) %collective-permute-start.5) | collective-permute-done | bytes 786464 | tf_op jit(solution)/shard_map/ppermute | solution.py:88
  473.6 2.2 add_convert_fusion.2
  478.0 10.3 %all-gather.6.cloned.1.call-done = bf16[1024,512]{0,1:T(8,128)(2,1)} async-done(((bf16[256,512]{0,1:T(8,128)(2,1)}), bf16[1024,512]{0,1:T(8,128)(2,1)}) %all-gather.6.cloned.1.call-update) | async-done | bytes 1048592 | tf_op jit(solution)/shard_map/all_gather | solution.py:93
  488.3 10.2 %fusion.5 = f32[1024,3072]{1,0:T(8,128)} fusion(bf16[1024,512]{0,1:T(8,128)(2,1)} %all-gather.6.cloned.1.call-done, bf16[1024,3072]{1,0:T(8,128)(2,1)} %param.10), kind=kOutput, calls=%fused_computation.9 | convolution fusion | flops 3221225472 | bytes 16777216 | tf_op jit(solution)/shard_map/dot_general | solution.py:94
  498.5 32.0 %all-gather.8.cloned.1.call-done = bf16[1024,512]{0,1:T(8,128)(2,1)} async-done(((bf16[256,512]{0,1:T(8,128)(2,1)}), bf16[1024,512]{0,1:T(8,128)(2,1)}) %all-gather.8.cloned.1.call-update) | async-done | bytes 1048592 | tf_op jit(solution)/shard_map/all_gather | solution.py:93
  530.5 13.9 %convolution_add_fusion = f32[1024,3072]{1,0:T(8,128)} fusion(f32[1024,3072]{1,0:T(8,128)} %fusion.5, bf16[1024,512]{0,1:T(8,128)(2,1)} %all-gather.8.cloned.1.call-done, bf16[1024,3072]{1,0:T(8,128)(2,1)} %param.10), kind=kOutput, calls=%fused_computation.7 | convolution fusion | flops 3224371200 | bytes 29360128 | tf_op jit(solution)/shard_map/dot_general | solution.py:94
  544.4 19.9 %reduce-scatter.9.cloned.1.call-done = f32[1024,1536]{1,0:T(8,128)} async-done(((f32[1024,3072]{1,0:T(8,128)}), f32[1024,1536]{1,0:T(8,128)}) %reduce-scatter.9.cloned.1.call-update) | async-done | bytes 6291472 | tf_op jit(solution)/shard_map/reduce_scatter | solution.py:98
  565.0 73.7 %reduce-scatter.11.cloned.1.call-done = f32[256,1536]{1,0:T(8,128)} async-done(((f32[1024,1536]{1,0:T(8,128)}), f32[256,1536]{1,0:T(8,128)}) %reduce-scatter.11.cloned.1.call-update) | async-done | bytes 1572880 | tf_op jit(solution)/shard_map/reduce_scatter | solution.py:99
  638.7 2.7 broadcast_add_fusion
  (44 shorter events, 6.7 us)
Async XLA Ops:
  6.5 31.7 %all-gather.4.cloned.1.call-start = ((), (), s32[]{:S(2)}) async-start(), calls=%async_computation.5 | async-start | bytes 2359296 | tf_op jit(solution)/shard_map/all_gather | solution.py:46
  40.8 84.9 %all-to-all-start = ((bf16[256,4,768]{2,0,1:T(8,128)(2,1)}), bf16[256,4,768]{2,0,1:T(8,128)(2,1)S(1)}, u32[]{:S(2)}, u32[]{:S(2)}) async-start(bf16[256,4,768]{2,0,1:T(8,128)(2,1)} %copy.27), calls=%async_computation | async-start | bytes 3145728 | tf_op jit(solution)/shard_map/all_to_all | solution.py:47
  46.1 236.1 %reduce-scatter.5.cloned.1.call-start = ((), (), s32[]{:S(2)}) async-start(), calls=%async_computation.6 | async-start | bytes 15728640 | tf_op jit(solution)/shard_map/reduce_scatter | solution.py:82
  82.0 43.7 %copy-start = (bf16[3072]{0:T(1024)(128)(2,1)S(1)}, bf16[3072]{0:T(1024)(128)(2,1)}, u32[]{:S(2)}) copy-start(bf16[3072]{0:T(1024)(128)(2,1)} %param.9) | copy-start | bytes 18436
  159.6 246.5 %reduce-scatter.7.cloned.1.call-start = ((), (), s32[]{:S(2)}) async-start(), calls=%async_computation.8 | async-start | bytes 15728640 | tf_op jit(solution)/shard_map/reduce_scatter | solution.py:82
  237.1 251.2 %all-gather.6.cloned.1.call-start = ((), (), s32[]{:S(2)}) async-start(), calls=%async_computation.7 | async-start | bytes 1310720 | tf_op jit(solution)/shard_map/all_gather | solution.py:93
  237.1 52.1 %collective-permute-start.3 = (s32[1]{0:T(128)}, s32[1]{0:T(128)}, u32[]{:S(2)}, u32[]{:S(2)}) collective-permute-start(s32[1]{0:T(128)} %param.7), channel_id=1, source_target_pairs={{0,0},{2,8},{4,16},{6,24},{8,2},{10,10},{12,18},{14,26},{16,4},{18... | collective-permute-start | bytes 20 | tf_op jit(solution)/shard_map/ppermute | solution.py:62
  284.9 127.8 %collective-permute-start = (bf16[256,1536]{0,1:T(8,128)(2,1)}, bf16[256,1536]{0,1:T(8,128)(2,1)}, u32[]{:S(2)}, u32[]{:S(2)}) collective-permute-start(bf16[256,1536]{0,1:T(8,128)(2,1)} %get-tuple-element.10), channel_id=1, source_target_pairs={{0,2},{2,0},{4,6},{6,4},{1,3},{3,1},{5,7},{7,5},{8,10},{10,8},{12,... | collective-permute-start | bytes 2359304 | tf_op jit(solution)/shard_map/ppermute | solution.py:88
  286.3 126.8 %collective-permute-start.1 = (bf16[256,1536]{0,1:T(8,128)(2,1)S(1)}, bf16[256,1536]{0,1:T(8,128)(2,1)}, u32[]{:S(2)}, u32[]{:S(2)}) collective-permute-start(bf16[256,1536]{0,1:T(8,128)(2,1)S(1)} %get-tuple-element.12), channel_id=1, source_target_pairs={{0,4},{2,6},{4,0},{6,2},{1,5},{3,7},{5,1},{7,3},{8,12},{10,14},{12... | collective-permute-start | bytes 2359304 | tf_op jit(solution)/shard_map/ppermute | solution.py:88
  288.8 124.4 %collective-permute-start.2 = (bf16[256,1536]{0,1:T(8,128)(2,1)S(1)}, bf16[256,1536]{0,1:T(8,128)(2,1)}, u32[]{:S(2)}, u32[]{:S(2)}) collective-permute-start(bf16[256,1536]{0,1:T(8,128)(2,1)S(1)} %get-tuple-element.11), channel_id=1, source_target_pairs={{0,6},{2,4},{4,2},{6,0},{1,7},{3,5},{5,3},{7,1},{8,14},{10,12},{12... | collective-permute-start | bytes 2359304 | tf_op jit(solution)/shard_map/ppermute | solution.py:88
  408.7 47.4 %collective-permute-start.4 = (bf16[256,1536]{0,1:T(8,128)(2,1)}, bf16[256,1536]{0,1:T(8,128)(2,1)}, u32[]{:S(2)}, u32[]{:S(2)}) collective-permute-start(bf16[256,1536]{0,1:T(8,128)(2,1)} %get-tuple-element.7), channel_id=1, source_target_pairs={{0,2},{2,0},{4,6},{6,4},{1,3},{3,1},{5,7},{7,5},{8,10},{10,8},{12,... | collective-permute-start | bytes 2359304 | tf_op jit(solution)/shard_map/ppermute | solution.py:88
  410.2 63.4 %collective-permute-start.5 = (bf16[256,1536]{0,1:T(8,128)(2,1)S(1)}, bf16[256,1536]{0,1:T(8,128)(2,1)}, u32[]{:S(2)}, u32[]{:S(2)}) collective-permute-start(bf16[256,1536]{0,1:T(8,128)(2,1)S(1)} %get-tuple-element.9), channel_id=1, source_target_pairs={{0,4},{2,6},{4,0},{6,2},{1,5},{3,7},{5,1},{7,3},{8,12},{10,14},{12... | collective-permute-start | bytes 2359304 | tf_op jit(solution)/shard_map/ppermute | solution.py:88
  412.6 61.0 %collective-permute-start.6 = (bf16[256,1536]{0,1:T(8,128)(2,1)S(1)}, bf16[256,1536]{0,1:T(8,128)(2,1)}, u32[]{:S(2)}, u32[]{:S(2)}) collective-permute-start(bf16[256,1536]{0,1:T(8,128)(2,1)S(1)} %get-tuple-element.8), channel_id=1, source_target_pairs={{0,6},{2,4},{4,2},{6,0},{1,7},{3,5},{5,3},{7,1},{8,14},{10,12},{12... | collective-permute-start | bytes 2359304 | tf_op jit(solution)/shard_map/ppermute | solution.py:88
  417.4 113.1 %all-gather.8.cloned.1.call-start = ((), (), s32[]{:S(2)}) async-start(), calls=%async_computation.9 | async-start | bytes 1310720 | tf_op jit(solution)/shard_map/all_gather | solution.py:93
  477.9 86.4 %reduce-scatter.9.cloned.1.call-start = ((), (), s32[]{:S(2)}) async-start(), calls=%async_computation.10 | async-start | bytes 18874368 | tf_op jit(solution)/shard_map/reduce_scatter | solution.py:98
  544.4 94.3 %reduce-scatter.11.cloned.1.call-start = ((), (), s32[]{:S(2)}) async-start(), calls=%async_computation.11 | async-start | bytes 7864320 | tf_op jit(solution)/shard_map/reduce_scatter | solution.py:99
  564.4 0.7 copy-start.1
Sparse Core Ops, SparseCore 0:
  9.0 12.4 all-gather.3
  159.7 122.4 reduce-scatter.4
  285.3 120.7 reduce-scatter.6
  417.5 70.7 all-gather.5
  489.7 40.7 all-gather.7
  544.5 19.7 reduce-scatter.8
  567.3 71.3 reduce-scatter.10

commit v5 on v4

--- a/solution.py
+++ b/solution.py
@@ -68,17 +68,18 @@
     n_streams = 2 if heads_block % 2 == 0 else 1
     piece = width // n_streams
     own_rows = prompt_of == t
-    block_of = lax.broadcasted_iota(jnp.int32, (1, n_tok, 1), 1)
-    here = own_rows[:, :, None] & (block_of == k)
-    bias = b_qkv.astype(jnp.float32).reshape(n_streams, piece)
-    w_split = w_qkv.reshape(w_qkv.shape[0], n_tok, n_streams, piece)
+    bias = b_qkv.astype(jnp.float32)
     w_rows = w_out.shape[0] // n_streams
+
+    def block(c, h):
+        w_cols = lax.dynamic_slice_in_dim(w_qkv, c * width + h * piece, piece, axis=1)
+        value = jnp.dot(panel, w_cols, preferred_element_type=jnp.float32)
+        value = value + jnp.where(own_rows & (c == k), bias[h * piece:(h + 1) * piece][None, :], 0.0)
+        return value.astype(jnp.bfloat16)
+
     terms = None
     for h in range(n_streams):
-        w_h = w_split[:, :, h, :].reshape(w_qkv.shape[0], n_tok * piece)
-        value = jnp.dot(panel, w_h, preferred_element_type=jnp.float32)
-        value = value.reshape(tokens, n_tok, piece) + jnp.where(here, bias[h][None, None, :], 0.0)
-        part = value.astype(jnp.bfloat16).reshape(tokens, n_tok * piece)
+        part = jnp.concatenate([block(c, h) for c in range(n_tok)], axis=1)
         slab_sum = lax.psum_scatter(part, "tok", scatter_dimension=1, tiled=True)
         if by_xor:
             blocks = slab_sum.reshape(n_blocks, rows_dev, piece)

time: 653 us -> 564 us (0.86)
  local copies, waits for them, and re-layouts: 198 us -> 12.1 us
  waiting for transfers between devices: 351 us -> 432 us
  other arithmetic: 8.21 us -> 26.3 us
    slice x4 -> x1, local copies, waits for them, and re-layouts: 123 us -> 0.01 us  [block(): bias[h * piece:(h + 1) * piece][None, :]]
    reduce_scatter x2, waiting for transfers between devices: 159 us -> 208 us  [shards(): slab_sum = lax.psum_scatter(part, 'tok', scatter_dimension=1, tiled=True)]
    convert_element_type x2, local copies, waits for them, and re-layouts: 33.5 us -> 0.54 us  [shards(): qkv_held = total.astype(jnp.bfloat16)]
    reshape x1 -> x0, local copies, waits for them, and re-layouts: 29.3 us -> none  [shards(): w_split = w_qkv.reshape(w_qkv.shape[0], n_tok, n_streams, piece)]
    all_to_all x1, waiting for transfers between devices: 0.01 us -> 19.5 us  [shards(): panel = lax.all_to_all(slab, 'tok', split_axis=1, concat_axis=0, tiled=True)]
    concatenate x0 -> x2, other arithmetic: none -> 17.9 us  [shards(): part = jnp.concatenate([block(c, h) for c in range(n_tok)], axis=1)]
    all_gather x1, waiting for transfers between devices: 0.01 us -> 12.7 us  [shards(): slab = lax.all_gather(features, 'out', axis=1, tiled=True)]
    dot_general x2 -> x8, matrix products: 32.9 us -> 36.1 us  [block(): value = jnp.dot(panel, w_cols, preferred_element_type=jnp.float32)]
  transfers between devices with their start and end apart: 15 -> 15, of which waited for: 8 -> 10; matrix products, arithmetic and copies ran while one was open for 33% -> 9% of each run, Pallas kernels for 0% -> 0%
where the time goes in v5:
time: 564 us; the launch traced here: 563 us
  waiting for transfers between devices  432 us (77%)
  matrix products  64.3 us (11%)
  other arithmetic  26.3 us (5%)
  starting transfers between devices  15.2 us (3%)
  between operations  13.6 us (2%)
  local copies, waits for them, and re-layouts  12.1 us (2%)
    reduce_scatter x2, waiting for transfers between devices, shards(): slab_sum = lax.psum_scatter(part, 'tok', scatter_dimension=1, tiled=True)  208 us
    reduce_scatter x1, waiting for transfers between devices, shards(): summed = lax.psum_scatter(summed, 'tok', scatter_dimension=0, tiled=True)  73.7 us
    ppermute x6, waiting for transfers between devices, shards(): total = total + lax.ppermute(blocks[s], 'ka', pairs).astype(jnp.float32)  55.7 us
    all_gather x2, waiting for transfers between devices, shards(): head_group = lax.all_gather(context, 'ka', axis=0, tiled=True)  42.3 us
    dot_general x8, matrix products, block(): value = jnp.dot(panel, w_cols, preferred_element_type=jnp.float32)  36.1 us
    dot_general x2, matrix products, shards(): jnp.dot(head_group, w_out[h * w_rows:(h + 1) * w_rows], preferred_element...  24.1 us
    reduce_scatter x1, waiting for transfers between devices, shards(): summed = lax.psum_scatter(terms, 'out', scatter_dimension=1, tiled=True)  19.9 us
    all_to_all x1, waiting for transfers between devices, shards(): panel = lax.all_to_all(slab, 'tok', split_axis=1, concat_axis=0, tiled=True)  19.5 us
  transfers between devices with their start and end apart: 15, of which 10 were waited for; matrix products, arithmetic and copies ran while one was open for 9% of the time, Pallas kernels for 0%

profile of v5, /device:TPU:0, one launch (start us, length us, event | category | flops | bytes accessed | tf_op | source)
XLA Modules:
  0.0 563.1 jit_solution(13229513793019668230)
XLA Ops:
  6.5 2.3 copy.25
  8.8 12.7 %all-gather.4.cloned.1.call-done = bf16[256,3072]{0,1:T(8,128)(2,1)} async-done(((bf16[256,1536]{0,1:T(8,128)(2,1)}), bf16[256,3072]{0,1:T(8,128)(2,1)}) %all-gather.4.cloned.1.call-update) | async-done | bytes 1572880 | tf_op jit(solution)/shard_map/all_gather | solution.py:46
  21.5 2.6 copy.26
  24.1 3.9 all-to-all-start
  28.2 19.5 %all-to-all-done = bf16[256,4,768]{2,0,1:T(8,128)(2,1)S(1)} async-done(((bf16[256,4,768]{2,0,1:T(8,128)(2,1)}), bf16[256,4,768]{2,0,1:T(8,128)(2,1)S(1)}, u32[]{:S(2)}, u32[]{:S(2)}) %all-to-all-start) | async-done | bytes 1572896 | tf_op jit(solution)/shard_map/all_to_all | solution.py:47
  48.7 4.5 add_convert_fusion.4
  53.2 4.5 add_convert_fusion.5
  57.7 4.5 add_convert_fusion.6
  62.2 4.5 add_convert_fusion.7
  66.7 9.0 %pad_maximum_fusion = bf16[1024,6144]{1,0:T(8,128)(2,1)} fusion(bf16[1024,1536]{1,0:T(8,128)(2,1)S(1)} %add_convert_fusion.4, bf16[1024,1536]{1,0:T(8,128)(2,1)S(1)} %add_convert_fusion.5, bf16[1024,1536]{1,0:T(8,128)(2,1)S(1)} %add_convert_fusion.6, bf16[1024,1536]{1,0:T(8,128)(2,1)S(1)} %add_convert_fusion.7), kind=kLoop, calls=%fused_computation.3 | loop fusion | flops 50331648 | bytes 25165824 | tf_op jit(solution)/shard_map/concatenate | solution.py:82
  75.9 4.5 add_convert_fusion
  80.4 4.5 add_convert_fusion.1
  84.9 4.5 add_convert_fusion.2
  89.4 4.7 add_convert_fusion.3
  94.1 9.0 %pad_maximum_fusion.1 = bf16[1024,6144]{1,0:T(8,128)(2,1)} fusion(bf16[1024,1536]{1,0:T(8,128)(2,1)S(1)} %add_convert_fusion, bf16[1024,1536]{1,0:T(8,128)(2,1)S(1)} %add_convert_fusion.1, bf16[1024,1536]{1,0:T(8,128)(2,1)S(1)} %add_convert_fusion.2, bf16[1024,1536]{1,0:T(8,128)(2,1)S(1)} %add_convert_fusion.3), kind=kLoop, calls=%fused_computation.4 | loop fusion | flops 50331648 | bytes 25165824 | tf_op jit(solution)/shard_map/concatenate | solution.py:82
  105.0 91.7 %reduce-scatter.5.cloned.1.call-done = bf16[1024,1536]{1,0:T(8,128)(2,1)} async-done(((bf16[1024,6144]{1,0:T(8,128)(2,1)}), bf16[1024,1536]{1,0:T(8,128)(2,1)}) %reduce-scatter.5.cloned.1.call-update) | async-done | bytes 3145744 | tf_op jit(solution)/shard_map/reduce_scatter | solution.py:83
  196.7 2.6 fusion.33
  200.9 2.4 collective-permute-start.1
  204.6 116.0 %reduce-scatter.7.cloned.1.call-done = bf16[1024,1536]{1,0:T(8,128)(2,1)} async-done(((bf16[1024,6144]{1,0:T(8,128)(2,1)}), bf16[1024,1536]{1,0:T(8,128)(2,1)}) %reduce-scatter.7.cloned.1.call-update) | async-done | bytes 3145744 | tf_op jit(solution)/shard_map/reduce_scatter | solution.py:83
  320.6 2.6 fusion.32
  324.7 2.4 collective-permute-start.5
  327.6 2.2 add_convert_fusion.9
  332.2 38.4 %collective-permute-done.4 = bf16[256,1536]{1,0:T(8,128)(2,1)} collective-permute-done((bf16[256,1536]{1,0:T(8,128)(2,1)}, bf16[256,1536]{1,0:T(8,128)(2,1)}, u32[]{:S(2)}, u32[]{:S(2)}) %collective-permute-start.4) | collective-permute-done | bytes 786464 | tf_op jit(solution)/shard_map/ppermute | solution.py:89
  370.6 17.4 %collective-permute-done.5 = bf16[256,1536]{1,0:T(8,128)(2,1)} collective-permute-done((bf16[256,1536]{1,0:T(8,128)(2,1)S(1)}, bf16[256,1536]{1,0:T(8,128)(2,1)}, u32[]{:S(2)}, u32[]{:S(2)}) %collective-permute-start.5) | collective-permute-done | bytes 786464 | tf_op jit(solution)/shard_map/ppermute | solution.py:89
  388.0 2.2 add_convert_fusion.8
  392.8 10.3 %all-gather.6.cloned.1.call-done = bf16[1024,512]{0,1:T(8,128)(2,1)} async-done(((bf16[256,512]{0,1:T(8,128)(2,1)}), bf16[1024,512]{0,1:T(8,128)(2,1)}) %all-gather.6.cloned.1.call-update) | async-done | bytes 1048592 | tf_op jit(solution)/shard_map/all_gather | solution.py:94
  403.1 10.2 %fusion.3 = f32[1024,3072]{1,0:T(8,128)} fusion(bf16[1024,512]{0,1:T(8,128)(2,1)} %all-gather.6.cloned.1.call-done, bf16[1024,3072]{1,0:T(8,128)(2,1)} %param.10), kind=kOutput, calls=%fused_computation.15 | convolution fusion | flops 3221225472 | bytes 16777216 | tf_op jit(solution)/shard_map/dot_general | solution.py:95
  413.3 32.0 %all-gather.8.cloned.1.call-done = bf16[1024,512]{0,1:T(8,128)(2,1)} async-done(((bf16[256,512]{0,1:T(8,128)(2,1)}), bf16[1024,512]{0,1:T(8,128)(2,1)}) %all-gather.8.cloned.1.call-update) | async-done | bytes 1048592 | tf_op jit(solution)/shard_map/all_gather | solution.py:94
  445.3 13.9 %convolution_add_fusion = f32[1024,3072]{1,0:T(8,128)} fusion(f32[1024,3072]{1,0:T(8,128)} %fusion.3, bf16[1024,512]{0,1:T(8,128)(2,1)} %all-gather.8.cloned.1.call-done, bf16[1024,3072]{1,0:T(8,128)(2,1)} %param.10), kind=kOutput, calls=%fused_computation.13 | convolution fusion | flops 3224371200 | bytes 29360128 | tf_op jit(solution)/shard_map/dot_general | solution.py:95
  459.2 19.9 %reduce-scatter.9.cloned.1.call-done = f32[1024,1536]{1,0:T(8,128)} async-done(((f32[1024,3072]{1,0:T(8,128)}), f32[1024,1536]{1,0:T(8,128)}) %reduce-scatter.9.cloned.1.call-update) | async-done | bytes 6291472 | tf_op jit(solution)/shard_map/reduce_scatter | solution.py:99
  479.8 73.7 %reduce-scatter.11.cloned.1.call-done = f32[256,1536]{1,0:T(8,128)} async-done(((f32[1024,1536]{1,0:T(8,128)}), f32[256,1536]{1,0:T(8,128)}) %reduce-scatter.11.cloned.1.call-update) | async-done | bytes 1572880 | tf_op jit(solution)/shard_map/reduce_scatter | solution.py:100
  553.5 2.7 broadcast_add_fusion
  (49 shorter events, 13.7 us)
Async XLA Ops:
  6.5 15.0 %all-gather.4.cloned.1.call-start = ((), (), s32[]{:S(2)}) async-start(), calls=%async_computation.5 | async-start | bytes 2359296 | tf_op jit(solution)/shard_map/all_gather | solution.py:46
  21.5 6.7 %copy-start = (bf16[3072]{0:T(1024)(128)(2,1)S(1)}, bf16[3072]{0:T(1024)(128)(2,1)}, u32[]{:S(2)}) copy-start(bf16[3072]{0:T(1024)(128)(2,1)} %param.9) | copy-start | bytes 18436
  24.1 23.6 %all-to-all-start = ((bf16[256,4,768]{2,0,1:T(8,128)(2,1)}), bf16[256,4,768]{2,0,1:T(8,128)(2,1)S(1)}, u32[]{:S(2)}, u32[]{:S(2)}) async-start(bf16[256,4,768]{2,0,1:T(8,128)(2,1)} %copy.26), calls=%async_computation | async-start | bytes 3145728 | tf_op jit(solution)/shard_map/all_to_all | solution.py:47
  28.0 168.7 %reduce-scatter.5.cloned.1.call-start = ((), (), s32[]{:S(2)}) async-start(), calls=%async_computation.6 | async-start | bytes 15728640 | tf_op jit(solution)/shard_map/reduce_scatter | solution.py:83
  75.7 244.9 %reduce-scatter.7.cloned.1.call-start = ((), (), s32[]{:S(2)}) async-start(), calls=%async_computation.8 | async-start | bytes 15728640 | tf_op jit(solution)/shard_map/reduce_scatter | solution.py:83
  103.1 300.0 %all-gather.6.cloned.1.call-start = ((), (), s32[]{:S(2)}) async-start(), calls=%async_computation.7 | async-start | bytes 1310720 | tf_op jit(solution)/shard_map/all_gather | solution.py:94
  103.1 100.6 %collective-permute-start.3 = (s32[1]{0:T(128)}, s32[1]{0:T(128)}, u32[]{:S(2)}, u32[]{:S(2)}) collective-permute-start(s32[1]{0:T(128)} %param.7), channel_id=1, source_target_pairs={{0,0},{2,8},{4,16},{6,24},{8,2},{10,10},{12,18},{14,26},{16,4},{18... | collective-permute-start | bytes 20 | tf_op jit(solution)/shard_map/ppermute | solution.py:62
  199.4 127.8 %collective-permute-start = (bf16[256,1536]{1,0:T(8,128)(2,1)}, bf16[256,1536]{1,0:T(8,128)(2,1)}, u32[]{:S(2)}, u32[]{:S(2)}) collective-permute-start(bf16[256,1536]{1,0:T(8,128)(2,1)} %get-tuple-element.8), channel_id=1, source_target_pairs={{0,2},{2,0},{4,6},{6,4},{1,3},{3,1},{5,7},{7,5},{8,10},{10,8},{12,... | collective-permute-start | bytes 2359304 | tf_op jit(solution)/shard_map/ppermute | solution.py:89
  200.9 126.8 %collective-permute-start.1 = (bf16[256,1536]{1,0:T(8,128)(2,1)S(1)}, bf16[256,1536]{1,0:T(8,128)(2,1)}, u32[]{:S(2)}, u32[]{:S(2)}) collective-permute-start(bf16[256,1536]{1,0:T(8,128)(2,1)S(1)} %get-tuple-element.10), channel_id=1, source_target_pairs={{0,4},{2,6},{4,0},{6,2},{1,5},{3,7},{5,1},{7,3},{8,12},{10,14},{12... | collective-permute-start | bytes 2359304 | tf_op jit(solution)/shard_map/ppermute | solution.py:89
  203.3 124.4 %collective-permute-start.2 = (bf16[256,1536]{1,0:T(8,128)(2,1)S(1)}, bf16[256,1536]{1,0:T(8,128)(2,1)}, u32[]{:S(2)}, u32[]{:S(2)}) collective-permute-start(bf16[256,1536]{1,0:T(8,128)(2,1)S(1)} %get-tuple-element.9), channel_id=1, source_target_pairs={{0,6},{2,4},{4,2},{6,0},{1,7},{3,5},{5,3},{7,1},{8,14},{10,12},{12... | collective-permute-start | bytes 2359304 | tf_op jit(solution)/shard_map/ppermute | solution.py:89
  323.2 47.4 %collective-permute-start.4 = (bf16[256,1536]{1,0:T(8,128)(2,1)}, bf16[256,1536]{1,0:T(8,128)(2,1)}, u32[]{:S(2)}, u32[]{:S(2)}) collective-permute-start(bf16[256,1536]{1,0:T(8,128)(2,1)} %get-tuple-element.5), channel_id=1, source_target_pairs={{0,2},{2,0},{4,6},{6,4},{1,3},{3,1},{5,7},{7,5},{8,10},{10,8},{12,... | collective-permute-start | bytes 2359304 | tf_op jit(solution)/shard_map/ppermute | solution.py:89
  324.7 63.2 %collective-permute-start.5 = (bf16[256,1536]{1,0:T(8,128)(2,1)S(1)}, bf16[256,1536]{1,0:T(8,128)(2,1)}, u32[]{:S(2)}, u32[]{:S(2)}) collective-permute-start(bf16[256,1536]{1,0:T(8,128)(2,1)S(1)} %get-tuple-element.7), channel_id=1, source_target_pairs={{0,4},{2,6},{4,0},{6,2},{1,5},{3,7},{5,1},{7,3},{8,12},{10,14},{12... | collective-permute-start | bytes 2359304 | tf_op jit(solution)/shard_map/ppermute | solution.py:89
  327.1 60.8 %collective-permute-start.6 = (bf16[256,1536]{1,0:T(8,128)(2,1)S(1)}, bf16[256,1536]{1,0:T(8,128)(2,1)}, u32[]{:S(2)}, u32[]{:S(2)}) collective-permute-start(bf16[256,1536]{1,0:T(8,128)(2,1)S(1)} %get-tuple-element.6), channel_id=1, source_target_pairs={{0,6},{2,4},{4,2},{6,0},{1,7},{3,5},{5,3},{7,1},{8,14},{10,12},{12... | collective-permute-start | bytes 2359304 | tf_op jit(solution)/shard_map/ppermute | solution.py:89
  332.2 113.1 %all-gather.8.cloned.1.call-start = ((), (), s32[]{:S(2)}) async-start(), calls=%async_computation.9 | async-start | bytes 1310720 | tf_op jit(solution)/shard_map/all_gather | solution.py:94
  392.6 86.6 %reduce-scatter.9.cloned.1.call-start = ((), (), s32[]{:S(2)}) async-start(), calls=%async_computation.10 | async-start | bytes 18874368 | tf_op jit(solution)/shard_map/reduce_scatter | solution.py:99
  459.2 94.3 %reduce-scatter.11.cloned.1.call-start = ((), (), s32[]{:S(2)}) async-start(), calls=%async_computation.11 | async-start | bytes 7864320 | tf_op jit(solution)/shard_map/reduce_scatter | solution.py:100
  479.1 0.7 copy-start.1
Sparse Core Ops, SparseCore 0:
  9.0 12.4 all-gather.3
  75.8 120.9 reduce-scatter.4
  199.8 120.7 reduce-scatter.6
  332.3 70.7 all-gather.5
  404.5 40.7 all-gather.7
  459.3 19.7 reduce-scatter.8
  482.1 71.3 reduce-scatter.10

commit v6 on v5

--- a/solution.py
+++ b/solution.py
@@ -46,15 +46,6 @@
     slab = lax.all_gather(features, "out", axis=1, tiled=True)
     panel = lax.all_to_all(slab, "tok", split_axis=1, concat_axis=0, tiled=True)
     tokens = panel.shape[0]
-    n_blocks = tokens // rows_dev
-    by_xor = n_blocks == n_ka and n_ka & (n_ka - 1) == 0
-    if by_xor:
-        order = jnp.bitwise_xor(k, jnp.arange(n_blocks))
-        panel = jnp.take(panel.reshape(n_blocks, rows_dev, -1), order, axis=0)
-        panel = panel.reshape(tokens, -1)
-        prompt_of = jnp.bitwise_xor(k, lax.broadcasted_iota(jnp.int32, (tokens, 1), 0) // rows_dev)
-    else:
-        prompt_of = lax.broadcasted_iota(jnp.int32, (tokens, 1), 0) // rows_dev
     cols = w_qkv.shape[1]
     width = cols // n_tok
     if n_tok == n_ka:
@@ -66,8 +57,9 @@
         own_lengths = lax.dynamic_slice_in_dim(all_lengths, k * per, per)
     heads_block = width // (3 * HD)
     n_streams = 2 if heads_block % 2 == 0 else 1
+    by_hand = n_tok == 4 and n_streams == 2
     piece = width // n_streams
-    own_rows = prompt_of == t
+    own_rows = (lax.broadcasted_iota(jnp.int32, (tokens, 1), 0) // rows_dev) == t
     bias = b_qkv.astype(jnp.float32)
     w_rows = w_out.shape[0] // n_streams
 
@@ -77,19 +69,30 @@
         value = value + jnp.where(own_rows & (c == k), bias[h * piece:(h + 1) * piece][None, :], 0.0)
         return value.astype(jnp.bfloat16)
 
+    def y_step(h):
+        blocks = [block(jnp.bitwise_xor(t, j), h) for j in range(4)]
+        y_pairs = [(i, i ^ 2) for i in range(4)]
+        low = blocks[0].astype(jnp.float32) + lax.ppermute(blocks[2], "tok", y_pairs).astype(jnp.float32)
+        high = blocks[1].astype(jnp.float32) + lax.ppermute(blocks[3], "tok", y_pairs).astype(jnp.float32)
+        return low, high.astype(jnp.bfloat16)
+
+    def x_step(low, high):
+        x_pairs = [(i, i ^ 1) for i in range(4)]
+        half = piece // 2
+        got = [lax.ppermute(high[:, i * half:(i + 1) * half], "tok", x_pairs) for i in range(2)]
+        return (low + jnp.concatenate(got, axis=1).astype(jnp.float32)).astype(jnp.bfloat16)
+
+    sums = []
+    for h in range(n_streams):
+        if by_hand and h == 1:
+            first, low, high = lax.optimization_barrier((sums[0], *y_step(h)))
+            sums = [first, x_step(low, high)]
+        else:
+            part = jnp.concatenate([block(c, h) for c in range(n_tok)], axis=1)
+            sums.append(lax.psum_scatter(part, "tok", scatter_dimension=1, tiled=True))
     terms = None
-    for h in range(n_streams):
-        part = jnp.concatenate([block(c, h) for c in range(n_tok)], axis=1)
-        slab_sum = lax.psum_scatter(part, "tok", scatter_dimension=1, tiled=True)
-        if by_xor:
-            blocks = slab_sum.reshape(n_blocks, rows_dev, piece)
-            total = blocks[0].astype(jnp.float32)
-            for s in range(1, n_ka):
-                pairs = [(i, i ^ s) for i in range(n_ka)]
-                total = total + lax.ppermute(blocks[s], "ka", pairs).astype(jnp.float32)
-            qkv_held = total.astype(jnp.bfloat16)
-        else:
-            qkv_held = lax.psum_scatter(slab_sum, "ka", scatter_dimension=0, tiled=True)
+    for h, slab_sum in enumerate(sums):
+        qkv_held = lax.psum_scatter(slab_sum, "ka", scatter_dimension=0, tiled=True)
         context = attention(qkv_held, own_lengths)
         head_group = lax.all_gather(context, "ka", axis=0, tiled=True)
         term = jnp.dot(

time: 564 us -> 640 us (1.13)
  waiting for transfers between devices: 432 us -> 519 us
  other arithmetic: 26.3 us -> 18.1 us
  matrix products: 64.3 us -> 70.7 us
    ppermute x6 -> x4, waiting for transfers between devices: 55.7 us -> 290 us  [the longest x1 130 us: y_step(): lax.ppermute(blocks[2], 'tok', y_pairs).astype(jnp.float32)]
    reduce_scatter x2 -> x3, waiting for transfers between devices: 208 us -> 55.1 us  [the longest x2 55.1 us: shards(): qkv_held = lax.psum_scatter(slab_sum, 'ka', scatter_dimension=0, tiled=True)]
    concatenate x2 -> x1, other arithmetic: 17.9 us -> 8.96 us  [shards(): part = jnp.concatenate([block(c, h) for c in range(n_tok)], axis=1)]
  transfers between devices with their start and end apart: 15 -> 14, of which waited for: 10 -> 11; matrix products, arithmetic and copies ran while one was open for 9% -> 7% of each run, Pallas kernels for 0% -> 0%
where the time goes in v6:
time: 640 us; the launch traced here: 639 us
  waiting for transfers between devices  519 us (81%)
  matrix products  70.7 us (11%)
  other arithmetic  18.1 us (3%)
  between operations  13.7 us (2%)
  starting transfers between devices  10.9 us (2%)
  local copies, waits for them, and re-layouts  6.68 us (1%)
    ppermute x1, waiting for transfers between devices, y_step(): lax.ppermute(blocks[2], 'tok', y_pairs).astype(jnp.float32)  130 us
    ppermute x1, waiting for transfers between devices, y_step(): lax.ppermute(blocks[3], 'tok', y_pairs).astype(jnp.float32)  93.1 us
    reduce_scatter x1, waiting for transfers between devices, shards(): summed = lax.psum_scatter(summed, 'tok', scatter_dimension=0, tiled=True)  73.7 us
    ppermute x2, waiting for transfers between devices, x_step(): lax.ppermute(high[:, i * half:(i + 1) * half], 'tok', x_pairs)  66.9 us
    reduce_scatter x2, waiting for transfers between devices, shards(): qkv_held = lax.psum_scatter(slab_sum, 'ka', scatter_dimension=0, tiled=True)  55.1 us
    all_gather x2, waiting for transfers between devices, shards(): head_group = lax.all_gather(context, 'ka', axis=0, tiled=True)  47.9 us
    dot_general x8, matrix products, block(): value = jnp.dot(panel, w_cols, preferred_element_type=jnp.float32)  42.5 us
    dot_general x2, matrix products, shards(): jnp.dot(head_group, w_out[h * w_rows:(h + 1) * w_rows], preferred_element...  24.1 us
  transfers between devices with their start and end apart: 14, of which 11 were waited for; matrix products, arithmetic and copies ran while one was open for 7% of the time, Pallas kernels for 0%

profile of v6, /device:TPU:0, one launch (start us, length us, event | category | flops | bytes accessed | tf_op | source)
XLA Modules:
  0.0 638.9 jit_solution(12887998931979907071)
XLA Ops:
  6.5 2.3 copy.33
  8.9 12.7 %all-gather.4.cloned.1.call-done = bf16[256,3072]{0,1:T(8,128)(2,1)} async-done(((bf16[256,1536]{0,1:T(8,128)(2,1)}), bf16[256,3072]{0,1:T(8,128)(2,1)}) %all-gather.4.cloned.1.call-update) | async-done | bytes 1572880 | tf_op jit(solution)/shard_map/all_gather | solution.py:46
  21.5 3.9 all-to-all-start
  25.5 19.7 %all-to-all-done = bf16[256,4,768]{0,2,1:T(8,128)(2,1)S(1)} async-done(((bf16[256,4,768]{0,2,1:T(8,128)(2,1)}), bf16[256,4,768]{0,2,1:T(8,128)(2,1)S(1)}, u32[]{:S(2)}, u32[]{:S(2)}) %all-to-all-start) | async-done | bytes 1572896 | tf_op jit(solution)/shard_map/all_to_all | solution.py:47
  45.9 5.0 add_convert_fusion.2
  50.9 4.5 add_convert_fusion.3
  55.4 4.5 add_convert_fusion.4
  59.9 4.5 add_convert_fusion.5
  64.4 9.0 %pad_maximum_fusion = bf16[1024,6144]{1,0:T(8,128)(2,1)} fusion(bf16[1024,1536]{1,0:T(8,128)(2,1)S(1)} %add_convert_fusion.2, bf16[1024,1536]{1,0:T(8,128)(2,1)S(1)} %add_convert_fusion.3, bf16[1024,1536]{1,0:T(8,128)(2,1)S(1)} %add_convert_fusion.4, bf16[1024,1536]{1,0:T(8,128)(2,1)S(1)} %add_convert_fusion.5), kind=kLoop, calls=%fused_computation.2 | loop fusion | flops 50331648 | bytes 25165824 | tf_op jit(solution)/shard_map/concatenate | solution.py:91
  73.5 5.6 fusion.4
  79.1 1.5 collective-permute-start
  80.6 5.7 fusion.2
  86.3 1.2 collective-permute-start.1
  87.5 129.8 %collective-permute-done = bf16[1024,1536]{1,0:T(8,128)(2,1)} collective-permute-done((bf16[1024,1536]{1,0:T(8,128)(2,1)}, bf16[1024,1536]{1,0:T(8,128)(2,1)}, u32[]{:S(2)}, u32[]{:S(2)}) %collective-permute-start) | collective-permute-done | bytes 3145760 | tf_op jit(solution)/shard_map/ppermute | solution.py:75
  217.2 6.8 %convert_add_fusion = f32[1024,1536]{1,0:T(8,128)} fusion(bf16[1024,1536]{1,0:T(8,128)(2,1)} %collective-permute-done, bf16[1024,768]{1,0:T(8,128)(2,1)S(1)} %bitcast.103, f32[1536]{0:T(1024)S(1)} %get-tuple-element.13, pred[1024]{0:T(1024)(128)(4,1)S(1)} %get-tuple-element.16, bf16[768,12288]{1,0:T(8,128)(2,1)} %param.8, s32[]{:T(128)S(6)} %select_n.82), kind=kOutput, calls=%fused_computation.13 | convolution fusion | flops 2425356288 | bytes 13376516 | tf_op jit(solution)/shard_map/dot_general | solution.py:68
  224.0 93.1 %collective-permute-done.1 = bf16[1024,1536]{1,0:T(8,128)(2,1)} collective-permute-done((bf16[1024,1536]{1,0:T(8,128)(2,1)}, bf16[1024,1536]{1,0:T(8,128)(2,1)}, u32[]{:S(2)}, u32[]{:S(2)}) %collective-permute-start.1) | collective-permute-done | bytes 3145760 | tf_op jit(solution)/shard_map/ppermute | solution.py:76
  317.1 5.9 add_convert_fusion.1
  323.5 1.5 collective-permute-start.3
  325.6 35.3 %collective-permute-done.3 = bf16[1024,768]{1,0:T(8,128)(2,1)S(1)} collective-permute-done((bf16[1024,768]{1,0:T(8,128)(2,1)S(1)}, bf16[1024,768]{1,0:T(8,128)(2,1)S(1)}, u32[]{:S(2)}, u32[]{:S(2)}) %collective-permute-start.3) | collective-permute-done | bytes 1572896 | tf_op jit(solution)/shard_map/ppermute | solution.py:82
  360.9 31.6 %collective-permute-done.4 = bf16[1024,768]{1,0:T(8,128)(2,1)S(1)} collective-permute-done((bf16[1024,768]{1,0:T(8,128)(2,1)S(1)}, bf16[1024,768]{1,0:T(8,128)(2,1)S(1)}, u32[]{:S(2)}, u32[]{:S(2)}) %collective-permute-start.4) | collective-permute-done | bytes 1572896 | tf_op jit(solution)/shard_map/ppermute | solution.py:82
  392.5 5.6 add_convert_fusion
  398.1 1.9 collective-permute-start.2
  400.8 1.4 copy.39
  404.4 55.1 %reduce-scatter.10.cloned.1.call-done = bf16[256,1536]{1,0:T(8,128)(2,1)} async-done(((bf16[1024,1536]{1,0:T(8,128)(2,1)}), bf16[256,1536]{1,0:T(8,128)(2,1)}) %reduce-scatter.10.cloned.1.call-update) | async-done | bytes 786448 | tf_op jit(solution)/shard_map/reduce_scatter | solution.py:95
  459.5 1.4 copy.44
  463.0 28.1 %all-gather.6.cloned.1.call-done = bf16[1024,512]{0,1:T(8,128)(2,1)} async-done(((bf16[256,512]{0,1:T(8,128)(2,1)}), bf16[1024,512]{0,1:T(8,128)(2,1)}) %all-gather.6.cloned.1.call-update) | async-done | bytes 1048592 | tf_op jit(solution)/shard_map/all_gather | solution.py:97
  491.1 10.2 %fusion.7 = f32[1024,3072]{1,0:T(8,128)} fusion(bf16[1024,512]{0,1:T(8,128)(2,1)} %all-gather.6.cloned.1.call-done, bf16[1024,3072]{1,0:T(8,128)(2,1)} %param.10), kind=kOutput, calls=%fused_computation.20 | convolution fusion | flops 3221225472 | bytes 16777216 | tf_op jit(solution)/shard_map/dot_general | solution.py:98
  501.4 19.7 %all-gather.8.cloned.1.call-done = bf16[1024,512]{0,1:T(8,128)(2,1)} async-done(((bf16[256,512]{0,1:T(8,128)(2,1)}), bf16[1024,512]{0,1:T(8,128)(2,1)}) %all-gather.8.cloned.1.call-update) | async-done | bytes 1048592 | tf_op jit(solution)/shard_map/all_gather | solution.py:97
  521.1 13.9 %convolution_add_fusion = f32[1024,3072]{1,0:T(8,128)} fusion(f32[1024,3072]{1,0:T(8,128)} %fusion.7, bf16[1024,512]{0,1:T(8,128)(2,1)} %all-gather.8.cloned.1.call-done, bf16[1024,3072]{1,0:T(8,128)(2,1)} %param.10), kind=kOutput, calls=%fused_computation.18 | convolution fusion | flops 3224371200 | bytes 29360128 | tf_op jit(solution)/shard_map/dot_general | solution.py:98
  535.0 19.9 %reduce-scatter.12.cloned.1.call-done = f32[1024,1536]{1,0:T(8,128)} async-done(((f32[1024,3072]{1,0:T(8,128)}), f32[1024,1536]{1,0:T(8,128)}) %reduce-scatter.12.cloned.1.call-update) | async-done | bytes 6291472 | tf_op jit(solution)/shard_map/reduce_scatter | solution.py:102
  555.6 73.7 %reduce-scatter.14.cloned.1.call-done = f32[256,1536]{1,0:T(8,128)} async-done(((f32[1024,1536]{1,0:T(8,128)}), f32[256,1536]{1,0:T(8,128)}) %reduce-scatter.14.cloned.1.call-update) | async-done | bytes 1572880 | tf_op jit(solution)/shard_map/reduce_scatter | solution.py:103
  629.3 2.7 broadcast_add_fusion
  (43 shorter events, 7.7 us)
Async XLA Ops:
  6.5 18.9 %copy-start.1 = (bf16[3072]{0:T(1024)(128)(2,1)S(1)}, bf16[3072]{0:T(1024)(128)(2,1)}, u32[]{:S(2)}) copy-start(bf16[3072]{0:T(1024)(128)(2,1)} %param.9) | copy-start | bytes 18436
  6.5 15.0 %all-gather.4.cloned.1.call-start = ((), (), s32[]{:S(2)}) async-start(), calls=%async_computation.6 | async-start | bytes 2359296 | tf_op jit(solution)/shard_map/all_gather | solution.py:46
  21.5 23.6 %all-to-all-start = ((bf16[256,4,768]{0,2,1:T(8,128)(2,1)}), bf16[256,4,768]{0,2,1:T(8,128)(2,1)S(1)}, u32[]{:S(2)}, u32[]{:S(2)}) async-start(bf16[256,4,768]{0,2,1:T(8,128)(2,1)} %bitcast.105), calls=%async_computation | async-start | bytes 3145728 | tf_op jit(solution)/shard_map/all_to_all | solution.py:47
  25.4 297.6 %reduce-scatter.6.cloned.1.call-start = ((), (), s32[]{:S(2)}) async-start(), calls=%async_computation.7 | async-start | bytes 15728640 | tf_op jit(solution)/shard_map/reduce_scatter | solution.py:92
  45.8 171.4 %copy-start = (bf16[4,256,768]{2,1,0:T(8,128)(2,1)}, bf16[4,256,768]{2,1,0:T(8,128)(2,1)S(1)}, u32[]{:S(2)}) copy-start(bf16[4,256,768]{2,1,0:T(8,128)(2,1)S(1)} %copy.34) | copy-start | bytes 4718596
  73.4 327.4 %reduce-scatter.8.cloned.1.call-start = ((), (), s32[]{:S(2)}) async-start(), calls=%async_computation.8 | async-start | bytes 3932160 | tf_op jit(solution)/shard_map/reduce_scatter | solution.py:95
  79.1 138.1 %collective-permute-start = (bf16[1024,1536]{1,0:T(8,128)(2,1)}, bf16[1024,1536]{1,0:T(8,128)(2,1)}, u32[]{:S(2)}, u32[]{:S(2)}) collective-permute-start(bf16[1024,1536]{1,0:T(8,128)(2,1)} %fusion.4), channel_id=1, source_target_pairs={{0,16},{8,24},{16,0},{24,8},{1,17},{9,25},{17,1},{25,9},{2,18},{10... | collective-permute-start | bytes 9437192 | tf_op jit(solution)/shard_map/ppermute | solution.py:75
  86.3 230.9 %collective-permute-start.1 = (bf16[1024,1536]{1,0:T(8,128)(2,1)}, bf16[1024,1536]{1,0:T(8,128)(2,1)}, u32[]{:S(2)}, u32[]{:S(2)}) collective-permute-start(bf16[1024,1536]{1,0:T(8,128)(2,1)} %fusion.2), channel_id=1, source_target_pairs={{0,16},{8,24},{16,0},{24,8},{1,17},{9,25},{17,1},{25,9},{2,18},{10... | collective-permute-start | bytes 9437192 | tf_op jit(solution)/shard_map/ppermute | solution.py:76
  323.1 136.4 %reduce-scatter.10.cloned.1.call-start = ((), (), s32[]{:S(2)}) async-start(), calls=%async_computation.10 | async-start | bytes 3932160 | tf_op jit(solution)/shard_map/reduce_scatter | solution.py:95
  323.5 37.4 %collective-permute-start.3 = (bf16[1024,768]{1,0:T(8,128)(2,1)S(1)}, bf16[1024,768]{1,0:T(8,128)(2,1)S(1)}, u32[]{:S(2)}, u32[]{:S(2)}) collective-permute-start(bf16[1024,768]{1,0:T(8,128)(2,1)S(1)} %get-tuple-element.11), channel_id=1, source_target_pairs={{0,8},{8,0},{16,24},{24,16},{1,9},{9,1},{17,25},{25,17},{2,10},{10... | collective-permute-start | bytes 4718600 | tf_op jit(solution)/shard_map/ppermute | solution.py:82
  325.0 67.5 %collective-permute-start.4 = (bf16[1024,768]{1,0:T(8,128)(2,1)S(1)}, bf16[1024,768]{1,0:T(8,128)(2,1)S(1)}, u32[]{:S(2)}, u32[]{:S(2)}) collective-permute-start(bf16[1024,768]{1,0:T(8,128)(2,1)S(1)} %get-tuple-element.12), channel_id=1, source_target_pairs={{0,8},{8,0},{16,24},{24,16},{1,9},{9,1},{17,25},{25,17},{2,10},{10... | collective-permute-start | bytes 4718600 | tf_op jit(solution)/shard_map/ppermute | solution.py:82
  398.1 93.1 %all-gather.6.cloned.1.call-start = ((), (), s32[]{:S(2)}) async-start(), calls=%async_computation.9 | async-start | bytes 1310720 | tf_op jit(solution)/shard_map/all_gather | solution.py:97
  398.1 1.9 collective-permute-start.2
  404.3 116.8 %all-gather.8.cloned.1.call-start = ((), (), s32[]{:S(2)}) async-start(), calls=%async_computation.11 | async-start | bytes 1310720 | tf_op jit(solution)/shard_map/all_gather | solution.py:97
  462.9 92.0 %reduce-scatter.12.cloned.1.call-start = ((), (), s32[]{:S(2)}) async-start(), calls=%async_computation.12 | async-start | bytes 18874368 | tf_op jit(solution)/shard_map/reduce_scatter | solution.py:102
  535.0 94.3 %reduce-scatter.14.cloned.1.call-start = ((), (), s32[]{:S(2)}) async-start(), calls=%async_computation.13 | async-start | bytes 7864320 | tf_op jit(solution)/shard_map/reduce_scatter | solution.py:103
  554.9 0.7 copy-start.2
Sparse Core Ops, SparseCore 0:
  9.0 12.4 all-gather.3
  73.5 221.8 reduce-scatter.5
  323.2 60.6 reduce-scatter.7
  398.2 61.2 reduce-scatter.9
  460.9 30.2 all-gather.5
  492.5 28.4 all-gather.7
  535.1 19.7 reduce-scatter.11
  557.9 71.3 reduce-scatter.13

commit v7 on v5

--- a/solution.py
+++ b/solution.py
@@ -47,14 +47,8 @@
     panel = lax.all_to_all(slab, "tok", split_axis=1, concat_axis=0, tiled=True)
     tokens = panel.shape[0]
     n_blocks = tokens // rows_dev
+    row_block = lax.broadcasted_iota(jnp.int32, (tokens, 1), 0) // rows_dev
     by_xor = n_blocks == n_ka and n_ka & (n_ka - 1) == 0
-    if by_xor:
-        order = jnp.bitwise_xor(k, jnp.arange(n_blocks))
-        panel = jnp.take(panel.reshape(n_blocks, rows_dev, -1), order, axis=0)
-        panel = panel.reshape(tokens, -1)
-        prompt_of = jnp.bitwise_xor(k, lax.broadcasted_iota(jnp.int32, (tokens, 1), 0) // rows_dev)
-    else:
-        prompt_of = lax.broadcasted_iota(jnp.int32, (tokens, 1), 0) // rows_dev
     cols = w_qkv.shape[1]
     width = cols // n_tok
     if n_tok == n_ka:
@@ -67,21 +61,28 @@
     heads_block = width // (3 * HD)
     n_streams = 2 if heads_block % 2 == 0 else 1
     piece = width // n_streams
-    own_rows = prompt_of == t
     bias = b_qkv.astype(jnp.float32)
+    col_block = lax.broadcasted_iota(jnp.int32, (1, n_tok * piece), 1) // piece
     w_rows = w_out.shape[0] // n_streams
-
-    def block(c, h):
-        w_cols = lax.dynamic_slice_in_dim(w_qkv, c * width + h * piece, piece, axis=1)
-        value = jnp.dot(panel, w_cols, preferred_element_type=jnp.float32)
-        value = value + jnp.where(own_rows & (c == k), bias[h * piece:(h + 1) * piece][None, :], 0.0)
-        return value.astype(jnp.bfloat16)
-
     terms = None
     for h in range(n_streams):
-        part = jnp.concatenate([block(c, h) for c in range(n_tok)], axis=1)
+        xor_rows = by_xor and h == 0 and n_streams > 1
+        if xor_rows:
+            order = jnp.bitwise_xor(k, jnp.arange(n_blocks))
+            rows_in = jnp.take(panel.reshape(n_blocks, rows_dev, -1), order, axis=0).reshape(tokens, -1)
+            prompt_of = jnp.bitwise_xor(k, row_block)
+        else:
+            rows_in = panel
+            prompt_of = row_block
+        w_h = jnp.concatenate(
+            [w_qkv[:, c * width + h * piece:c * width + (h + 1) * piece] for c in range(n_tok)], axis=1
+        )
+        value = jnp.dot(rows_in, w_h, preferred_element_type=jnp.float32)
+        here = (prompt_of == t) & (col_block == k)
+        bias_row = jnp.tile(bias[h * piece:(h + 1) * piece], n_tok)[None, :]
+        part = (value + jnp.where(here, bias_row, 0.0)).astype(jnp.bfloat16)
         slab_sum = lax.psum_scatter(part, "tok", scatter_dimension=1, tiled=True)
-        if by_xor:
+        if xor_rows:
             blocks = slab_sum.reshape(n_blocks, rows_dev, piece)
             total = blocks[0].astype(jnp.float32)
             for s in range(1, n_ka):

time: 564 us -> 617 us (1.094)
  waiting for transfers between devices: 432 us -> 500 us
  other arithmetic: 26.3 us -> 5.37 us
  local copies, waits for them, and re-layouts: 12.1 us -> 23.9 us
    ppermute x6 -> x3, waiting for transfers between devices: 55.7 us -> 93.5 us  [shards(): total = total + lax.ppermute(blocks[s], 'ka', pairs).astype(jnp.float32)]
    all_gather x2, waiting for transfers between devices: 42.3 us -> 65.9 us  [shards(): head_group = lax.all_gather(context, 'ka', axis=0, tiled=True)]
    reduce_scatter x2, waiting for transfers between devices: 208 us -> 226 us  [shards(): slab_sum = lax.psum_scatter(part, 'tok', scatter_dimension=1, tiled=True)]
    concatenate x2 -> x0, other arithmetic: 17.9 us -> none  [shards(): part = jnp.concatenate([block(c, h) for c in range(n_tok)], axis=1)]
    slice x1 -> x2, local copies, waits for them, and re-layouts: 0.01 us -> 14.1 us  [the longest x1 13.4 us: shards(): w_qkv[:, c * width + h * piece:c * width + (h + 1) * piece]]
    all_to_all x1, waiting for transfers between devices: 19.5 us -> 6.3 us  [shards(): panel = lax.all_to_all(slab, 'tok', split_axis=1, concat_axis=0, tiled=True)]
    dot_general x8 -> x2, matrix products: 36.1 us -> 34.8 us  [shards(): value = jnp.dot(rows_in, w_h, preferred_element_type=jnp.float32)]
  transfers between devices with their start and end apart: 15 -> 13, of which waited for: 10 -> 12; matrix products, arithmetic and copies ran while one was open for 9% -> 9% of each run, Pallas kernels for 0% -> 0%
where the time goes in v7:
time: 617 us; the launch traced here: 616 us
  waiting for transfers between devices  500 us (81%)
  matrix products  63 us (10%)
  local copies, waits for them, and re-layouts  23.9 us (4%)
  between operations  13.6 us (2%)
  starting transfers between devices  10.8 us (2%)
    reduce_scatter x2, waiting for transfers between devices, shards(): slab_sum = lax.psum_scatter(part, 'tok', scatter_dimension=1, tiled=True)  226 us
    ppermute x3, waiting for transfers between devices, shards(): total = total + lax.ppermute(blocks[s], 'ka', pairs).astype(jnp.float32)  93.5 us
    reduce_scatter x1, waiting for transfers between devices, shards(): summed = lax.psum_scatter(summed, 'tok', scatter_dimension=0, tiled=True)  73.7 us
    all_gather x2, waiting for transfers between devices, shards(): head_group = lax.all_gather(context, 'ka', axis=0, tiled=True)  65.9 us
    dot_general x2, matrix products, shards(): value = jnp.dot(rows_in, w_h, preferred_element_type=jnp.float32)  34.8 us
    dot_general x2, matrix products, shards(): jnp.dot(head_group, w_out[h * w_rows:(h + 1) * w_rows], preferred_element...  24.1 us
    reduce_scatter x1, waiting for transfers between devices, shards(): summed = lax.psum_scatter(terms, 'out', scatter_dimension=1, tiled=True)  19.9 us
    slice x1, local copies, waits for them, and re-layouts, shards(): w_qkv[:, c * width + h * piece:c * width + (h + 1) * piece]  13.4 us
  transfers between devices with their start and end apart: 13, of which 12 were waited for; matrix products, arithmetic and copies ran while one was open for 9% of the time, Pallas kernels for 0%

profile of v7, /device:TPU:0, one launch (start us, length us, event | category | flops | bytes accessed | tf_op | source)
XLA Modules:
  0.0 616.3 jit_solution(3420522373702060427)
XLA Ops:
  6.5 2.3 copy.27
  8.9 0.8 fusion.48
  9.6 11.9 %all-gather.4.cloned.1.call-done = bf16[256,3072]{0,1:T(8,128)(2,1)} async-done(((bf16[256,1536]{0,1:T(8,128)(2,1)}), bf16[256,3072]{0,1:T(8,128)(2,1)}) %all-gather.4.cloned.1.call-update) | async-done | bytes 1572880 | tf_op jit(solution)/shard_map/all_gather | solution.py:46
  21.5 2.6 copy.28
  24.1 3.9 all-to-all-start
  28.0 13.4 %fusion.46 = (bf16[768,1536]{1,0:T(8,128)(2,1)}, bf16[768,1536]{1,0:T(8,128)(2,1)}, bf16[768,1536]{1,0:T(8,128)(2,1)}, bf16[768,1536]{1,0:T(8,128)(2,1)}, bf16[7...) fusion(bf16[768,12288]{1,0:T(8,128)(2,1)} %param.8), kind=kLoop, calls=%fused_computation.79 | loop fusion | bytes 37748736 | tf_op jit(solution)/shard_map/slice | solution.py:78
  41.4 6.3 %all-to-all-done = bf16[256,4,768]{2,0,1:T(8,128)(2,1)S(1)} async-done(((bf16[256,4,768]{2,0,1:T(8,128)(2,1)}), bf16[256,4,768]{2,0,1:T(8,128)(2,1)S(1)}, u32[]{:S(2)}, u32[]{:S(2)}) %all-to-all-start) | async-done | bytes 1572896 | tf_op jit(solution)/shard_map/all_to_all | solution.py:47
  47.7 17.4 %fusion.2 = bf16[1024,6144]{1,0:T(8,128)(2,1)} fusion(bf16[1024,768]{1,0:T(8,128)(2,1)S(1)} %bitcast.73, f32[6144]{0:T(1024)S(1)} %broadcast_in_dim.78, pred[6144]{0:T(1024)(128)(4,1)S(1)} %fusion.27, pred[1024]{0:T(1024)(128)(4,1)S(1)} %fusion.33, bf16[768,1536]{1,0:T(8,128)(2,1)} %get-tuple-element.11, bf16[768,1536]{1,0:T(8,128)(2,1)} %get-tuple-element.12, ...), kind=kOutput, calls=%fused_computation.4 | convolution fusion | flops 9726590976 | bytes 23624704 | tf_op jit(solution)/shard_map/dot_general | solution.py:80
  65.5 0.6 gather_fusion
  66.5 17.4 %add_convert_fusion = bf16[1024,6144]{1,0:T(8,128)(2,1)} fusion(bf16[1024,768]{1,0:T(8,128)(2,1)S(1)} %bitcast_select_fusion, f32[6144]{0:T(1024)S(1)} %broadcast_in_dim.73, pred[6144]{0:T(1024)(128)(4,1)S(1)} %fusion.27, pred[1024]{0:T(1024)(128)(4,1)S(1)} %fusion.35, bf16[768,1536]{1,0:T(8,128)(2,1)} %get-tuple-element.7, ...), kind=kOutput, calls=%fused_computation.5 | convolution fusion | flops 9726590976 | bytes 23624704 | tf_op jit(solution)/shard_map/dot_general | solution.py:80
  84.0 102.2 %reduce-scatter.8.cloned.1.call-done = bf16[1024,1536]{1,0:T(8,128)(2,1)} async-done(((bf16[1024,6144]{1,0:T(8,128)(2,1)}), bf16[1024,1536]{1,0:T(8,128)(2,1)}) %reduce-scatter.8.cloned.1.call-update) | async-done | bytes 3145744 | tf_op jit(solution)/shard_map/reduce_scatter | solution.py:84
  186.3 123.8 %reduce-scatter.6.cloned.1.call-done = bf16[1024,1536]{1,0:T(8,128)(2,1)} async-done(((bf16[1024,6144]{1,0:T(8,128)(2,1)}), bf16[1024,1536]{1,0:T(8,128)(2,1)}) %reduce-scatter.6.cloned.1.call-update) | async-done | bytes 3145744 | tf_op jit(solution)/shard_map/reduce_scatter | solution.py:84
  310.0 1.8 fusion.47
  311.8 1.5 collective-permute-start
  313.4 2.4 collective-permute-start.1
  316.3 1.8 collective-permute-start.3
  318.9 60.1 %collective-permute-done = bf16[256,1536]{1,0:T(8,128)(2,1)S(1)} collective-permute-done((bf16[256,1536]{1,0:T(8,128)(2,1)S(1)}, bf16[256,1536]{1,0:T(8,128)(2,1)S(1)}, u32[]{:S(2)}, u32[]{:S(2)}) %collective-permute-start) | collective-permute-done | bytes 786464 | tf_op jit(solution)/shard_map/ppermute | solution.py:90
  379.0 7.4 %collective-permute-done.1 = bf16[256,1536]{1,0:T(8,128)(2,1)S(1)} collective-permute-done((bf16[256,1536]{1,0:T(8,128)(2,1)S(1)}, bf16[256,1536]{1,0:T(8,128)(2,1)S(1)}, u32[]{:S(2)}, u32[]{:S(2)}) %collective-permute-start.1) | collective-permute-done | bytes 786464 | tf_op jit(solution)/shard_map/ppermute | solution.py:90
  386.3 26.1 %collective-permute-done.2 = bf16[256,1536]{1,0:T(8,128)(2,1)S(1)} collective-permute-done((bf16[256,1536]{1,0:T(8,128)(2,1)S(1)}, bf16[256,1536]{1,0:T(8,128)(2,1)S(1)}, u32[]{:S(2)}, u32[]{:S(2)}) %collective-permute-start.2) | collective-permute-done | bytes 786464 | tf_op jit(solution)/shard_map/ppermute | solution.py:90
  412.4 1.5 add_convert_fusion.1
  415.1 1.1 convolution_convert_fusion.1
  416.3 2.3 reduce-scatter.10.cloned.1.call-done
  418.6 1.4 copy.35
  420.9 1.1 convolution_convert_fusion
  422.3 46.2 %all-gather.6.cloned.1.call-done = bf16[1024,512]{0,1:T(8,128)(2,1)} async-done(((bf16[256,512]{0,1:T(8,128)(2,1)}), bf16[1024,512]{0,1:T(8,128)(2,1)}) %all-gather.6.cloned.1.call-update) | async-done | bytes 1048592 | tf_op jit(solution)/shard_map/all_gather | solution.py:95
  468.5 10.2 %fusion.18 = f32[1024,3072]{1,0:T(8,128)} fusion(bf16[1024,512]{0,1:T(8,128)(2,1)} %all-gather.6.cloned.1.call-done, bf16[1024,3072]{1,0:T(8,128)(2,1)} %param.10), kind=kOutput, calls=%fused_computation.22 | convolution fusion | flops 3221225472 | bytes 16777216 | tf_op jit(solution)/shard_map/dot_general | solution.py:96
  478.8 19.7 %all-gather.8.cloned.1.call-done = bf16[1024,512]{0,1:T(8,128)(2,1)} async-done(((bf16[256,512]{0,1:T(8,128)(2,1)}), bf16[1024,512]{0,1:T(8,128)(2,1)}) %all-gather.8.cloned.1.call-update) | async-done | bytes 1048592 | tf_op jit(solution)/shard_map/all_gather | solution.py:95
  498.5 13.9 %convolution_add_fusion = f32[1024,3072]{1,0:T(8,128)} fusion(f32[1024,3072]{1,0:T(8,128)} %fusion.18, bf16[1024,512]{0,1:T(8,128)(2,1)} %all-gather.8.cloned.1.call-done, bf16[1024,3072]{1,0:T(8,128)(2,1)} %param.10), kind=kOutput, calls=%fused_computation.20 | convolution fusion | flops 3224371200 | bytes 29360128 | tf_op jit(solution)/shard_map/dot_general | solution.py:96
  512.5 19.9 %reduce-scatter.12.cloned.1.call-done = f32[1024,1536]{1,0:T(8,128)} async-done(((f32[1024,3072]{1,0:T(8,128)}), f32[1024,1536]{1,0:T(8,128)}) %reduce-scatter.12.cloned.1.call-update) | async-done | bytes 6291472 | tf_op jit(solution)/shard_map/reduce_scatter | solution.py:100
  532.4 0.7 copy-done
  533.1 73.7 %reduce-scatter.14.cloned.1.call-done = f32[256,1536]{1,0:T(8,128)} async-done(((f32[1024,1536]{1,0:T(8,128)}), f32[256,1536]{1,0:T(8,128)}) %reduce-scatter.14.cloned.1.call-update) | async-done | bytes 1572880 | tf_op jit(solution)/shard_map/reduce_scatter | solution.py:101
  606.7 2.7 broadcast_add_fusion
  (40 shorter events, 4.6 us)
Async XLA Ops:
  6.5 15.0 %all-gather.4.cloned.1.call-start = ((), (), s32[]{:S(2)}) async-start(), calls=%async_computation.6 | async-start | bytes 2359296 | tf_op jit(solution)/shard_map/all_gather | solution.py:46
  24.1 23.6 %all-to-all-start = ((bf16[256,4,768]{2,0,1:T(8,128)(2,1)}), bf16[256,4,768]{2,0,1:T(8,128)(2,1)S(1)}, u32[]{:S(2)}, u32[]{:S(2)}) async-start(bf16[256,4,768]{2,0,1:T(8,128)(2,1)} %copy.28), calls=%async_computation | async-start | bytes 3145728 | tf_op jit(solution)/shard_map/all_to_all | solution.py:47
  28.0 158.2 %reduce-scatter.8.cloned.1.call-start = ((), (), s32[]{:S(2)}) async-start(), calls=%async_computation.9 | async-start | bytes 15728640 | tf_op jit(solution)/shard_map/reduce_scatter | solution.py:84
  65.1 244.9 %reduce-scatter.6.cloned.1.call-start = ((), (), s32[]{:S(2)}) async-start(), calls=%async_computation.7 | async-start | bytes 15728640 | tf_op jit(solution)/shard_map/reduce_scatter | solution.py:84
  83.9 334.6 %reduce-scatter.10.cloned.1.call-start = ((), (), s32[]{:S(2)}) async-start(), calls=%async_computation.10 | async-start | bytes 3932160 | tf_op jit(solution)/shard_map/reduce_scatter | solution.py:93
  186.2 282.3 %all-gather.6.cloned.1.call-start = ((), (), s32[]{:S(2)}) async-start(), calls=%async_computation.8 | async-start | bytes 1310720 | tf_op jit(solution)/shard_map/all_gather | solution.py:95
  311.8 67.1 %collective-permute-start = (bf16[256,1536]{1,0:T(8,128)(2,1)S(1)}, bf16[256,1536]{1,0:T(8,128)(2,1)S(1)}, u32[]{:S(2)}, u32[]{:S(2)}) collective-permute-start(bf16[256,1536]{1,0:T(8,128)(2,1)S(1)} %get-tuple-element.13), channel_id=1, source_target_pairs={{0,2},{2,0},{4,6},{6,4},{1,3},{3,1},{5,7},{7,5},{8,10},{10,8},{12,... | collective-permute-start | bytes 2359304 | tf_op jit(solution)/shard_map/ppermute | solution.py:90
  313.4 73.0 %collective-permute-start.1 = (bf16[256,1536]{1,0:T(8,128)(2,1)S(1)}, bf16[256,1536]{1,0:T(8,128)(2,1)S(1)}, u32[]{:S(2)}, u32[]{:S(2)}) collective-permute-start(bf16[256,1536]{1,0:T(8,128)(2,1)S(1)} %get-tuple-element.15), channel_id=1, source_target_pairs={{0,4},{2,6},{4,0},{6,2},{1,5},{3,7},{5,1},{7,3},{8,12},{10,14},{12... | collective-permute-start | bytes 2359304 | tf_op jit(solution)/shard_map/ppermute | solution.py:90
  315.8 96.6 %collective-permute-start.2 = (bf16[256,1536]{1,0:T(8,128)(2,1)S(1)}, bf16[256,1536]{1,0:T(8,128)(2,1)S(1)}, u32[]{:S(2)}, u32[]{:S(2)}) collective-permute-start(bf16[256,1536]{1,0:T(8,128)(2,1)S(1)} %get-tuple-element.14), channel_id=1, source_target_pairs={{0,6},{2,4},{4,2},{6,0},{1,7},{3,5},{5,3},{7,1},{8,14},{10,12},{12... | collective-permute-start | bytes 2359304 | tf_op jit(solution)/shard_map/ppermute | solution.py:90
  316.3 1.8 collective-permute-start.3
  416.2 82.2 %all-gather.8.cloned.1.call-start = ((), (), s32[]{:S(2)}) async-start(), calls=%async_computation.11 | async-start | bytes 1310720 | tf_op jit(solution)/shard_map/all_gather | solution.py:95
  422.0 110.3 %reduce-scatter.12.cloned.1.call-start = ((), (), s32[]{:S(2)}) async-start(), calls=%async_computation.12 | async-start | bytes 18874368 | tf_op jit(solution)/shard_map/reduce_scatter | solution.py:100
  512.4 94.3 %reduce-scatter.14.cloned.1.call-start = ((), (), s32[]{:S(2)}) async-start(), calls=%async_computation.13 | async-start | bytes 7864320 | tf_op jit(solution)/shard_map/reduce_scatter | solution.py:101
  532.4 0.7 copy-start
Sparse Core Ops, SparseCore 0:
  9.0 12.4 all-gather.3
  65.2 120.9 reduce-scatter.7
  189.3 120.7 reduce-scatter.5
  312.2 106.3 reduce-scatter.9
  420.0 48.4 all-gather.5
  469.9 28.4 all-gather.7
  512.5 19.7 reduce-scatter.11
  535.4 71.3 reduce-scatter.13

commit v8 on v5

--- a/solution.py
+++ b/solution.py
@@ -39,7 +39,7 @@
     return context.astype(jnp.bfloat16).reshape(prompts * SEQ, heads_dev * HD)
 
 
-def shards(features, lengths, w_qkv, b_qkv, w_out, b_out, n_tok, n_ka):
+def shards(features, lengths, w_qkv, b_qkv, w_out, b_out, n_tok, n_ka, n_out):
     t = lax.axis_index("tok")
     k = lax.axis_index("ka")
     rows_dev = features.shape[0]
@@ -92,17 +92,20 @@
             qkv_held = lax.psum_scatter(slab_sum, "ka", scatter_dimension=0, tiled=True)
         context = attention(qkv_held, own_lengths)
         head_group = lax.all_gather(context, "ka", axis=0, tiled=True)
-        term = jnp.dot(
-            head_group, w_out[h * w_rows:(h + 1) * w_rows], preferred_element_type=jnp.float32
+        term = jnp.einsum(
+            "tsd,doc->tosc",
+            head_group.reshape(n_tok, tokens // n_tok, -1),
+            w_out[h * w_rows:(h + 1) * w_rows].reshape(w_rows, n_out, -1),
+            preferred_element_type=jnp.float32,
         )
         terms = term if terms is None else terms + term
-    summed = lax.psum_scatter(terms, "out", scatter_dimension=1, tiled=True)
-    summed = lax.psum_scatter(summed, "tok", scatter_dimension=0, tiled=True)
-    return summed + b_out.astype(jnp.float32)
+    terms = terms.reshape(n_tok * n_out, tokens // n_tok, -1)
+    summed = lax.psum_scatter(terms, ("tok", "out"), scatter_dimension=0, tiled=True)
+    return summed[0] + b_out.astype(jnp.float32)
 
 
 def solution(mesh):
-    n_tok, n_ka = mesh.shape["tok"], mesh.shape["ka"]
+    n_tok, n_ka, n_out = mesh.shape["tok"], mesh.shape["ka"], mesh.shape["out"]
     placed = (
         P("tok", ("ka", "out")),
         P("tok"),
@@ -113,7 +116,7 @@
     )
 
     def body(*args):
-        return shards(*args, n_tok=n_tok, n_ka=n_ka)
+        return shards(*args, n_tok=n_tok, n_ka=n_ka, n_out=n_out)
 
     return jax.shard_map(
         body, mesh=mesh, in_specs=placed, out_specs=P("tok", ("ka", "out")), check_vma=False

time: 564 us -> 559 us (level)
  waiting for transfers between devices: 432 us -> 416 us
  local copies, waits for them, and re-layouts: 12.1 us -> 27 us
    all_gather x2, waiting for transfers between devices: 42.3 us -> 28.8 us  [shards(): head_group = lax.all_gather(context, 'ka', axis=0, tiled=True)]
    unnamed x5 -> x7, local copies, waits for them, and re-layouts: 2.95 us -> 8.99 us
    reduce_scatter x2 -> x1, waiting for transfers between devices: 93.6 us -> 90.2 us  [shards(): lax.psum_scatter(terms, ('tok', 'out'), scatter_dimension=0, tiled=True)]
  transfers between devices with their start and end apart: 15 -> 14, of which waited for: 10 -> 8; matrix products, arithmetic and copies ran while one was open for 9% -> 12% of each run, Pallas kernels for 0% -> 0%
where the time goes in v8:
time: 559 us; the launch traced here: 558 us
  waiting for transfers between devices  416 us (74%)
  matrix products  59.9 us (11%)
  local copies, waits for them, and re-layouts  27 us (5%)
  other arithmetic  26.3 us (5%)
  starting transfers between devices  15.2 us (3%)
  between operations  13.7 us (2%)
    reduce_scatter x2, waiting for transfers between devices, shards(): slab_sum = lax.psum_scatter(part, 'tok', scatter_dimension=1, tiled=True)  209 us
    reduce_scatter x1, waiting for transfers between devices, shards(): lax.psum_scatter(terms, ('tok', 'out'), scatter_dimension=0, tiled=True)  90.2 us
    ppermute x6, waiting for transfers between devices, shards(): total = total + lax.ppermute(blocks[s], 'ka', pairs).astype(jnp.float32)  56.2 us
    dot_general x8, matrix products, block(): value = jnp.dot(panel, w_cols, preferred_element_type=jnp.float32)  36.1 us
    all_gather x2, waiting for transfers between devices, shards(): head_group = lax.all_gather(context, 'ka', axis=0, tiled=True)  28.8 us
    dot_general x2, matrix products, shards(): jnp.einsum('tsd,doc->tosc', head_group.reshape(n_tok, tokens // n_tok, -1...  19.7 us
    all_to_all x1, waiting for transfers between devices, shards(): panel = lax.all_to_all(slab, 'tok', split_axis=1, concat_axis=0, tiled=True)  19.5 us
    concatenate x2, other arithmetic, shards(): part = jnp.concatenate([block(c, h) for c in range(n_tok)], axis=1)  18 us
  transfers between devices with their start and end apart: 14, of which 8 were waited for; matrix products, arithmetic and copies ran while one was open for 12% of the time, Pallas kernels for 0%

profile of v8, /device:TPU:0, one launch (start us, length us, event | category | flops | bytes accessed | tf_op | source)
XLA Modules:
  0.0 558.1 jit_solution(2109988091365647547)
XLA Ops:
  6.5 2.3 copy.33
  8.8 12.7 %all-gather.4.cloned.1.call-done = bf16[256,3072]{0,1:T(8,128)(2,1)} async-done(((bf16[256,1536]{0,1:T(8,128)(2,1)}), bf16[256,3072]{0,1:T(8,128)(2,1)}) %all-gather.4.cloned.1.call-update) | async-done | bytes 1572880 | tf_op jit(solution)/shard_map/all_gather | solution.py:46
  21.5 2.6 copy.34
  24.1 3.9 all-to-all-start
  28.2 19.5 %all-to-all-done = bf16[256,4,768]{2,0,1:T(8,128)(2,1)S(1)} async-done(((bf16[256,4,768]{2,0,1:T(8,128)(2,1)}), bf16[256,4,768]{2,0,1:T(8,128)(2,1)S(1)}, u32[]{:S(2)}, u32[]{:S(2)}) %all-to-all-start) | async-done | bytes 1572896 | tf_op jit(solution)/shard_map/all_to_all | solution.py:47
  48.7 4.5 add_convert_fusion.4
  53.2 4.5 add_convert_fusion.5
  57.7 4.5 add_convert_fusion.6
  62.2 4.5 add_convert_fusion.7
  66.7 9.0 %pad_maximum_fusion = bf16[1024,6144]{1,0:T(8,128)(2,1)} fusion(bf16[1024,1536]{1,0:T(8,128)(2,1)S(1)} %add_convert_fusion.4, bf16[1024,1536]{1,0:T(8,128)(2,1)S(1)} %add_convert_fusion.5, bf16[1024,1536]{1,0:T(8,128)(2,1)S(1)} %add_convert_fusion.6, bf16[1024,1536]{1,0:T(8,128)(2,1)S(1)} %add_convert_fusion.7), kind=kLoop, calls=%fused_computation.3 | loop fusion | flops 50331648 | bytes 25165824 | tf_op jit(solution)/shard_map/concatenate | solution.py:82
  75.9 4.5 add_convert_fusion
  80.4 4.5 add_convert_fusion.1
  84.9 4.5 add_convert_fusion.2
  89.4 4.7 add_convert_fusion.3
  94.1 9.0 %pad_maximum_fusion.1 = bf16[1024,6144]{1,0:T(8,128)(2,1)} fusion(bf16[1024,1536]{1,0:T(8,128)(2,1)S(1)} %add_convert_fusion, bf16[1024,1536]{1,0:T(8,128)(2,1)S(1)} %add_convert_fusion.1, bf16[1024,1536]{1,0:T(8,128)(2,1)S(1)} %add_convert_fusion.2, bf16[1024,1536]{1,0:T(8,128)(2,1)S(1)} %add_convert_fusion.3), kind=kLoop, calls=%fused_computation.4 | loop fusion | flops 50331648 | bytes 25165824 | tf_op jit(solution)/shard_map/concatenate | solution.py:82
  105.1 91.7 %reduce-scatter.4.cloned.1.call-done = bf16[1024,1536]{1,0:T(8,128)(2,1)} async-done(((bf16[1024,6144]{1,0:T(8,128)(2,1)}), bf16[1024,1536]{1,0:T(8,128)(2,1)}) %reduce-scatter.4.cloned.1.call-update) | async-done | bytes 3145744 | tf_op jit(solution)/shard_map/reduce_scatter | solution.py:83
  200.1 2.4 collective-permute-start.1
  203.7 116.9 %reduce-scatter.6.cloned.1.call-done = bf16[1024,1536]{1,0:T(8,128)(2,1)} async-done(((bf16[1024,6144]{1,0:T(8,128)(2,1)}), bf16[1024,1536]{1,0:T(8,128)(2,1)}) %reduce-scatter.6.cloned.1.call-update) | async-done | bytes 3145744 | tf_op jit(solution)/shard_map/reduce_scatter | solution.py:83
  320.6 2.9 fusion.30
  325.1 2.4 collective-permute-start.5
  332.6 38.1 %collective-permute-done.4 = bf16[256,1536]{1,0:T(8,128)(2,1)} collective-permute-done((bf16[256,1536]{1,0:T(8,128)(2,1)}, bf16[256,1536]{1,0:T(8,128)(2,1)}, u32[]{:S(2)}, u32[]{:S(2)}) %collective-permute-start.4) | collective-permute-done | bytes 786464 | tf_op jit(solution)/shard_map/ppermute | solution.py:89
  370.7 18.0 %collective-permute-done.5 = bf16[256,1536]{1,0:T(8,128)(2,1)} collective-permute-done((bf16[256,1536]{1,0:T(8,128)(2,1)}, bf16[256,1536]{1,0:T(8,128)(2,1)}, u32[]{:S(2)}, u32[]{:S(2)}) %collective-permute-start.5) | collective-permute-done | bytes 786464 | tf_op jit(solution)/shard_map/ppermute | solution.py:89
  393.6 4.9 fusion.29
  398.5 2.9 copy.62
  401.4 3.2 copy.66
  404.6 2.3 copy.40
  406.9 10.2 %fusion.35 = f32[4,256,2,1536]{3,1,2,0:T(8,128)} fusion(bf16[4,256,512,1]{2,1,3,0:T(8,128)(2,1)} %bitcast.108, bf16[512,2,1536,1]{0,2,1,3:T(8,128)(2,1)} %bitcast.100), kind=kOutput, calls=%fused_computation.77 | convolution fusion | flops 3221225472 | bytes 16777216 | tf_op jit(solution)/shard_map/tsd,doc->tosc/dot_general | solution.py:95
  417.1 28.7 %all-gather.8.cloned.1.call-done = bf16[1024,512]{0,1:T(8,128)(2,1)} async-done(((bf16[256,512]{0,1:T(8,128)(2,1)}), bf16[1024,512]{0,1:T(8,128)(2,1)}) %all-gather.8.cloned.1.call-update) | async-done | bytes 1048592 | tf_op jit(solution)/shard_map/all_gather | solution.py:94
  445.8 2.3 copy.48
  448.1 9.5 %convolution_add_fusion = f32[4,256,2,1536]{3,1,2,0:T(8,128)} fusion(f32[4,256,2,1536]{3,1,2,0:T(8,128)} %fusion.35, bf16[4,256,512,1]{2,1,3,0:T(8,128)(2,1)} %bitcast.99, bf16[512,2,1536,1]{0,2,1,3:T(8,128)(2,1)S(1)} %bitcast.97), kind=kOutput, calls=%fused_computation.13 | convolution fusion | flops 3224371200 | bytes 29360128 | tf_op jit(solution)/shard_map/tsd,doc->tosc/dot_general | solution.py:95
  458.3 90.2 %reduce-scatter.8.cloned.1.call-done = f32[1,256,1536]{2,1,0:T(8,128)} async-done(((f32[8,256,1536]{2,1,0:T(8,128)}), f32[1,256,1536]{2,1,0:T(8,128)}) %reduce-scatter.8.cloned.1.call-update) | async-done | bytes 1572880 | tf_op jit(solution)/shard_map/reduce_scatter | solution.py:103
  548.5 2.7 bitcast_add_fusion
  (51 shorter events, 19.9 us)
Async XLA Ops:
  6.5 15.0 %all-gather.4.cloned.1.call-start = ((), (), s32[]{:S(2)}) async-start(), calls=%async_computation.4 | async-start | bytes 2359296 | tf_op jit(solution)/shard_map/all_gather | solution.py:46
  21.5 6.7 %copy-start = (bf16[3072]{0:T(1024)(128)(2,1)S(1)}, bf16[3072]{0:T(1024)(128)(2,1)}, u32[]{:S(2)}) copy-start(bf16[3072]{0:T(1024)(128)(2,1)} %param.9) | copy-start | bytes 18436
  24.1 23.6 %all-to-all-start = ((bf16[256,4,768]{2,0,1:T(8,128)(2,1)}), bf16[256,4,768]{2,0,1:T(8,128)(2,1)S(1)}, u32[]{:S(2)}, u32[]{:S(2)}) async-start(bf16[256,4,768]{2,0,1:T(8,128)(2,1)} %copy.34), calls=%async_computation | async-start | bytes 3145728 | tf_op jit(solution)/shard_map/all_to_all | solution.py:47
  28.0 168.8 %reduce-scatter.4.cloned.1.call-start = ((), (), s32[]{:S(2)}) async-start(), calls=%async_computation.5 | async-start | bytes 15728640 | tf_op jit(solution)/shard_map/reduce_scatter | solution.py:83
  75.7 244.9 %reduce-scatter.6.cloned.1.call-start = ((), (), s32[]{:S(2)}) async-start(), calls=%async_computation.7 | async-start | bytes 15728640 | tf_op jit(solution)/shard_map/reduce_scatter | solution.py:83
  103.1 301.5 %all-gather.6.cloned.1.call-start = ((), (), s32[]{:S(2)}) async-start(), calls=%async_computation.6 | async-start | bytes 1310720 | tf_op jit(solution)/shard_map/all_gather | solution.py:94
  103.2 99.8 %collective-permute-start.3 = (s32[1]{0:T(128)}, s32[1]{0:T(128)}, u32[]{:S(2)}, u32[]{:S(2)}) collective-permute-start(s32[1]{0:T(128)} %param.7), channel_id=1, source_target_pairs={{0,0},{2,8},{4,16},{6,24},{8,2},{10,10},{12,18},{14,26},{16,4},{18... | collective-permute-start | bytes 20 | tf_op jit(solution)/shard_map/ppermute | solution.py:62
  198.5 128.9 %collective-permute-start = (bf16[256,1536]{1,0:T(8,128)(2,1)S(1)}, bf16[256,1536]{1,0:T(8,128)(2,1)}, u32[]{:S(2)}, u32[]{:S(2)}) collective-permute-start(bf16[256,1536]{1,0:T(8,128)(2,1)S(1)} %get-tuple-element.10), channel_id=1, source_target_pairs={{0,2},{2,0},{4,6},{6,4},{1,3},{3,1},{5,7},{7,5},{8,10},{10,8},{12,... | collective-permute-start | bytes 2359304 | tf_op jit(solution)/shard_map/ppermute | solution.py:89
  200.1 127.9 %collective-permute-start.1 = (bf16[256,1536]{1,0:T(8,128)(2,1)S(1)}, bf16[256,1536]{1,0:T(8,128)(2,1)}, u32[]{:S(2)}, u32[]{:S(2)}) collective-permute-start(bf16[256,1536]{1,0:T(8,128)(2,1)S(1)} %get-tuple-element.12), channel_id=1, source_target_pairs={{0,4},{2,6},{4,0},{6,2},{1,5},{3,7},{5,1},{7,3},{8,12},{10,14},{12... | collective-permute-start | bytes 2359304 | tf_op jit(solution)/shard_map/ppermute | solution.py:89
  202.5 125.5 %collective-permute-start.2 = (bf16[256,1536]{1,0:T(8,128)(2,1)S(1)}, bf16[256,1536]{1,0:T(8,128)(2,1)}, u32[]{:S(2)}, u32[]{:S(2)}) collective-permute-start(bf16[256,1536]{1,0:T(8,128)(2,1)S(1)} %get-tuple-element.11), channel_id=1, source_target_pairs={{0,6},{2,4},{4,2},{6,0},{1,7},{3,5},{5,3},{7,1},{8,14},{10,12},{12... | collective-permute-start | bytes 2359304 | tf_op jit(solution)/shard_map/ppermute | solution.py:89
  323.6 47.2 %collective-permute-start.4 = (bf16[256,1536]{1,0:T(8,128)(2,1)}, bf16[256,1536]{1,0:T(8,128)(2,1)}, u32[]{:S(2)}, u32[]{:S(2)}) collective-permute-start(bf16[256,1536]{1,0:T(8,128)(2,1)} %get-tuple-element.7), channel_id=1, source_target_pairs={{0,2},{2,0},{4,6},{6,4},{1,3},{3,1},{5,7},{7,5},{8,10},{10,8},{12,... | collective-permute-start | bytes 2359304 | tf_op jit(solution)/shard_map/ppermute | solution.py:89
  325.1 63.7 %collective-permute-start.5 = (bf16[256,1536]{1,0:T(8,128)(2,1)}, bf16[256,1536]{1,0:T(8,128)(2,1)}, u32[]{:S(2)}, u32[]{:S(2)}) collective-permute-start(bf16[256,1536]{1,0:T(8,128)(2,1)} %get-tuple-element.9), channel_id=1, source_target_pairs={{0,4},{2,6},{4,0},{6,2},{1,5},{3,7},{5,1},{7,3},{8,12},{10,14},{12... | collective-permute-start | bytes 2359304 | tf_op jit(solution)/shard_map/ppermute | solution.py:89
  327.5 61.3 %collective-permute-start.6 = (bf16[256,1536]{1,0:T(8,128)(2,1)S(1)}, bf16[256,1536]{1,0:T(8,128)(2,1)}, u32[]{:S(2)}, u32[]{:S(2)}) collective-permute-start(bf16[256,1536]{1,0:T(8,128)(2,1)S(1)} %get-tuple-element.8), channel_id=1, source_target_pairs={{0,6},{2,4},{4,2},{6,0},{1,7},{3,5},{5,3},{7,1},{8,14},{10,12},{12... | collective-permute-start | bytes 2359304 | tf_op jit(solution)/shard_map/ppermute | solution.py:89
  332.5 113.3 %all-gather.8.cloned.1.call-start = ((), (), s32[]{:S(2)}) async-start(), calls=%async_computation.8 | async-start | bytes 1310720 | tf_op jit(solution)/shard_map/all_gather | solution.py:94
  393.3 155.2 %reduce-scatter.8.cloned.1.call-start = ((), (), s32[]{:S(2)}) async-start(), calls=%async_computation.9 | async-start | bytes 14155776 | tf_op jit(solution)/shard_map/reduce_scatter | solution.py:103
  457.6 0.7 copy-start.1
Sparse Core Ops, SparseCore 0:
  9.0 12.4 all-gather.3
  75.8 120.9 reduce-scatter.3
  199.9 120.7 reduce-scatter.5
  332.6 70.7 all-gather.5
  404.8 40.9 all-gather.7
  457.8 90.6 reduce-scatter.7

commit v9 on v8

--- a/solution.py
+++ b/solution.py
@@ -44,7 +44,18 @@
     k = lax.axis_index("ka")
     rows_dev = features.shape[0]
     slab = lax.all_gather(features, "out", axis=1, tiled=True)
-    panel = lax.all_to_all(slab, "tok", split_axis=1, concat_axis=0, tiled=True)
+    chunk = slab.shape[1] // n_tok
+    if n_tok & (n_tok - 1) == 0:
+        pieces = [None] * n_tok
+        pieces[0] = lax.dynamic_slice_in_dim(slab, t * chunk, chunk, axis=1)
+        for s in range(1, n_tok):
+            owed = lax.dynamic_slice_in_dim(slab, jnp.bitwise_xor(t, s) * chunk, chunk, axis=1)
+            pieces[s] = lax.ppermute(owed, "tok", [(i, i ^ s) for i in range(n_tok)])
+        stacked = jnp.stack(pieces)
+        panel = jnp.take(stacked, jnp.bitwise_xor(t, jnp.arange(n_tok)), axis=0)
+        panel = panel.reshape(n_tok * rows_dev, chunk)
+    else:
+        panel = lax.all_to_all(slab, "tok", split_axis=1, concat_axis=0, tiled=True)
     tokens = panel.shape[0]
     n_blocks = tokens // rows_dev
     by_xor = n_blocks == n_ka and n_ka & (n_ka - 1) == 0

time: 559 us -> 556 us (level)
    all_to_all x1 -> x0, waiting for transfers between devices: 19.5 us -> none  [shards(): panel = lax.all_to_all(slab, 'tok', split_axis=1, concat_axis=0, tiled=True)]
    ppermute x0 -> x3, waiting for transfers between devices: none -> 17.7 us  [shards(): pieces[s] = lax.ppermute(owed, 'tok', [(i, i ^ s) for i in range(n_tok)])]
  transfers between devices with their start and end apart: 14 -> 16, of which waited for: 8 -> 9; matrix products, arithmetic and copies ran while one was open for 12% -> 12% of each run, Pallas kernels for 0% -> 0%
where the time goes in v9:
time: 556 us; the launch traced here: 555 us
  waiting for transfers between devices  416 us (75%)
  matrix products  60 us (11%)
  other arithmetic  26.7 us (5%)
  local copies, waits for them, and re-layouts  24.2 us (4%)
  starting transfers between devices  14.9 us (3%)
  between operations  13.7 us (2%)
    reduce_scatter x2, waiting for transfers between devices, shards(): slab_sum = lax.psum_scatter(part, 'tok', scatter_dimension=1, tiled=True)  208 us
    reduce_scatter x1, waiting for transfers between devices, shards(): lax.psum_scatter(terms, ('tok', 'out'), scatter_dimension=0, tiled=True)  90.2 us
    ppermute x6, waiting for transfers between devices, shards(): total = total + lax.ppermute(blocks[s], 'ka', pairs).astype(jnp.float32)  56.2 us
    dot_general x8, matrix products, block(): value = jnp.dot(panel, w_cols, preferred_element_type=jnp.float32)  36.2 us
    all_gather x2, waiting for transfers between devices, shards(): head_group = lax.all_gather(context, 'ka', axis=0, tiled=True)  28.8 us
    dot_general x2, matrix products, shards(): jnp.einsum('tsd,doc->tosc', head_group.reshape(n_tok, tokens // n_tok, -1...  19.7 us
    concatenate x2, other arithmetic, shards(): part = jnp.concatenate([block(c, h) for c in range(n_tok)], axis=1)  18 us
    ppermute x3, waiting for transfers between devices, shards(): pieces[s] = lax.ppermute(owed, 'tok', [(i, i ^ s) for i in range(n_tok)])  17.7 us
  transfers between devices with their start and end apart: 16, of which 9 were waited for; matrix products, arithmetic and copies ran while one was open for 12% of the time, Pallas kernels for 0%

profile of v9, /device:TPU:0, one launch (start us, length us, event | category | flops | bytes accessed | tf_op | source)
XLA Modules:
  0.0 555.3 jit_solution(4675299752848228208)
XLA Ops:
  7.4 14.0 %all-gather.4.cloned.1.call-done = bf16[256,3072]{1,0:T(8,128)(2,1)} async-done(((bf16[256,1536]{1,0:T(8,128)(2,1)}), bf16[256,3072]{1,0:T(8,128)(2,1)}) %all-gather.4.cloned.1.call-update) | async-done | bytes 1572880 | tf_op jit(solution)/shard_map/all_gather | solution.py:46
  26.5 8.4 %collective-permute-done = bf16[256,768]{1,0:T(8,128)(2,1)S(1)} collective-permute-done((bf16[256,768]{1,0:T(8,128)(2,1)S(1)}, bf16[256,768]{1,0:T(8,128)(2,1)S(1)}, u32[]{:S(2)}, u32[]{:S(2)}) %collective-permute-start) | collective-permute-done | bytes 393248 | tf_op jit(solution)/shard_map/ppermute | solution.py:53
  34.9 9.2 %collective-permute-done.1 = bf16[256,768]{1,0:T(8,128)(2,1)S(1)} collective-permute-done((bf16[256,768]{1,0:T(8,128)(2,1)S(1)}, bf16[256,768]{1,0:T(8,128)(2,1)S(1)}, u32[]{:S(2)}, u32[]{:S(2)}) %collective-permute-start.1) | collective-permute-done | bytes 393248 | tf_op jit(solution)/shard_map/ppermute | solution.py:53
  46.1 4.5 add_convert_fusion.5
  50.6 4.5 add_convert_fusion.6
  55.1 4.5 add_convert_fusion.7
  59.6 4.5 add_convert_fusion.4
  64.1 8.9 %pad_maximum_fusion = bf16[1024,6144]{1,0:T(8,128)(2,1)} fusion(bf16[1024,1536]{1,0:T(8,128)(2,1)S(1)} %add_convert_fusion.4, bf16[1024,1536]{1,0:T(8,128)(2,1)S(1)} %add_convert_fusion.5, bf16[1024,1536]{1,0:T(8,128)(2,1)S(1)} %add_convert_fusion.6, bf16[1024,1536]{1,0:T(8,128)(2,1)S(1)} %add_convert_fusion.7), kind=kLoop, calls=%fused_computation.4 | loop fusion | flops 50331648 | bytes 25165824 | tf_op jit(solution)/shard_map/concatenate | solution.py:93
  73.3 4.5 add_convert_fusion
  77.8 4.5 add_convert_fusion.1
  82.3 4.5 add_convert_fusion.2
  86.8 4.8 add_convert_fusion.3
  91.6 9.0 %pad_maximum_fusion.1 = bf16[1024,6144]{1,0:T(8,128)(2,1)} fusion(bf16[1024,1536]{1,0:T(8,128)(2,1)S(1)} %add_convert_fusion, bf16[1024,1536]{1,0:T(8,128)(2,1)S(1)} %add_convert_fusion.1, bf16[1024,1536]{1,0:T(8,128)(2,1)S(1)} %add_convert_fusion.2, bf16[1024,1536]{1,0:T(8,128)(2,1)S(1)} %add_convert_fusion.3), kind=kLoop, calls=%fused_computation.5 | loop fusion | flops 50331648 | bytes 25165824 | tf_op jit(solution)/shard_map/concatenate | solution.py:93
  102.6 91.4 %reduce-scatter.4.cloned.1.call-done = bf16[1024,1536]{1,0:T(8,128)(2,1)} async-done(((bf16[1024,6144]{1,0:T(8,128)(2,1)}), bf16[1024,1536]{1,0:T(8,128)(2,1)}) %reduce-scatter.4.cloned.1.call-update) | async-done | bytes 3145744 | tf_op jit(solution)/shard_map/reduce_scatter | solution.py:94
  197.3 2.4 collective-permute-start.4
  201.0 116.8 %reduce-scatter.6.cloned.1.call-done = bf16[1024,1536]{1,0:T(8,128)(2,1)} async-done(((bf16[1024,6144]{1,0:T(8,128)(2,1)}), bf16[1024,1536]{1,0:T(8,128)(2,1)}) %reduce-scatter.6.cloned.1.call-update) | async-done | bytes 3145744 | tf_op jit(solution)/shard_map/reduce_scatter | solution.py:94
  317.8 2.9 fusion.29
  322.3 2.4 collective-permute-start.8
  325.2 2.2 add_convert_fusion.9
  329.8 38.2 %collective-permute-done.7 = bf16[256,1536]{1,0:T(8,128)(2,1)} collective-permute-done((bf16[256,1536]{1,0:T(8,128)(2,1)}, bf16[256,1536]{1,0:T(8,128)(2,1)}, u32[]{:S(2)}, u32[]{:S(2)}) %collective-permute-start.7) | collective-permute-done | bytes 786464 | tf_op jit(solution)/shard_map/ppermute | solution.py:100
  367.9 18.0 %collective-permute-done.8 = bf16[256,1536]{1,0:T(8,128)(2,1)} collective-permute-done((bf16[256,1536]{1,0:T(8,128)(2,1)}, bf16[256,1536]{1,0:T(8,128)(2,1)}, u32[]{:S(2)}, u32[]{:S(2)}) %collective-permute-start.8) | collective-permute-done | bytes 786464 | tf_op jit(solution)/shard_map/ppermute | solution.py:100
  385.9 2.3 add_convert_fusion.8
  390.8 4.9 fusion.28
  395.7 2.8 copy.44
  398.6 3.2 copy.48
  401.8 2.3 copy.22
  404.1 10.2 %fusion.34 = f32[4,256,2,1536]{3,1,2,0:T(8,128)} fusion(bf16[4,256,512,1]{2,1,3,0:T(8,128)(2,1)} %bitcast.114, bf16[512,2,1536,1]{0,2,1,3:T(8,128)(2,1)} %bitcast.99), kind=kOutput, calls=%fused_computation.85 | convolution fusion | flops 3221225472 | bytes 16777216 | tf_op jit(solution)/shard_map/tsd,doc->tosc/dot_general | solution.py:106
  414.3 28.8 %all-gather.8.cloned.1.call-done = bf16[1024,512]{0,1:T(8,128)(2,1)} async-done(((bf16[256,512]{0,1:T(8,128)(2,1)}), bf16[1024,512]{0,1:T(8,128)(2,1)}) %all-gather.8.cloned.1.call-update) | async-done | bytes 1048592 | tf_op jit(solution)/shard_map/all_gather | solution.py:105
  443.0 2.3 copy.30
  445.3 9.5 %convolution_add_fusion = f32[4,256,2,1536]{3,1,2,0:T(8,128)} fusion(f32[4,256,2,1536]{3,1,2,0:T(8,128)} %fusion.34, bf16[4,256,512,1]{2,1,3,0:T(8,128)(2,1)} %bitcast.98, bf16[512,2,1536,1]{0,2,1,3:T(8,128)(2,1)S(1)} %bitcast.97), kind=kOutput, calls=%fused_computation.14 | convolution fusion | flops 3224371200 | bytes 29360128 | tf_op jit(solution)/shard_map/tsd,doc->tosc/dot_general | solution.py:106
  455.5 90.2 %reduce-scatter.8.cloned.1.call-done = f32[1,256,1536]{2,1,0:T(8,128)} async-done(((f32[8,256,1536]{2,1,0:T(8,128)}), f32[1,256,1536]{2,1,0:T(8,128)}) %reduce-scatter.8.cloned.1.call-update) | async-done | bytes 1572880 | tf_op jit(solution)/shard_map/reduce_scatter | solution.py:114
  545.7 2.7 bitcast_add_fusion
  (57 shorter events, 22.1 us)
Async XLA Ops:
  6.5 19.9 %copy-start = (bf16[3072]{0:T(1024)(128)(2,1)S(1)}, bf16[3072]{0:T(1024)(128)(2,1)}, u32[]{:S(2)}) copy-start(bf16[3072]{0:T(1024)(128)(2,1)} %param.11) | copy-start | bytes 18436
  6.5 14.9 %all-gather.4.cloned.1.call-start = ((), (), s32[]{:S(2)}) async-start(), calls=%async_computation.3 | async-start | bytes 2359296 | tf_op jit(solution)/shard_map/all_gather | solution.py:46
  7.3 186.7 %reduce-scatter.4.cloned.1.call-start = ((), (), s32[]{:S(2)}) async-start(), calls=%async_computation.4 | async-start | bytes 15728640 | tf_op jit(solution)/shard_map/reduce_scatter | solution.py:94
  22.9 12.0 %collective-permute-start = (bf16[256,768]{1,0:T(8,128)(2,1)S(1)}, bf16[256,768]{1,0:T(8,128)(2,1)S(1)}, u32[]{:S(2)}, u32[]{:S(2)}) collective-permute-start(bf16[256,768]{1,0:T(8,128)(2,1)S(1)} %get-tuple-element.17), channel_id=1, source_target_pairs={{0,8},{8,0},{16,24},{24,16},{1,9},{9,1},{17,25},{25,17},{2,10},{10... | collective-permute-start | bytes 1179656 | tf_op jit(solution)/shard_map/ppermute | solution.py:53
  24.7 19.5 %collective-permute-start.1 = (bf16[256,768]{1,0:T(8,128)(2,1)S(1)}, bf16[256,768]{1,0:T(8,128)(2,1)S(1)}, u32[]{:S(2)}, u32[]{:S(2)}) collective-permute-start(bf16[256,768]{1,0:T(8,128)(2,1)S(1)} %get-tuple-element.16), channel_id=1, source_target_pairs={{0,16},{8,24},{16,0},{24,8},{1,17},{9,25},{17,1},{25,9},{2,18},{10... | collective-permute-start | bytes 1179656 | tf_op jit(solution)/shard_map/ppermute | solution.py:53
  26.2 18.0 %collective-permute-start.2 = (bf16[256,768]{1,0:T(8,128)(2,1)S(1)}, bf16[256,768]{1,0:T(8,128)(2,1)S(1)}, u32[]{:S(2)}, u32[]{:S(2)}) collective-permute-start(bf16[256,768]{1,0:T(8,128)(2,1)S(1)} %get-tuple-element.15), channel_id=1, source_target_pairs={{0,24},{8,16},{16,8},{24,0},{1,25},{9,17},{17,9},{25,1},{2,26},{10... | collective-permute-start | bytes 1179656 | tf_op jit(solution)/shard_map/ppermute | solution.py:53
  73.1 244.7 %reduce-scatter.6.cloned.1.call-start = ((), (), s32[]{:S(2)}) async-start(), calls=%async_computation.6 | async-start | bytes 15728640 | tf_op jit(solution)/shard_map/reduce_scatter | solution.py:94
  100.6 301.1 %all-gather.6.cloned.1.call-start = ((), (), s32[]{:S(2)}) async-start(), calls=%async_computation.5 | async-start | bytes 1310720 | tf_op jit(solution)/shard_map/all_gather | solution.py:105
  100.7 99.5 %collective-permute-start.6 = (s32[1]{0:T(128)}, s32[1]{0:T(128)}, u32[]{:S(2)}, u32[]{:S(2)}) collective-permute-start(s32[1]{0:T(128)} %param.9), channel_id=1, source_target_pairs={{0,0},{2,8},{4,16},{6,24},{8,2},{10,10},{12,18},{14,26},{16,4},{18... | collective-permute-start | bytes 20 | tf_op jit(solution)/shard_map/ppermute | solution.py:73
  195.7 129.0 %collective-permute-start.3 = (bf16[256,1536]{1,0:T(8,128)(2,1)S(1)}, bf16[256,1536]{1,0:T(8,128)(2,1)}, u32[]{:S(2)}, u32[]{:S(2)}) collective-permute-start(bf16[256,1536]{1,0:T(8,128)(2,1)S(1)} %get-tuple-element.11), channel_id=1, source_target_pairs={{0,2},{2,0},{4,6},{6,4},{1,3},{3,1},{5,7},{7,5},{8,10},{10,8},{12,... | collective-permute-start | bytes 2359304 | tf_op jit(solution)/shard_map/ppermute | solution.py:100
  197.3 127.9 %collective-permute-start.4 = (bf16[256,1536]{1,0:T(8,128)(2,1)S(1)}, bf16[256,1536]{1,0:T(8,128)(2,1)}, u32[]{:S(2)}, u32[]{:S(2)}) collective-permute-start(bf16[256,1536]{1,0:T(8,128)(2,1)S(1)} %get-tuple-element.13), channel_id=1, source_target_pairs={{0,4},{2,6},{4,0},{6,2},{1,5},{3,7},{5,1},{7,3},{8,12},{10,14},{12... | collective-permute-start | bytes 2359304 | tf_op jit(solution)/shard_map/ppermute | solution.py:100
  199.7 125.5 %collective-permute-start.5 = (bf16[256,1536]{1,0:T(8,128)(2,1)S(1)}, bf16[256,1536]{1,0:T(8,128)(2,1)}, u32[]{:S(2)}, u32[]{:S(2)}) collective-permute-start(bf16[256,1536]{1,0:T(8,128)(2,1)S(1)} %get-tuple-element.12), channel_id=1, source_target_pairs={{0,6},{2,4},{4,2},{6,0},{1,7},{3,5},{5,3},{7,1},{8,14},{10,12},{12... | collective-permute-start | bytes 2359304 | tf_op jit(solution)/shard_map/ppermute | solution.py:100
  320.8 47.2 %collective-permute-start.7 = (bf16[256,1536]{1,0:T(8,128)(2,1)}, bf16[256,1536]{1,0:T(8,128)(2,1)}, u32[]{:S(2)}, u32[]{:S(2)}) collective-permute-start(bf16[256,1536]{1,0:T(8,128)(2,1)} %get-tuple-element.8), channel_id=1, source_target_pairs={{0,2},{2,0},{4,6},{6,4},{1,3},{3,1},{5,7},{7,5},{8,10},{10,8},{12,... | collective-permute-start | bytes 2359304 | tf_op jit(solution)/shard_map/ppermute | solution.py:100
  322.3 63.7 %collective-permute-start.8 = (bf16[256,1536]{1,0:T(8,128)(2,1)}, bf16[256,1536]{1,0:T(8,128)(2,1)}, u32[]{:S(2)}, u32[]{:S(2)}) collective-permute-start(bf16[256,1536]{1,0:T(8,128)(2,1)} %get-tuple-element.10), channel_id=1, source_target_pairs={{0,4},{2,6},{4,0},{6,2},{1,5},{3,7},{5,1},{7,3},{8,12},{10,14},{12... | collective-permute-start | bytes 2359304 | tf_op jit(solution)/shard_map/ppermute | solution.py:100
  324.7 61.2 %collective-permute-start.9 = (bf16[256,1536]{1,0:T(8,128)(2,1)S(1)}, bf16[256,1536]{1,0:T(8,128)(2,1)}, u32[]{:S(2)}, u32[]{:S(2)}) collective-permute-start(bf16[256,1536]{1,0:T(8,128)(2,1)S(1)} %get-tuple-element.9), channel_id=1, source_target_pairs={{0,6},{2,4},{4,2},{6,0},{1,7},{3,5},{5,3},{7,1},{8,14},{10,12},{12... | collective-permute-start | bytes 2359304 | tf_op jit(solution)/shard_map/ppermute | solution.py:100
  329.7 113.3 %all-gather.8.cloned.1.call-start = ((), (), s32[]{:S(2)}) async-start(), calls=%async_computation.7 | async-start | bytes 1310720 | tf_op jit(solution)/shard_map/all_gather | solution.py:105
  390.5 155.2 %reduce-scatter.8.cloned.1.call-start = ((), (), s32[]{:S(2)}) async-start(), calls=%async_computation.8 | async-start | bytes 14155776 | tf_op jit(solution)/shard_map/reduce_scatter | solution.py:114
  454.8 0.7 copy-start.1
Sparse Core Ops, SparseCore 0:
  8.9 12.4 all-gather.3
  73.2 120.7 reduce-scatter.3
  197.1 120.7 reduce-scatter.5
  329.8 70.7 all-gather.5
  402.0 40.9 all-gather.7
  455.0 90.6 reduce-scatter.7

commit v10 on v9

--- a/solution.py
+++ b/solution.py
@@ -82,15 +82,17 @@
     bias = b_qkv.astype(jnp.float32)
     w_rows = w_out.shape[0] // n_streams
 
-    def block(c, h):
-        w_cols = lax.dynamic_slice_in_dim(w_qkv, c * width + h * piece, piece, axis=1)
-        value = jnp.dot(panel, w_cols, preferred_element_type=jnp.float32)
-        value = value + jnp.where(own_rows & (c == k), bias[h * piece:(h + 1) * piece][None, :], 0.0)
-        return value.astype(jnp.bfloat16)
+    col_block = lax.broadcasted_iota(jnp.int32, (1, n_tok * piece), 1) // piece
+    here = own_rows & (col_block == k)
 
     terms = None
     for h in range(n_streams):
-        part = jnp.concatenate([block(c, h) for c in range(n_tok)], axis=1)
+        w_h = jnp.concatenate(
+            [w_qkv[:, c * width + h * piece:c * width + (h + 1) * piece] for c in range(n_tok)], axis=1
+        )
+        value = jnp.dot(panel, w_h, preferred_element_type=jnp.float32)
+        bias_row = jnp.tile(bias[h * piece:(h + 1) * piece], n_tok)[None, :]
+        part = (value + jnp.where(here, bias_row, 0.0)).astype(jnp.bfloat16)
         slab_sum = lax.psum_scatter(part, "tok", scatter_dimension=1, tiled=True)
         if by_xor:
             blocks = slab_sum.reshape(n_blocks, rows_dev, piece)

time: 556 us -> 551 us (level)
  local copies, waits for them, and re-layouts: 24.2 us -> 41.3 us
  other arithmetic: 26.7 us -> 9.85 us
    concatenate x2 -> x0, other arithmetic: 18 us -> none  [shards(): part = jnp.concatenate([block(c, h) for c in range(n_tok)], axis=1)]
    slice x1 -> x2, local copies, waits for them, and re-layouts: 0.01 us -> 14.3 us  [the longest x1 13.5 us: shards(): w_qkv[:, c * width + h * piece:c * width + (h + 1) * piece]]
    all_gather x1, waiting for transfers between devices: 14 us -> 0.02 us  [shards(): slab = lax.all_gather(features, 'out', axis=1, tiled=True)]
    reduce_scatter x2, waiting for transfers between devices: 208 us -> 217 us  [shards(): slab_sum = lax.psum_scatter(part, 'tok', scatter_dimension=1, tiled=True)]
    dot_general x8 -> x2, matrix products: 36.2 us -> 35 us  [shards(): value = jnp.dot(panel, w_h, preferred_element_type=jnp.float32)]
  transfers between devices with their start and end apart: 16 -> 16, of which waited for: 9 -> 8; matrix products, arithmetic and copies ran while one was open for 12% -> 13% of each run, Pallas kernels for 0% -> 0%
where the time goes in v10:
time: 551 us; the launch traced here: 550 us
  waiting for transfers between devices  411 us (75%)
  matrix products  58.7 us (11%)
  local copies, waits for them, and re-layouts  41.3 us (7%)
  starting transfers between devices  15.9 us (3%)
  between operations  13.7 us (2%)
  other arithmetic  9.85 us (2%)
    reduce_scatter x2, waiting for transfers between devices, shards(): slab_sum = lax.psum_scatter(part, 'tok', scatter_dimension=1, tiled=True)  217 us
    reduce_scatter x1, waiting for transfers between devices, shards(): lax.psum_scatter(terms, ('tok', 'out'), scatter_dimension=0, tiled=True)  90.2 us
    ppermute x6, waiting for transfers between devices, shards(): total = total + lax.ppermute(blocks[s], 'ka', pairs).astype(jnp.float32)  56.1 us
    dot_general x2, matrix products, shards(): value = jnp.dot(panel, w_h, preferred_element_type=jnp.float32)  35 us
    all_gather x2, waiting for transfers between devices, shards(): head_group = lax.all_gather(context, 'ka', axis=0, tiled=True)  28.8 us
    dot_general x2, matrix products, shards(): jnp.einsum('tsd,doc->tosc', head_group.reshape(n_tok, tokens // n_tok, -1...  19.7 us
    ppermute x3, waiting for transfers between devices, shards(): pieces[s] = lax.ppermute(owed, 'tok', [(i, i ^ s) for i in range(n_tok)])  17.4 us
    slice x1, local copies, waits for them, and re-layouts, shards(): w_qkv[:, c * width + h * piece:c * width + (h + 1) * piece]  13.5 us
  transfers between devices with their start and end apart: 16, of which 8 were waited for; matrix products, arithmetic and copies ran while one was open for 13% of the time, Pallas kernels for 0%

profile of v10, /device:TPU:0, one launch (start us, length us, event | category | flops | bytes accessed | tf_op | source)
XLA Modules:
  0.0 550.3 jit_solution(7277942607117833040)
XLA Ops:
  8.2 13.5 %fusion.44 = (bf16[768,1536]{1,0:T(8,128)(2,1)}, bf16[768,1536]{1,0:T(8,128)(2,1)}, bf16[768,1536]{1,0:T(8,128)(2,1)}, bf16[768,1536]{1,0:T(8,128)(2,1)}, bf16[7...) fusion(bf16[768,12288]{1,0:T(8,128)(2,1)} %param.10), kind=kLoop, calls=%fused_computation.87 | loop fusion | bytes 37748736 | tf_op jit(solution)/shard_map/slice | solution.py:91
  21.7 1.5 dynamic-slice_bitcast_fusion
  23.2 3.0 collective-permute-start
  26.2 1.5 collective-permute-start.1
  27.8 8.4 %collective-permute-done = bf16[256,768]{1,0:T(8,128)(2,1)S(1)} collective-permute-done((bf16[256,768]{1,0:T(8,128)(2,1)S(1)}, bf16[256,768]{1,0:T(8,128)(2,1)S(1)}, u32[]{:S(2)}, u32[]{:S(2)}) %collective-permute-start) | collective-permute-done | bytes 393248 | tf_op jit(solution)/shard_map/ppermute | solution.py:53
  36.2 9.0 %collective-permute-done.1 = bf16[256,768]{1,0:T(8,128)(2,1)S(1)} collective-permute-done((bf16[256,768]{1,0:T(8,128)(2,1)S(1)}, bf16[256,768]{1,0:T(8,128)(2,1)S(1)}, u32[]{:S(2)}, u32[]{:S(2)}) %collective-permute-start.1) | collective-permute-done | bytes 393248 | tf_op jit(solution)/shard_map/ppermute | solution.py:53
  47.4 2.1 gather_fusion.1
  49.7 17.9 %fusion.3 = bf16[1024,6144]{1,0:T(8,128)(2,1)} fusion(bf16[1024,768]{1,0:T(8,128)(2,1)S(1)} %bitcast.100, f32[6144]{0:T(1024)S(1)} %broadcast_in_dim.64, pred[6144]{0:T(1024)(128)(4,1)S(1)} %fusion.27, pred[1024]{0:T(1024)(128)(4,1)S(1)} %fusion.32, bf16[768,1536]{1,0:T(8,128)(2,1)} %get-tuple-element.8, bf16[768,1536]{1,0:T(8,128)(2,1)} %get-tuple-element.9, ...), kind=kOutput, calls=%fused_computation.7 | convolution fusion | flops 9726590976 | bytes 23624704 | tf_op jit(solution)/shard_map/dot_general | solution.py:93
  69.3 17.1 %fusion.5 = bf16[1024,6144]{1,0:T(8,128)(2,1)} fusion(bf16[1024,768]{1,0:T(8,128)(2,1)} %bitcast.101, f32[6144]{0:T(1024)S(1)} %broadcast_in_dim.69, pred[6144]{0:T(1024)(128)(4,1)S(1)} %fusion.27, pred[1024]{0:T(1024)(128)(4,1)S(1)} %fusion.32, bf16[768,1536]{1,0:T(8,128)(2,1)} %get-tuple-element.12, bf16[768,1536]{1,0:T(8,128)(2,1)} %get-tuple-element.13, ...), kind=kOutput, calls=%fused_computation.9 | convolution fusion | flops 9726590976 | bytes 23624704 | tf_op jit(solution)/shard_map/dot_general | solution.py:93
  86.5 1.9 collective-permute-start.6
  88.4 100.6 %reduce-scatter.4.cloned.1.call-done = bf16[1024,1536]{1,0:T(8,128)(2,1)} async-done(((bf16[1024,6144]{1,0:T(8,128)(2,1)}), bf16[1024,1536]{1,0:T(8,128)(2,1)}) %reduce-scatter.4.cloned.1.call-update) | async-done | bytes 3145744 | tf_op jit(solution)/shard_map/reduce_scatter | solution.py:96
  188.9 1.8 fusion.47
  190.7 1.5 collective-permute-start.3
  192.2 2.4 collective-permute-start.4
  196.0 116.8 %reduce-scatter.6.cloned.1.call-done = bf16[1024,1536]{1,0:T(8,128)(2,1)} async-done(((bf16[1024,6144]{1,0:T(8,128)(2,1)}), bf16[1024,1536]{1,0:T(8,128)(2,1)}) %reduce-scatter.6.cloned.1.call-update) | async-done | bytes 3145744 | tf_op jit(solution)/shard_map/reduce_scatter | solution.py:96
  312.8 3.0 fusion.46
  315.8 1.5 collective-permute-start.7
  317.2 2.4 collective-permute-start.8
  320.2 2.2 add_convert_fusion.1
  324.8 38.2 %collective-permute-done.7 = bf16[256,1536]{1,0:T(8,128)(2,1)} collective-permute-done((bf16[256,1536]{1,0:T(8,128)(2,1)}, bf16[256,1536]{1,0:T(8,128)(2,1)}, u32[]{:S(2)}, u32[]{:S(2)}) %collective-permute-start.7) | collective-permute-done | bytes 786464 | tf_op jit(solution)/shard_map/ppermute | solution.py:102
  362.9 18.0 %collective-permute-done.8 = bf16[256,1536]{1,0:T(8,128)(2,1)} collective-permute-done((bf16[256,1536]{1,0:T(8,128)(2,1)}, bf16[256,1536]{1,0:T(8,128)(2,1)}, u32[]{:S(2)}, u32[]{:S(2)}) %collective-permute-start.8) | collective-permute-done | bytes 786464 | tf_op jit(solution)/shard_map/ppermute | solution.py:102
  380.9 2.3 add_convert_fusion
  385.8 4.9 fusion.45
  390.7 2.8 copy.44
  393.5 3.2 copy.48
  396.7 2.3 copy.22
  399.0 10.2 %fusion.51 = f32[4,256,2,1536]{3,1,2,0:T(8,128)} fusion(bf16[4,256,512,1]{2,1,3,0:T(8,128)(2,1)} %bitcast.102, bf16[512,2,1536,1]{0,2,1,3:T(8,128)(2,1)} %bitcast.93), kind=kOutput, calls=%fused_computation.94 | convolution fusion | flops 3221225472 | bytes 16777216 | tf_op jit(solution)/shard_map/tsd,doc->tosc/dot_general | solution.py:108
  409.2 28.8 %all-gather.8.cloned.1.call-done = bf16[1024,512]{0,1:T(8,128)(2,1)} async-done(((bf16[256,512]{0,1:T(8,128)(2,1)}), bf16[1024,512]{0,1:T(8,128)(2,1)}) %all-gather.8.cloned.1.call-update) | async-done | bytes 1048592 | tf_op jit(solution)/shard_map/all_gather | solution.py:107
  438.0 2.3 copy.30
  440.3 9.5 %convolution_add_fusion = f32[4,256,2,1536]{3,1,2,0:T(8,128)} fusion(f32[4,256,2,1536]{3,1,2,0:T(8,128)} %fusion.51, bf16[4,256,512,1]{2,1,3,0:T(8,128)(2,1)} %bitcast.92, bf16[512,2,1536,1]{0,2,1,3:T(8,128)(2,1)S(1)} %bitcast.91), kind=kOutput, calls=%fused_computation.24 | convolution fusion | flops 3224371200 | bytes 29360128 | tf_op jit(solution)/shard_map/tsd,doc->tosc/dot_general | solution.py:108
  450.5 90.2 %reduce-scatter.8.cloned.1.call-done = f32[1,256,1536]{2,1,0:T(8,128)} async-done(((f32[8,256,1536]{2,1,0:T(8,128)}), f32[1,256,1536]{2,1,0:T(8,128)}) %reduce-scatter.8.cloned.1.call-update) | async-done | bytes 1572880 | tf_op jit(solution)/shard_map/reduce_scatter | solution.py:116
  540.7 2.7 bitcast_add_fusion
  (56 shorter events, 13.1 us)
Async XLA Ops:
  6.5 15.2 %all-gather.4.cloned.1.call-start = ((), (), s32[]{:S(2)}) async-start(), calls=%async_computation.3 | async-start | bytes 2359296 | tf_op jit(solution)/shard_map/all_gather | solution.py:46
  7.3 181.7 %reduce-scatter.4.cloned.1.call-start = ((), (), s32[]{:S(2)}) async-start(), calls=%async_computation.4 | async-start | bytes 15728640 | tf_op jit(solution)/shard_map/reduce_scatter | solution.py:96
  23.2 13.0 %collective-permute-start = (bf16[256,768]{1,0:T(8,128)(2,1)S(1)}, bf16[256,768]{1,0:T(8,128)(2,1)S(1)}, u32[]{:S(2)}, u32[]{:S(2)}) collective-permute-start(bf16[256,768]{1,0:T(8,128)(2,1)S(1)} %get-tuple-element.25), channel_id=1, source_target_pairs={{0,8},{8,0},{16,24},{24,16},{1,9},{9,1},{17,25},{25,17},{2,10},{10... | collective-permute-start | bytes 1179656 | tf_op jit(solution)/shard_map/ppermute | solution.py:53
  26.2 19.0 %collective-permute-start.1 = (bf16[256,768]{1,0:T(8,128)(2,1)S(1)}, bf16[256,768]{1,0:T(8,128)(2,1)S(1)}, u32[]{:S(2)}, u32[]{:S(2)}) collective-permute-start(bf16[256,768]{1,0:T(8,128)(2,1)S(1)} %get-tuple-element.24), channel_id=1, source_target_pairs={{0,16},{8,24},{16,0},{24,8},{1,17},{9,25},{17,1},{25,9},{2,18},{10... | collective-permute-start | bytes 1179656 | tf_op jit(solution)/shard_map/ppermute | solution.py:53
  27.8 17.5 %collective-permute-start.2 = (bf16[256,768]{1,0:T(8,128)(2,1)S(1)}, bf16[256,768]{1,0:T(8,128)(2,1)S(1)}, u32[]{:S(2)}, u32[]{:S(2)}) collective-permute-start(bf16[256,768]{1,0:T(8,128)(2,1)S(1)} %get-tuple-element.23), channel_id=1, source_target_pairs={{0,24},{8,16},{16,8},{24,0},{1,25},{9,17},{17,9},{25,1},{2,26},{10... | collective-permute-start | bytes 1179656 | tf_op jit(solution)/shard_map/ppermute | solution.py:53
  49.7 17.9 %copy-start.1 = (bf16[4,256,768]{2,1,0:T(8,128)(2,1)}, bf16[4,256,768]{2,1,0:T(8,128)(2,1)S(1)}, u32[]{:S(2)}) copy-start(bf16[4,256,768]{2,1,0:T(8,128)(2,1)S(1)} %broadcast_select_fusion) | copy-start | bytes 4718596
  67.7 1.7 copy-start
  67.7 245.1 %reduce-scatter.6.cloned.1.call-start = ((), (), s32[]{:S(2)}) async-start(), calls=%async_computation.6 | async-start | bytes 15728640 | tf_op jit(solution)/shard_map/reduce_scatter | solution.py:96
  86.4 310.3 %all-gather.6.cloned.1.call-start = ((), (), s32[]{:S(2)}) async-start(), calls=%async_computation.5 | async-start | bytes 1310720 | tf_op jit(solution)/shard_map/all_gather | solution.py:107
  86.5 108.7 %collective-permute-start.6 = (s32[1]{0:T(128)}, s32[1]{0:T(128)}, u32[]{:S(2)}, u32[]{:S(2)}) collective-permute-start(s32[1]{0:T(128)} %param.9), channel_id=1, source_target_pairs={{0,0},{2,8},{4,16},{6,24},{8,2},{10,10},{12,18},{14,26},{16,4},{18... | collective-permute-start | bytes 20 | tf_op jit(solution)/shard_map/ppermute | solution.py:73
  190.7 129.0 %collective-permute-start.3 = (bf16[256,1536]{1,0:T(8,128)(2,1)S(1)}, bf16[256,1536]{1,0:T(8,128)(2,1)}, u32[]{:S(2)}, u32[]{:S(2)}) collective-permute-start(bf16[256,1536]{1,0:T(8,128)(2,1)S(1)} %get-tuple-element.19), channel_id=1, source_target_pairs={{0,2},{2,0},{4,6},{6,4},{1,3},{3,1},{5,7},{7,5},{8,10},{10,8},{12,... | collective-permute-start | bytes 2359304 | tf_op jit(solution)/shard_map/ppermute | solution.py:102
  192.2 127.9 %collective-permute-start.4 = (bf16[256,1536]{1,0:T(8,128)(2,1)S(1)}, bf16[256,1536]{1,0:T(8,128)(2,1)}, u32[]{:S(2)}, u32[]{:S(2)}) collective-permute-start(bf16[256,1536]{1,0:T(8,128)(2,1)S(1)} %get-tuple-element.21), channel_id=1, source_target_pairs={{0,4},{2,6},{4,0},{6,2},{1,5},{3,7},{5,1},{7,3},{8,12},{10,14},{12... | collective-permute-start | bytes 2359304 | tf_op jit(solution)/shard_map/ppermute | solution.py:102
  194.7 125.5 %collective-permute-start.5 = (bf16[256,1536]{1,0:T(8,128)(2,1)S(1)}, bf16[256,1536]{1,0:T(8,128)(2,1)}, u32[]{:S(2)}, u32[]{:S(2)}) collective-permute-start(bf16[256,1536]{1,0:T(8,128)(2,1)S(1)} %get-tuple-element.20), channel_id=1, source_target_pairs={{0,6},{2,4},{4,2},{6,0},{1,7},{3,5},{5,3},{7,1},{8,14},{10,12},{12... | collective-permute-start | bytes 2359304 | tf_op jit(solution)/shard_map/ppermute | solution.py:102
  315.8 47.2 %collective-permute-start.7 = (bf16[256,1536]{1,0:T(8,128)(2,1)}, bf16[256,1536]{1,0:T(8,128)(2,1)}, u32[]{:S(2)}, u32[]{:S(2)}) collective-permute-start(bf16[256,1536]{1,0:T(8,128)(2,1)} %get-tuple-element.16), channel_id=1, source_target_pairs={{0,2},{2,0},{4,6},{6,4},{1,3},{3,1},{5,7},{7,5},{8,10},{10,8},{12,... | collective-permute-start | bytes 2359304 | tf_op jit(solution)/shard_map/ppermute | solution.py:102
  317.2 63.7 %collective-permute-start.8 = (bf16[256,1536]{1,0:T(8,128)(2,1)}, bf16[256,1536]{1,0:T(8,128)(2,1)}, u32[]{:S(2)}, u32[]{:S(2)}) collective-permute-start(bf16[256,1536]{1,0:T(8,128)(2,1)} %get-tuple-element.18), channel_id=1, source_target_pairs={{0,4},{2,6},{4,0},{6,2},{1,5},{3,7},{5,1},{7,3},{8,12},{10,14},{12... | collective-permute-start | bytes 2359304 | tf_op jit(solution)/shard_map/ppermute | solution.py:102
  319.7 61.2 %collective-permute-start.9 = (bf16[256,1536]{1,0:T(8,128)(2,1)S(1)}, bf16[256,1536]{1,0:T(8,128)(2,1)}, u32[]{:S(2)}, u32[]{:S(2)}) collective-permute-start(bf16[256,1536]{1,0:T(8,128)(2,1)S(1)} %get-tuple-element.17), channel_id=1, source_target_pairs={{0,6},{2,4},{4,2},{6,0},{1,7},{3,5},{5,3},{7,1},{8,14},{10,12},{12... | collective-permute-start | bytes 2359304 | tf_op jit(solution)/shard_map/ppermute | solution.py:102
  324.7 113.3 %all-gather.8.cloned.1.call-start = ((), (), s32[]{:S(2)}) async-start(), calls=%async_computation.7 | async-start | bytes 1310720 | tf_op jit(solution)/shard_map/all_gather | solution.py:107
  385.5 155.2 %reduce-scatter.8.cloned.1.call-start = ((), (), s32[]{:S(2)}) async-start(), calls=%async_computation.8 | async-start | bytes 14155776 | tf_op jit(solution)/shard_map/reduce_scatter | solution.py:116
  449.8 0.7 copy-start.2
Sparse Core Ops, SparseCore 0:
  8.9 12.4 all-gather.3
  67.8 121.0 reduce-scatter.3
  192.0 120.7 reduce-scatter.5
  324.8 70.7 all-gather.5
  397.0 40.9 all-gather.7
  450.0 90.7 reduce-scatter.7

commit v11 on v10

--- a/solution.py
+++ b/solution.py
@@ -104,7 +104,14 @@
         else:
             qkv_held = lax.psum_scatter(slab_sum, "ka", scatter_dimension=0, tiled=True)
         context = attention(qkv_held, own_lengths)
-        head_group = lax.all_gather(context, "ka", axis=0, tiled=True)
+        if by_xor and h == n_streams - 1 and n_streams > 1:
+            pieces = [context] + [
+                lax.ppermute(context, "ka", [(i, i ^ s) for i in range(n_ka)]) for s in range(1, n_ka)
+            ]
+            head_group = jnp.take(jnp.stack(pieces), jnp.bitwise_xor(k, jnp.arange(n_ka)), axis=0)
+            head_group = head_group.reshape(n_ka * context.shape[0], -1)
+        else:
+            head_group = lax.all_gather(context, "ka", axis=0, tiled=True)
         term = jnp.einsum(
             "tsd,doc->tosc",
             head_group.reshape(n_tok, tokens // n_tok, -1),

time: 551 us -> 552 us (level)
  starting transfers between devices: 15.9 us -> 34.3 us
  waiting for transfers between devices: 411 us -> 401 us
  matrix products: 58.7 us -> 53 us
    all_gather x2 -> x1, waiting for transfers between devices: 28.8 us -> 6.35 us  [shards(): head_group = lax.all_gather(context, 'ka', axis=0, tiled=True)]
    ppermute x0 -> x3, starting transfers between devices: none -> 18.4 us  [shards(): lax.ppermute(context, 'ka', [(i, i ^ s) for i in range(n_ka)])]
    ppermute x0 -> x3, waiting for transfers between devices: none -> 17.5 us  [shards(): lax.ppermute(context, 'ka', [(i, i ^ s) for i in range(n_ka)])]
    dot_general x2, matrix products: 19.7 us -> 12 us  [shards(): jnp.einsum('tsd,doc->tosc', head_group.reshape(n_tok, tokens // n_tok, -1...]
    ppermute x6, waiting for transfers between devices: 56.1 us -> 49.1 us  [shards(): total = total + lax.ppermute(blocks[s], 'ka', pairs).astype(jnp.float32)]
  transfers between devices with their start and end apart: 16 -> 18, of which waited for: 8 -> 9; matrix products, arithmetic and copies ran while one was open for 13% -> 11% of each run, Pallas kernels for 0% -> 0%
where the time goes in v11:
time: 552 us
  waiting for transfers between devices  401 us (73%)
  matrix products  53 us (10%)
  local copies, waits for them, and re-layouts  40 us (7%)
  starting transfers between devices  34.3 us (6%)
  between operations  13.4 us (2%)
  other arithmetic  9.89 us (2%)
    reduce_scatter x2, waiting for transfers between devices, shards(): slab_sum = lax.psum_scatter(part, 'tok', scatter_dimension=1, tiled=True)  217 us
    reduce_scatter x1, waiting for transfers between devices, shards(): lax.psum_scatter(terms, ('tok', 'out'), scatter_dimension=0, tiled=True)  92.8 us
    ppermute x6, waiting for transfers between devices, shards(): total = total + lax.ppermute(blocks[s], 'ka', pairs).astype(jnp.float32)  49.1 us
    dot_general x2, matrix products, shards(): value = jnp.dot(panel, w_h, preferred_element_type=jnp.float32)  35 us
    ppermute x3, starting transfers between devices, shards(): lax.ppermute(context, 'ka', [(i, i ^ s) for i in range(n_ka)])  18.4 us
    ppermute x3, waiting for transfers between devices, shards(): lax.ppermute(context, 'ka', [(i, i ^ s) for i in range(n_ka)])  17.5 us
    ppermute x3, waiting for transfers between devices, shards(): pieces[s] = lax.ppermute(owed, 'tok', [(i, i ^ s) for i in range(n_tok)])  17.4 us
    slice x1, local copies, waits for them, and re-layouts, shards(): w_qkv[:, c * width + h * piece:c * width + (h + 1) * piece]  13.6 us
  transfers between devices with their start and end apart: 18, of which 9 were waited for; matrix products, arithmetic and copies ran while one was open for 11% of the time, Pallas kernels for 0%

profile of v11, /device:TPU:0, one launch (start us, length us, event | category | flops | bytes accessed | tf_op | source)
XLA Modules:
  0.0 551.9 jit_solution(17019818660527526286)
XLA Ops:
  8.2 13.6 %fusion.50 = (bf16[768,1536]{1,0:T(8,128)(2,1)}, bf16[768,1536]{1,0:T(8,128)(2,1)}, bf16[768,1536]{1,0:T(8,128)(2,1)}, bf16[768,1536]{1,0:T(8,128)(2,1)}, bf16[7...) fusion(bf16[768,12288]{1,0:T(8,128)(2,1)} %param.10), kind=kLoop, calls=%fused_computation.97 | loop fusion | bytes 37748736 | tf_op jit(solution)/shard_map/slice | solution.py:91
  23.2 3.1 collective-permute-start
  26.3 1.5 collective-permute-start.1
  27.9 8.4 %collective-permute-done = bf16[256,768]{1,0:T(8,128)(2,1)S(1)} collective-permute-done((bf16[256,768]{1,0:T(8,128)(2,1)S(1)}, bf16[256,768]{1,0:T(8,128)(2,1)S(1)}, u32[]{:S(2)}, u32[]{:S(2)}) %collective-permute-start) | collective-permute-done | bytes 393248 | tf_op jit(solution)/shard_map/ppermute | solution.py:53
  36.3 9.0 %collective-permute-done.1 = bf16[256,768]{1,0:T(8,128)(2,1)S(1)} collective-permute-done((bf16[256,768]{1,0:T(8,128)(2,1)S(1)}, bf16[256,768]{1,0:T(8,128)(2,1)S(1)}, u32[]{:S(2)}, u32[]{:S(2)}) %collective-permute-start.1) | collective-permute-done | bytes 393248 | tf_op jit(solution)/shard_map/ppermute | solution.py:53
  47.2 17.9 %fusion.3 = bf16[1024,6144]{1,0:T(8,128)(2,1)} fusion(bf16[1024,768]{1,0:T(8,128)(2,1)S(1)} %bitcast.105, f32[6144]{0:T(1024)S(1)} %broadcast_in_dim.74, pred[6144]{0:T(1024)(128)(4,1)S(1)} %fusion.31, pred[1024]{0:T(1024)(128)(4,1)S(1)} %fusion.36, bf16[768,1536]{1,0:T(8,128)(2,1)} %get-tuple-element.8, bf16[768,1536]{1,0:T(8,128)(2,1)} %get-tuple-element.9, ...), kind=kOutput, calls=%fused_computation.8 | convolution fusion | flops 9726590976 | bytes 23624704 | tf_op jit(solution)/shard_map/dot_general | solution.py:93
  66.8 17.1 %fusion.5 = bf16[1024,6144]{1,0:T(8,128)(2,1)} fusion(bf16[1024,768]{1,0:T(8,128)(2,1)} %bitcast.106, f32[6144]{0:T(1024)S(1)} %broadcast_in_dim.80, pred[6144]{0:T(1024)(128)(4,1)S(1)} %fusion.31, pred[1024]{0:T(1024)(128)(4,1)S(1)} %fusion.36, bf16[768,1536]{1,0:T(8,128)(2,1)} %get-tuple-element.12, bf16[768,1536]{1,0:T(8,128)(2,1)} %get-tuple-element.13, ...), kind=kOutput, calls=%fused_computation.10 | convolution fusion | flops 9726590976 | bytes 23624704 | tf_op jit(solution)/shard_map/dot_general | solution.py:93
  84.0 1.9 collective-permute-start.6
  85.9 100.6 %reduce-scatter.4.cloned.1.call-done = bf16[1024,1536]{1,0:T(8,128)(2,1)} async-done(((bf16[1024,6144]{1,0:T(8,128)(2,1)}), bf16[1024,1536]{1,0:T(8,128)(2,1)}) %reduce-scatter.4.cloned.1.call-update) | async-done | bytes 3145744 | tf_op jit(solution)/shard_map/reduce_scatter | solution.py:96
  186.4 1.8 fusion.53
  188.2 1.6 collective-permute-start.3
  189.8 2.4 collective-permute-start.4
  193.4 116.9 %reduce-scatter.6.cloned.1.call-done = bf16[1024,1536]{1,0:T(8,128)(2,1)} async-done(((bf16[1024,6144]{1,0:T(8,128)(2,1)}), bf16[1024,1536]{1,0:T(8,128)(2,1)}) %reduce-scatter.6.cloned.1.call-update) | async-done | bytes 3145744 | tf_op jit(solution)/shard_map/reduce_scatter | solution.py:96
  310.3 3.0 fusion.52
  313.3 1.5 collective-permute-start.7
  314.8 2.4 collective-permute-start.8
  317.7 2.2 add_convert_fusion.1
  321.1 27.8 %collective-permute-done.7 = bf16[256,1536]{1,0:T(8,128)(2,1)} collective-permute-done((bf16[256,1536]{1,0:T(8,128)(2,1)}, bf16[256,1536]{1,0:T(8,128)(2,1)}, u32[]{:S(2)}, u32[]{:S(2)}) %collective-permute-start.7) | collective-permute-done | bytes 786464 | tf_op jit(solution)/shard_map/ppermute | solution.py:102
  348.9 21.3 %collective-permute-done.8 = bf16[256,1536]{1,0:T(8,128)(2,1)} collective-permute-done((bf16[256,1536]{1,0:T(8,128)(2,1)}, bf16[256,1536]{1,0:T(8,128)(2,1)}, u32[]{:S(2)}, u32[]{:S(2)}) %collective-permute-start.8) | collective-permute-done | bytes 786464 | tf_op jit(solution)/shard_map/ppermute | solution.py:102
  370.2 2.2 add_convert_fusion
  376.0 2.1 convolution_convert_fusion
  378.9 16.0 %collective-permute-start.10 = (bf16[256,512]{1,0:T(8,128)(2,1)}, bf16[256,512]{1,0:T(8,128)(2,1)}, u32[]{:S(2)}, u32[]{:S(2)}) collective-permute-start(bf16[256,512]{1,0:T(8,128)(2,1)} %copy.29), channel_id=1, source_target_pairs={{0,2},{2,0},{4,6},{6,4},{1,3},{3,1},{5,7},{7,5},{8,10},{10,8},{12,... | collective-permute-start | bytes 786440 | tf_op jit(solution)/shard_map/ppermute | solution.py:109
  397.3 5.0 fusion.51
  402.2 4.7 copy.46
  406.9 2.8 copy.50
  409.9 17.5 %collective-permute-done.11 = bf16[256,512]{1,0:T(8,128)(2,1)} collective-permute-done((bf16[256,512]{1,0:T(8,128)(2,1)}, bf16[256,512]{1,0:T(8,128)(2,1)}, u32[]{:S(2)}, u32[]{:S(2)}) %collective-permute-start.11) | collective-permute-done | bytes 262176 | tf_op jit(solution)/shard_map/ppermute | solution.py:109
  429.2 6.4 %all-gather.5.cloned.1.call-done = bf16[1024,512]{0,1:T(8,128)(2,1)} async-done(((bf16[256,512]{0,1:T(8,128)(2,1)}), bf16[1024,512]{0,1:T(8,128)(2,1)}) %all-gather.5.cloned.1.call-update) | async-done | bytes 1048592 | tf_op jit(solution)/shard_map/all_gather | solution.py:114
  435.6 1.5 copy.21
  437.1 5.5 fusion.57
  442.6 6.5 %convolution_add_fusion = f32[4,256,2,1536]{3,1,2,0:T(8,128)} fusion(f32[4,256,2,1536]{3,1,2,0:T(8,128)S(1)} %fusion.57, bf16[512,2,1536,1]{0,2,1,3:T(8,128)(2,1)S(1)} %bitcast.97, bf16[4,256,512]{2,1,0:T(8,128)(2,1)S(1)} %gather_fusion, pred[4]{0:T(512)(128)(4,1)S(1)} %get-tuple-element.28), kind=kOutput, calls=%fused_computation.25 | convolution fusion | flops 3224895488 | bytes 29360132 | tf_op jit(solution)/shard_map/tsd,doc->tosc/dot_general | solution.py:115
  449.8 92.8 %reduce-scatter.8.cloned.1.call-done = f32[1,256,1536]{2,1,0:T(8,128)} async-done(((f32[8,256,1536]{2,1,0:T(8,128)}), f32[1,256,1536]{2,1,0:T(8,128)}) %reduce-scatter.8.cloned.1.call-update) | async-done | bytes 1572880 | tf_op jit(solution)/shard_map/reduce_scatter | solution.py:123
  542.6 2.7 bitcast_add_fusion
  (66 shorter events, 19.1 us)
Async XLA Ops:
  6.5 15.2 %all-gather.3.cloned.1.call-start = ((), (), s32[]{:S(2)}) async-start(), calls=%async_computation.3 | async-start | bytes 2359296 | tf_op jit(solution)/shard_map/all_gather | solution.py:46
  7.3 179.2 %reduce-scatter.4.cloned.1.call-start = ((), (), s32[]{:S(2)}) async-start(), calls=%async_computation.4 | async-start | bytes 15728640 | tf_op jit(solution)/shard_map/reduce_scatter | solution.py:96
  23.2 13.0 %collective-permute-start = (bf16[256,768]{1,0:T(8,128)(2,1)S(1)}, bf16[256,768]{1,0:T(8,128)(2,1)S(1)}, u32[]{:S(2)}, u32[]{:S(2)}) collective-permute-start(bf16[256,768]{1,0:T(8,128)(2,1)S(1)} %get-tuple-element.25), channel_id=1, source_target_pairs={{0,8},{8,0},{16,24},{24,16},{1,9},{9,1},{17,25},{25,17},{2,10},{10... | collective-permute-start | bytes 1179656 | tf_op jit(solution)/shard_map/ppermute | solution.py:53
  26.3 19.0 %collective-permute-start.1 = (bf16[256,768]{1,0:T(8,128)(2,1)S(1)}, bf16[256,768]{1,0:T(8,128)(2,1)S(1)}, u32[]{:S(2)}, u32[]{:S(2)}) collective-permute-start(bf16[256,768]{1,0:T(8,128)(2,1)S(1)} %get-tuple-element.24), channel_id=1, source_target_pairs={{0,16},{8,24},{16,0},{24,8},{1,17},{9,25},{17,1},{25,9},{2,18},{10... | collective-permute-start | bytes 1179656 | tf_op jit(solution)/shard_map/ppermute | solution.py:53
  27.8 17.4 %collective-permute-start.2 = (bf16[256,768]{1,0:T(8,128)(2,1)S(1)}, bf16[256,768]{1,0:T(8,128)(2,1)S(1)}, u32[]{:S(2)}, u32[]{:S(2)}) collective-permute-start(bf16[256,768]{1,0:T(8,128)(2,1)S(1)} %get-tuple-element.23), channel_id=1, source_target_pairs={{0,24},{8,16},{16,8},{24,0},{1,25},{9,17},{17,9},{25,1},{2,26},{10... | collective-permute-start | bytes 1179656 | tf_op jit(solution)/shard_map/ppermute | solution.py:53
  47.2 17.9 %copy-start.2 = (bf16[4,256,768]{2,1,0:T(8,128)(2,1)}, bf16[4,256,768]{2,1,0:T(8,128)(2,1)S(1)}, u32[]{:S(2)}) copy-start(bf16[4,256,768]{2,1,0:T(8,128)(2,1)S(1)} %broadcast_select_fusion) | copy-start | bytes 4718596
  65.2 1.7 copy-start.1
  65.2 245.1 %reduce-scatter.6.cloned.1.call-start = ((), (), s32[]{:S(2)}) async-start(), calls=%async_computation.6 | async-start | bytes 15728640 | tf_op jit(solution)/shard_map/reduce_scatter | solution.py:96
  83.9 351.7 %all-gather.5.cloned.1.call-start = ((), (), s32[]{:S(2)}) async-start(), calls=%async_computation.5 | async-start | bytes 1310720 | tf_op jit(solution)/shard_map/all_gather | solution.py:114
  84.0 108.7 %collective-permute-start.6 = (s32[1]{0:T(128)}, s32[1]{0:T(128)}, u32[]{:S(2)}, u32[]{:S(2)}) collective-permute-start(s32[1]{0:T(128)} %param.9), channel_id=1, source_target_pairs={{0,0},{2,8},{4,16},{6,24},{8,2},{10,10},{12,18},{14,26},{16,4},{18... | collective-permute-start | bytes 20 | tf_op jit(solution)/shard_map/ppermute | solution.py:73
  188.2 129.0 %collective-permute-start.3 = (bf16[256,1536]{1,0:T(8,128)(2,1)S(1)}, bf16[256,1536]{1,0:T(8,128)(2,1)}, u32[]{:S(2)}, u32[]{:S(2)}) collective-permute-start(bf16[256,1536]{1,0:T(8,128)(2,1)S(1)} %get-tuple-element.19), channel_id=1, source_target_pairs={{0,2},{2,0},{4,6},{6,4},{1,3},{3,1},{5,7},{7,5},{8,10},{10,8},{12,... | collective-permute-start | bytes 2359304 | tf_op jit(solution)/shard_map/ppermute | solution.py:102
  189.8 127.9 %collective-permute-start.4 = (bf16[256,1536]{1,0:T(8,128)(2,1)S(1)}, bf16[256,1536]{1,0:T(8,128)(2,1)}, u32[]{:S(2)}, u32[]{:S(2)}) collective-permute-start(bf16[256,1536]{1,0:T(8,128)(2,1)S(1)} %get-tuple-element.21), channel_id=1, source_target_pairs={{0,4},{2,6},{4,0},{6,2},{1,5},{3,7},{5,1},{7,3},{8,12},{10,14},{12... | collective-permute-start | bytes 2359304 | tf_op jit(solution)/shard_map/ppermute | solution.py:102
  192.2 125.5 %collective-permute-start.5 = (bf16[256,1536]{1,0:T(8,128)(2,1)S(1)}, bf16[256,1536]{1,0:T(8,128)(2,1)}, u32[]{:S(2)}, u32[]{:S(2)}) collective-permute-start(bf16[256,1536]{1,0:T(8,128)(2,1)S(1)} %get-tuple-element.20), channel_id=1, source_target_pairs={{0,6},{2,4},{4,2},{6,0},{1,7},{3,5},{5,3},{7,1},{8,14},{10,12},{12... | collective-permute-start | bytes 2359304 | tf_op jit(solution)/shard_map/ppermute | solution.py:102
  313.3 35.6 %collective-permute-start.7 = (bf16[256,1536]{1,0:T(8,128)(2,1)}, bf16[256,1536]{1,0:T(8,128)(2,1)}, u32[]{:S(2)}, u32[]{:S(2)}) collective-permute-start(bf16[256,1536]{1,0:T(8,128)(2,1)} %get-tuple-element.16), channel_id=1, source_target_pairs={{0,2},{2,0},{4,6},{6,4},{1,3},{3,1},{5,7},{7,5},{8,10},{10,8},{12,... | collective-permute-start | bytes 2359304 | tf_op jit(solution)/shard_map/ppermute | solution.py:102
  314.8 55.4 %collective-permute-start.8 = (bf16[256,1536]{1,0:T(8,128)(2,1)}, bf16[256,1536]{1,0:T(8,128)(2,1)}, u32[]{:S(2)}, u32[]{:S(2)}) collective-permute-start(bf16[256,1536]{1,0:T(8,128)(2,1)} %get-tuple-element.18), channel_id=1, source_target_pairs={{0,4},{2,6},{4,0},{6,2},{1,5},{3,7},{5,1},{7,3},{8,12},{10,14},{12... | collective-permute-start | bytes 2359304 | tf_op jit(solution)/shard_map/ppermute | solution.py:102
  317.2 53.0 %collective-permute-start.9 = (bf16[256,1536]{1,0:T(8,128)(2,1)S(1)}, bf16[256,1536]{1,0:T(8,128)(2,1)}, u32[]{:S(2)}, u32[]{:S(2)}) collective-permute-start(bf16[256,1536]{1,0:T(8,128)(2,1)S(1)} %get-tuple-element.17), channel_id=1, source_target_pairs={{0,6},{2,4},{4,2},{6,0},{1,7},{3,5},{5,3},{7,1},{8,14},{10,12},{12... | collective-permute-start | bytes 2359304 | tf_op jit(solution)/shard_map/ppermute | solution.py:102
  375.1 167.4 %reduce-scatter.8.cloned.1.call-start = ((), (), s32[]{:S(2)}) async-start(), calls=%async_computation.7 | async-start | bytes 14155776 | tf_op jit(solution)/shard_map/reduce_scatter | solution.py:123
  378.9 31.0 %collective-permute-start.10 = (bf16[256,512]{1,0:T(8,128)(2,1)}, bf16[256,512]{1,0:T(8,128)(2,1)}, u32[]{:S(2)}, u32[]{:S(2)}) collective-permute-start(bf16[256,512]{1,0:T(8,128)(2,1)} %copy.29), channel_id=1, source_target_pairs={{0,2},{2,0},{4,6},{6,4},{1,3},{3,1},{5,7},{7,5},{8,10},{10,8},{12,... | collective-permute-start | bytes 786440 | tf_op jit(solution)/shard_map/ppermute | solution.py:109
  394.9 32.5 %collective-permute-start.11 = (bf16[256,512]{1,0:T(8,128)(2,1)}, bf16[256,512]{1,0:T(8,128)(2,1)}, u32[]{:S(2)}, u32[]{:S(2)}) collective-permute-start(bf16[256,512]{1,0:T(8,128)(2,1)} %copy.29), channel_id=1, source_target_pairs={{0,4},{2,6},{4,0},{6,2},{1,5},{3,7},{5,1},{7,3},{8,12},{10,14},{12... | collective-permute-start | bytes 786440 | tf_op jit(solution)/shard_map/ppermute | solution.py:109
  395.8 31.6 %collective-permute-start.12 = (bf16[256,512]{1,0:T(8,128)(2,1)}, bf16[256,512]{1,0:T(8,128)(2,1)}, u32[]{:S(2)}, u32[]{:S(2)}) collective-permute-start(bf16[256,512]{1,0:T(8,128)(2,1)} %copy.29), channel_id=1, source_target_pairs={{0,6},{2,4},{4,2},{6,0},{1,7},{3,5},{5,3},{7,1},{8,14},{10,12},{12... | collective-permute-start | bytes 786440 | tf_op jit(solution)/shard_map/ppermute | solution.py:109
  437.1 5.5 copy-start
  449.1 0.7 copy-start.3
Sparse Core Ops, SparseCore 0:
  8.9 12.4 all-gather.2
  65.3 121.0 reduce-scatter.3
  189.5 120.7 reduce-scatter.5
  375.3 60.2 all-gather.4
  449.3 93.2 reduce-scatter.7

commit v12 on v10

--- a/solution.py
+++ b/solution.py
@@ -76,7 +76,7 @@
         per = all_lengths.shape[0] // n_ka
         own_lengths = lax.dynamic_slice_in_dim(all_lengths, k * per, per)
     heads_block = width // (3 * HD)
-    n_streams = 2 if heads_block % 2 == 0 else 1
+    n_streams = 4 if heads_block % 4 == 0 else (2 if heads_block % 2 == 0 else 1)
     piece = width // n_streams
     own_rows = prompt_of == t
     bias = b_qkv.astype(jnp.float32)

time: 551 us -> 665 us (1.21)
  blocking collectives: 0 us -> 70.7 us
  matrix products: 58.7 us -> 95.9 us
  waiting for transfers between devices: 411 us -> 375 us
  local copies, waits for them, and re-layouts: 41.3 us -> 60.9 us
  starting transfers between devices: 15.9 us -> 33 us
    all_gather x0 -> x4, blocking collectives: none -> 70.7 us  [shards(): head_group = lax.all_gather(context, 'ka', axis=0, tiled=True)]
    all_gather x2 -> x0, waiting for transfers between devices: 28.8 us -> none  [shards(): head_group = lax.all_gather(context, 'ka', axis=0, tiled=True)]
    dot_general x2 -> x4, matrix products: 19.7 us -> 38.7 us  [shards(): jnp.einsum('tsd,doc->tosc', head_group.reshape(n_tok, tokens // n_tok, -1...]
    ppermute x6 -> x12, starting transfers between devices: 8.84 us -> 26.2 us  [shards(): total = total + lax.ppermute(blocks[s], 'ka', pairs).astype(jnp.float32)]
    ppermute x6 -> x12, waiting for transfers between devices: 56.1 us -> 39.8 us  [shards(): total = total + lax.ppermute(blocks[s], 'ka', pairs).astype(jnp.float32)]
    reduce_scatter x2 -> x4, waiting for transfers between devices: 217 us -> 227 us  [shards(): slab_sum = lax.psum_scatter(part, 'tok', scatter_dimension=1, tiled=True)]
    dot_general x2 -> x4, matrix products: 0.71 us -> 8.17 us  [attention(): jnp.einsum('pshd,pthd->phst', table[:, :, :, 0], table[:, :, :, 1], prefe...]
    convert_element_type x2 -> x4, local copies, waits for them, and re-layouts: 0.54 us -> 7.66 us  [shards(): qkv_held = total.astype(jnp.bfloat16)]
  transfers between devices with their start and end apart: 16 -> 22, of which waited for: 8 -> 9; matrix products, arithmetic and copies ran while one was open for 13% -> 13% of each run, Pallas kernels for 0% -> 0%
where the time goes in v12:
time: 665 us; the launch traced here: 664 us
  waiting for transfers between devices  375 us (56%)
  matrix products  95.9 us (14%)
  blocking collectives  70.7 us (11%)
  local copies, waits for them, and re-layouts  60.9 us (9%)
  starting transfers between devices  33 us (5%)
  other arithmetic  14.5 us (2%)
  between operations  13.8 us (2%)
    reduce_scatter x4, waiting for transfers between devices, shards(): slab_sum = lax.psum_scatter(part, 'tok', scatter_dimension=1, tiled=True)  227 us
    reduce_scatter x1, waiting for transfers between devices, shards(): lax.psum_scatter(terms, ('tok', 'out'), scatter_dimension=0, tiled=True)  90.2 us
    all_gather x4, blocking collectives, shards(): head_group = lax.all_gather(context, 'ka', axis=0, tiled=True)  70.7 us
    ppermute x12, waiting for transfers between devices, shards(): total = total + lax.ppermute(blocks[s], 'ka', pairs).astype(jnp.float32)  39.8 us
    dot_general x4, matrix products, shards(): jnp.einsum('tsd,doc->tosc', head_group.reshape(n_tok, tokens // n_tok, -1...  38.7 us
    dot_general x4, matrix products, shards(): value = jnp.dot(panel, w_h, preferred_element_type=jnp.float32)  37.5 us
    ppermute x12, starting transfers between devices, shards(): total = total + lax.ppermute(blocks[s], 'ka', pairs).astype(jnp.float32)  26.2 us
    ppermute x3, waiting for transfers between devices, shards(): pieces[s] = lax.ppermute(owed, 'tok', [(i, i ^ s) for i in range(n_tok)])  17.4 us
  transfers between devices with their start and end apart: 22, of which 9 were waited for; matrix products, arithmetic and copies ran while one was open for 13% of the time, Pallas kernels for 0%

profile of v12, /device:TPU:0, one launch (start us, length us, event | category | flops | bytes accessed | tf_op | source)
XLA Modules:
  0.0 664.1 jit_solution(6851708325635121261)
XLA Ops:
  8.2 13.6 %fusion.78 = (bf16[768,768]{1,0:T(8,128)(2,1)}, bf16[768,768]{1,0:T(8,128)(2,1)}, bf16[768,768]{1,0:T(8,128)(2,1)}, bf16[768,768]{1,0:T(8,128)(2,1)}, bf16[768,7...) fusion(bf16[768,12288]{1,0:T(8,128)(2,1)} %param.10), kind=kLoop, calls=%fused_computation.137 | loop fusion | bytes 37748736 | tf_op jit(solution)/shard_map/slice | solution.py:91
  23.2 3.0 collective-permute-start
  27.8 8.4 %collective-permute-done = bf16[256,768]{1,0:T(8,128)(2,1)S(1)} collective-permute-done((bf16[256,768]{1,0:T(8,128)(2,1)S(1)}, bf16[256,768]{1,0:T(8,128)(2,1)S(1)}, u32[]{:S(2)}, u32[]{:S(2)}) %collective-permute-start) | collective-permute-done | bytes 393248 | tf_op jit(solution)/shard_map/ppermute | solution.py:53
  36.2 9.1 %collective-permute-done.1 = bf16[256,768]{1,0:T(8,128)(2,1)S(1)} collective-permute-done((bf16[256,768]{1,0:T(8,128)(2,1)S(1)}, bf16[256,768]{1,0:T(8,128)(2,1)S(1)}, u32[]{:S(2)}, u32[]{:S(2)}) %collective-permute-start.1) | collective-permute-done | bytes 393248 | tf_op jit(solution)/shard_map/ppermute | solution.py:53
  51.2 8.1 %fusion.11 = bf16[1024,3072]{1,0:T(8,128)(2,1)} fusion(f32[3072]{0:T(1024)S(1)} %broadcast_in_dim.113, pred[3072]{0:T(1024)(128)(4,1)S(1)} %fusion.53, pred[1024]{0:T(1024)(128)(4,1)S(1)} %fusion.58, bf16[1024,768]{1,0:T(8,128)(2,1)S(1)} %bitcast.177, bf16[768,768]{1,0:T(8,128)(2,1)} %get-tuple-element.20, bf16[768,768]{1,0:T(8,128)(2,1)} %get-tuple-element.21, ...), kind=kOutput, calls=%fused_computation.17 | convolution fusion | flops 4863295488 | bytes 12599296 | tf_op jit(solution)/shard_map/dot_general | solution.py:93
  60.6 9.7 %fusion.7 = bf16[1024,3072]{1,0:T(8,128)(2,1)} fusion(f32[3072]{0:T(1024)S(1)} %broadcast_in_dim.109, pred[3072]{0:T(1024)(128)(4,1)S(1)} %fusion.53, pred[1024]{0:T(1024)(128)(4,1)S(1)} %fusion.58, bf16[1024,768]{1,0:T(8,128)(2,1)S(1)} %bitcast.178, bf16[768,768]{1,0:T(8,128)(2,1)S(1)} %copy-done.5, bf16[768,768]{1,0:T(8,128)(2,1)} %get-tuple-element.13, ...), kind=kOutput, calls=%fused_computation.13 | convolution fusion | flops 4863295488 | bytes 12599296 | tf_op jit(solution)/shard_map/dot_general | solution.py:93
  71.5 9.8 %fusion.5 = bf16[1024,3072]{1,0:T(8,128)(2,1)} fusion(f32[3072]{0:T(1024)S(1)} %broadcast_in_dim.104, pred[3072]{0:T(1024)(128)(4,1)S(1)} %fusion.53, pred[1024]{0:T(1024)(128)(4,1)S(1)} %fusion.58, bf16[1024,768]{1,0:T(8,128)(2,1)S(1)} %bitcast.179, bf16[768,768]{1,0:T(8,128)(2,1)S(1)} %copy-done.4, bf16[768,768]{1,0:T(8,128)(2,1)} %get-tuple-element.17, ...), kind=kOutput, calls=%fused_computation.11 | convolution fusion | flops 4863295488 | bytes 12599296 | tf_op jit(solution)/shard_map/dot_general | solution.py:93
  82.6 9.9 %fusion.9 = bf16[1024,3072]{1,0:T(8,128)(2,1)} fusion(f32[3072]{0:T(1024)S(1)} %broadcast_in_dim.111, pred[3072]{0:T(1024)(128)(4,1)S(1)} %fusion.53, pred[1024]{0:T(1024)(128)(4,1)S(1)} %fusion.58, bf16[1024,768]{1,0:T(8,128)(2,1)S(1)} %bitcast.180, bf16[768,768]{1,0:T(8,128)(2,1)S(1)} %copy-done.3, bf16[768,768]{1,0:T(8,128)(2,1)} %get-tuple-element.9, ...), kind=kOutput, calls=%fused_computation.15 | convolution fusion | flops 4863295488 | bytes 12599296 | tf_op jit(solution)/shard_map/dot_general | solution.py:93
  94.4 5.4 fusion.79
  99.7 2.6 copy.82
  107.1 22.9 %reduce-scatter.12.cloned.1.call-done = bf16[1024,768]{1,0:T(8,128)(2,1)} async-done(((bf16[1024,3072]{1,0:T(8,128)(2,1)}), bf16[1024,768]{1,0:T(8,128)(2,1)}) %reduce-scatter.12.cloned.1.call-update) | async-done | bytes 1572880 | tf_op jit(solution)/shard_map/reduce_scatter | solution.py:96
  133.8 2.4 collective-permute-start.14
  136.7 66.6 %reduce-scatter.8.cloned.1.call-done = bf16[1024,768]{1,0:T(8,128)(2,1)} async-done(((bf16[1024,3072]{1,0:T(8,128)(2,1)}), bf16[1024,768]{1,0:T(8,128)(2,1)}) %reduce-scatter.8.cloned.1.call-update) | async-done | bytes 1572880 | tf_op jit(solution)/shard_map/reduce_scatter | solution.py:96
  203.2 2.3 fusion.81
  207.1 2.4 collective-permute-start.8
  209.5 66.8 %reduce-scatter.6.cloned.1.call-done = bf16[1024,768]{1,0:T(8,128)(2,1)} async-done(((bf16[1024,3072]{1,0:T(8,128)(2,1)}), bf16[1024,768]{1,0:T(8,128)(2,1)}) %reduce-scatter.6.cloned.1.call-update) | async-done | bytes 1572880 | tf_op jit(solution)/shard_map/reduce_scatter | solution.py:96
  278.6 70.8 %reduce-scatter.10.cloned.1.call-done = bf16[1024,768]{1,0:T(8,128)(2,1)} async-done(((bf16[1024,3072]{1,0:T(8,128)(2,1)}), bf16[1024,768]{1,0:T(8,128)(2,1)}) %reduce-scatter.10.cloned.1.call-update) | async-done | bytes 1572880 | tf_op jit(solution)/shard_map/reduce_scatter | solution.py:96
  351.7 3.3 collective-permute-start.9
  363.6 3.3 collective-permute-start.5
  367.0 8.2 %collective-permute-start.11 = (bf16[256,768]{1,0:T(8,128)(2,1)}, bf16[256,768]{1,0:T(8,128)(2,1)}, u32[]{:S(2)}, u32[]{:S(2)}) collective-permute-start(bf16[256,768]{1,0:T(8,128)(2,1)} %get-tuple-element.37), channel_id=1, source_target_pairs={{0,4},{2,6},{4,0},{6,2},{1,5},{3,7},{5,1},{7,3},{8,12},{10,14},{12... | collective-permute-start | bytes 1179656 | tf_op jit(solution)/shard_map/ppermute | solution.py:102
  384.8 14.8 %collective-permute-done.4 = bf16[256,768]{1,0:T(8,128)(2,1)} collective-permute-done((bf16[256,768]{1,0:T(8,128)(2,1)}, bf16[256,768]{1,0:T(8,128)(2,1)}, u32[]{:S(2)}, u32[]{:S(2)}) %collective-permute-start.4) | collective-permute-done | bytes 393248 | tf_op jit(solution)/shard_map/ppermute | solution.py:102
  407.2 25.0 %collective-permute-done.11 = bf16[256,768]{1,0:T(8,128)(2,1)} collective-permute-done((bf16[256,768]{1,0:T(8,128)(2,1)}, bf16[256,768]{1,0:T(8,128)(2,1)}, u32[]{:S(2)}, u32[]{:S(2)}) %collective-permute-start.11) | collective-permute-done | bytes 393248 | tf_op jit(solution)/shard_map/ppermute | solution.py:102
  441.4 23.0 %all_gather.19 = bf16[1024,256]{0,1:T(8,128)(2,1)} all-gather(bf16[256,256]{0,1:T(8,128)(2,1)S(1)} %bitcast.196), channel_id=1, replica_groups=mesh['tok'=4,'ka'=4,'out'=2] {'ka'}, dimensions={0}, use_global_device_ids=true | all-gather | bytes 655360 | tf_op jit(solution)/shard_map/all_gather | solution.py:107
  468.0 15.6 %all_gather.17 = bf16[1024,256]{0,1:T(8,128)(2,1)} all-gather(bf16[256,256]{0,1:T(8,128)(2,1)S(1)} %bitcast.197), channel_id=1, replica_groups=mesh['tok'=4,'ka'=4,'out'=2] {'ka'}, dimensions={0}, use_global_device_ids=true | all-gather | bytes 655360 | tf_op jit(solution)/shard_map/all_gather | solution.py:107
  487.1 16.5 %all_gather.16 = bf16[1024,256]{0,1:T(8,128)(2,1)} all-gather(bf16[256,256]{0,1:T(8,128)(2,1)S(1)} %bitcast.198), channel_id=1, replica_groups=mesh['tok'=4,'ka'=4,'out'=2] {'ka'}, dimensions={0}, use_global_device_ids=true | all-gather | bytes 655360 | tf_op jit(solution)/shard_map/all_gather | solution.py:107
  507.2 15.6 %all_gather.18 = bf16[1024,256]{0,1:T(8,128)(2,1)} all-gather(bf16[256,256]{0,1:T(8,128)(2,1)S(1)} %bitcast.199), channel_id=1, replica_groups=mesh['tok'=4,'ka'=4,'out'=2] {'ka'}, dimensions={0}, use_global_device_ids=true | all-gather | bytes 655360 | tf_op jit(solution)/shard_map/all_gather | solution.py:107
  524.9 8.1 %fusion.90 = f32[4,256,2,1536]{3,1,2,0:T(8,128)} fusion(bf16[4,256,256,1]{2,1,3,0:T(8,128)(2,1)} %bitcast.174, bf16[256,2,1536,1]{0,2,1,3:T(8,128)(2,1)} %bitcast.172), kind=kOutput, calls=%fused_computation.149 | convolution fusion | flops 1610612736 | bytes 14680064 | tf_op jit(solution)/shard_map/tsd,doc->tosc/dot_general | solution.py:108
  533.0 6.3 fusion.89
  539.3 6.4 fusion.91
  545.7 17.9 %add_add_fusion = f32[4,256,2,1536]{3,1,2,0:T(8,128)} fusion(f32[4,256,2,1536]{3,1,2,0:T(8,128)} %fusion.91, f32[4,256,2,1536]{3,1,2,0:T(8,128)} %fusion.89, f32[4,256,2,1536]{3,1,2,0:T(8,128)} %fusion.90, bf16[4,256,256,1]{2,1,3,0:T(8,128)(2,1)} %bitcast.173, bf16[256,2,1536,1]{0,2,1,3:T(8,128)(2,1)S(1)} %bitcast.169), kind=kOutput, calls=%fused_computation.18 | convolution fusion | flops 1620049920 | bytes 52428800 | tf_op jit(solution)/shard_map/tsd,doc->tosc/dot_general | solution.py:108
  564.3 90.2 %reduce-scatter.14.cloned.1.call-done = f32[1,256,1536]{2,1,0:T(8,128)} async-done(((f32[8,256,1536]{2,1,0:T(8,128)}), f32[1,256,1536]{2,1,0:T(8,128)}) %reduce-scatter.14.cloned.1.call-update) | async-done | bytes 1572880 | tf_op jit(solution)/shard_map/reduce_scatter | solution.py:116
  654.5 2.7 bitcast_add_fusion
  (108 shorter events, 79.8 us)
Async XLA Ops:
  6.5 15.2 %all-gather.2.cloned.1.call-start = ((), (), s32[]{:S(2)}) async-start(), calls=%async_computation.5 | async-start | bytes 2359296 | tf_op jit(solution)/shard_map/all_gather | solution.py:46
  7.3 122.7 %reduce-scatter.12.cloned.1.call-start = ((), (), s32[]{:S(2)}) async-start(), calls=%async_computation.9 | async-start | bytes 7864320 | tf_op jit(solution)/shard_map/reduce_scatter | solution.py:96
  23.2 13.0 %collective-permute-start = (bf16[256,768]{1,0:T(8,128)(2,1)S(1)}, bf16[256,768]{1,0:T(8,128)(2,1)S(1)}, u32[]{:S(2)}, u32[]{:S(2)}) collective-permute-start(bf16[256,768]{1,0:T(8,128)(2,1)S(1)} %get-tuple-element.41), channel_id=1, source_target_pairs={{0,8},{8,0},{16,24},{24,16},{1,9},{9,1},{17,25},{25,17},{2,10},{10... | collective-permute-start | bytes 1179656 | tf_op jit(solution)/shard_map/ppermute | solution.py:53
  26.3 19.0 %collective-permute-start.1 = (bf16[256,768]{1,0:T(8,128)(2,1)S(1)}, bf16[256,768]{1,0:T(8,128)(2,1)S(1)}, u32[]{:S(2)}, u32[]{:S(2)}) collective-permute-start(bf16[256,768]{1,0:T(8,128)(2,1)S(1)} %get-tuple-element.40), channel_id=1, source_target_pairs={{0,16},{8,24},{16,0},{24,8},{1,17},{9,25},{17,1},{25,9},{2,18},{10... | collective-permute-start | bytes 1179656 | tf_op jit(solution)/shard_map/ppermute | solution.py:53
  27.8 17.5 %collective-permute-start.2 = (bf16[256,768]{1,0:T(8,128)(2,1)S(1)}, bf16[256,768]{1,0:T(8,128)(2,1)S(1)}, u32[]{:S(2)}, u32[]{:S(2)}) collective-permute-start(bf16[256,768]{1,0:T(8,128)(2,1)S(1)} %get-tuple-element.39), channel_id=1, source_target_pairs={{0,24},{8,16},{16,8},{24,0},{1,25},{9,17},{17,9},{25,1},{2,26},{10... | collective-permute-start | bytes 1179656 | tf_op jit(solution)/shard_map/ppermute | solution.py:53
  49.5 1.3 copy-start.6
  49.6 1.6 copy-start.7
  59.3 1.3 copy-start.5
  59.3 143.9 %reduce-scatter.8.cloned.1.call-start = ((), (), s32[]{:S(2)}) async-start(), calls=%async_computation.7 | async-start | bytes 7864320 | tf_op jit(solution)/shard_map/reduce_scatter | solution.py:96
  70.3 1.3 copy-start.4
  70.3 206.0 %reduce-scatter.6.cloned.1.call-start = ((), (), s32[]{:S(2)}) async-start(), calls=%async_computation.6 | async-start | bytes 7864320 | tf_op jit(solution)/shard_map/reduce_scatter | solution.py:96
  81.3 1.3 copy-start.3
  81.3 268.1 %reduce-scatter.10.cloned.1.call-start = ((), (), s32[]{:S(2)}) async-start(), calls=%async_computation.8 | async-start | bytes 7864320 | tf_op jit(solution)/shard_map/reduce_scatter | solution.py:96
  92.5 562.0 %reduce-scatter.14.cloned.1.call-start = ((), (), s32[]{:S(2)}) async-start(), calls=%async_computation.10 | async-start | bytes 14155776 | tf_op jit(solution)/shard_map/reduce_scatter | solution.py:116
  92.5 13.8 %collective-permute-start.6 = (s32[1]{0:T(128)}, s32[1]{0:T(128)}, u32[]{:S(2)}, u32[]{:S(2)}) collective-permute-start(s32[1]{0:T(128)} %param.9), channel_id=1, source_target_pairs={{0,0},{2,8},{4,16},{6,24},{8,2},{10,10},{12,18},{14,26},{16,4},{18... | collective-permute-start | bytes 20 | tf_op jit(solution)/shard_map/ppermute | solution.py:73
  132.3 219.4 %collective-permute-start.13 = (bf16[256,768]{1,0:T(8,128)(2,1)}, bf16[256,768]{1,0:T(8,128)(2,1)}, u32[]{:S(2)}, u32[]{:S(2)}) collective-permute-start(bf16[256,768]{1,0:T(8,128)(2,1)} %get-tuple-element.26), channel_id=1, source_target_pairs={{0,2},{2,0},{4,6},{6,4},{1,3},{3,1},{5,7},{7,5},{8,10},{10,8},{12,... | collective-permute-start | bytes 1179656 | tf_op jit(solution)/shard_map/ppermute | solution.py:102
  133.8 221.2 %collective-permute-start.14 = (bf16[256,768]{1,0:T(8,128)(2,1)}, bf16[256,768]{1,0:T(8,128)(2,1)}, u32[]{:S(2)}, u32[]{:S(2)}) collective-permute-start(bf16[256,768]{1,0:T(8,128)(2,1)} %get-tuple-element.28), channel_id=1, source_target_pairs={{0,4},{2,6},{4,0},{6,2},{1,5},{3,7},{5,1},{7,3},{8,12},{10,14},{12... | collective-permute-start | bytes 1179656 | tf_op jit(solution)/shard_map/ppermute | solution.py:102
  136.2 218.8 %collective-permute-start.15 = (bf16[256,768]{1,0:T(8,128)(2,1)}, bf16[256,768]{1,0:T(8,128)(2,1)}, u32[]{:S(2)}, u32[]{:S(2)}) collective-permute-start(bf16[256,768]{1,0:T(8,128)(2,1)} %get-tuple-element.27), channel_id=1, source_target_pairs={{0,6},{2,4},{4,2},{6,0},{1,7},{3,5},{5,3},{7,1},{8,14},{10,12},{12... | collective-permute-start | bytes 1179656 | tf_op jit(solution)/shard_map/ppermute | solution.py:102
  205.6 158.1 %collective-permute-start.7 = (bf16[256,768]{1,0:T(8,128)(2,1)}, bf16[256,768]{1,0:T(8,128)(2,1)}, u32[]{:S(2)}, u32[]{:S(2)}) collective-permute-start(bf16[256,768]{1,0:T(8,128)(2,1)} %get-tuple-element.29), channel_id=1, source_target_pairs={{0,2},{2,0},{4,6},{6,4},{1,3},{3,1},{5,7},{7,5},{8,10},{10,8},{12,... | collective-permute-start | bytes 1179656 | tf_op jit(solution)/shard_map/ppermute | solution.py:102
  207.1 159.9 %collective-permute-start.8 = (bf16[256,768]{1,0:T(8,128)(2,1)}, bf16[256,768]{1,0:T(8,128)(2,1)}, u32[]{:S(2)}, u32[]{:S(2)}) collective-permute-start(bf16[256,768]{1,0:T(8,128)(2,1)} %get-tuple-element.31), channel_id=1, source_target_pairs={{0,4},{2,6},{4,0},{6,2},{1,5},{3,7},{5,1},{7,3},{8,12},{10,14},{12... | collective-permute-start | bytes 1179656 | tf_op jit(solution)/shard_map/ppermute | solution.py:102
  351.7 15.3 %collective-permute-start.9 = (bf16[256,768]{1,0:T(8,128)(2,1)}, bf16[256,768]{1,0:T(8,128)(2,1)}, u32[]{:S(2)}, u32[]{:S(2)}) collective-permute-start(bf16[256,768]{1,0:T(8,128)(2,1)} %get-tuple-element.30), channel_id=1, source_target_pairs={{0,6},{2,4},{4,2},{6,0},{1,7},{3,5},{5,3},{7,1},{8,14},{10,12},{12... | collective-permute-start | bytes 1179656 | tf_op jit(solution)/shard_map/ppermute | solution.py:102
  355.0 27.8 %collective-permute-start.3 = (bf16[256,768]{1,0:T(8,128)(2,1)}, bf16[256,768]{1,0:T(8,128)(2,1)}, u32[]{:S(2)}, u32[]{:S(2)}) collective-permute-start(bf16[256,768]{1,0:T(8,128)(2,1)} %get-tuple-element.32), channel_id=1, source_target_pairs={{0,2},{2,0},{4,6},{6,4},{1,3},{3,1},{5,7},{7,5},{8,10},{10,8},{12,... | collective-permute-start | bytes 1179656 | tf_op jit(solution)/shard_map/ppermute | solution.py:102
  355.0 44.6 %collective-permute-start.4 = (bf16[256,768]{1,0:T(8,128)(2,1)}, bf16[256,768]{1,0:T(8,128)(2,1)}, u32[]{:S(2)}, u32[]{:S(2)}) collective-permute-start(bf16[256,768]{1,0:T(8,128)(2,1)} %get-tuple-element.34), channel_id=1, source_target_pairs={{0,4},{2,6},{4,0},{6,2},{1,5},{3,7},{5,1},{7,3},{8,12},{10,14},{12... | collective-permute-start | bytes 1179656 | tf_op jit(solution)/shard_map/ppermute | solution.py:102
  363.6 35.9 %collective-permute-start.5 = (bf16[256,768]{1,0:T(8,128)(2,1)}, bf16[256,768]{1,0:T(8,128)(2,1)}, u32[]{:S(2)}, u32[]{:S(2)}) collective-permute-start(bf16[256,768]{1,0:T(8,128)(2,1)} %get-tuple-element.33), channel_id=1, source_target_pairs={{0,6},{2,4},{4,2},{6,0},{1,7},{3,5},{5,3},{7,1},{8,14},{10,12},{12... | collective-permute-start | bytes 1179656 | tf_op jit(solution)/shard_map/ppermute | solution.py:102
  367.0 40.2 %collective-permute-start.10 = (bf16[256,768]{1,0:T(8,128)(2,1)}, bf16[256,768]{1,0:T(8,128)(2,1)}, u32[]{:S(2)}, u32[]{:S(2)}) collective-permute-start(bf16[256,768]{1,0:T(8,128)(2,1)} %get-tuple-element.35), channel_id=1, source_target_pairs={{0,2},{2,0},{4,6},{6,4},{1,3},{3,1},{5,7},{7,5},{8,10},{10,8},{12,... | collective-permute-start | bytes 1179656 | tf_op jit(solution)/shard_map/ppermute | solution.py:102
  367.0 65.2 %collective-permute-start.11 = (bf16[256,768]{1,0:T(8,128)(2,1)}, bf16[256,768]{1,0:T(8,128)(2,1)}, u32[]{:S(2)}, u32[]{:S(2)}) collective-permute-start(bf16[256,768]{1,0:T(8,128)(2,1)} %get-tuple-element.37), channel_id=1, source_target_pairs={{0,4},{2,6},{4,0},{6,2},{1,5},{3,7},{5,1},{7,3},{8,12},{10,14},{12... | collective-permute-start | bytes 1179656 | tf_op jit(solution)/shard_map/ppermute | solution.py:102
  382.8 49.4 %collective-permute-start.12 = (bf16[256,768]{1,0:T(8,128)(2,1)}, bf16[256,768]{1,0:T(8,128)(2,1)}, u32[]{:S(2)}, u32[]{:S(2)}) collective-permute-start(bf16[256,768]{1,0:T(8,128)(2,1)} %get-tuple-element.36), channel_id=1, source_target_pairs={{0,6},{2,4},{4,2},{6,0},{1,7},{3,5},{5,3},{7,1},{8,14},{10,12},{12... | collective-permute-start | bytes 1179656 | tf_op jit(solution)/shard_map/ppermute | solution.py:102
  524.9 8.1 %copy-start = (bf16[256,3072]{0,1:T(8,128)(2,1)S(1)}, bf16[256,3072]{0,1:T(8,128)(2,1)}, u32[]{:S(2)}) copy-start(bf16[256,3072]{0,1:T(8,128)(2,1)} %copy.78) | copy-start | bytes 4718596
  524.9 8.1 %copy-start.1 = (bf16[1024,256]{1,0:T(8,128)(2,1)S(1)}, bf16[1024,256]{1,0:T(8,128)(2,1)}, u32[]{:S(2)}) copy-start(bf16[1024,256]{1,0:T(8,128)(2,1)} %copy.32) | copy-start | bytes 1572868
  533.0 6.3 copy-start.2
  563.6 0.7 copy-start.8
Sparse Core Ops, SparseCore 0:
  8.9 12.4 all-gather.1
  59.4 70.5 reduce-scatter.11
  133.0 70.2 reduce-scatter.7
  206.1 70.1 reduce-scatter.5
  279.1 70.2 reduce-scatter.9
  563.7 90.7 reduce-scatter.13

commit v13 on v10

--- a/solution.py
+++ b/solution.py
@@ -105,13 +105,11 @@
             qkv_held = lax.psum_scatter(slab_sum, "ka", scatter_dimension=0, tiled=True)
         context = attention(qkv_held, own_lengths)
         head_group = lax.all_gather(context, "ka", axis=0, tiled=True)
-        term = jnp.einsum(
-            "tsd,doc->tosc",
-            head_group.reshape(n_tok, tokens // n_tok, -1),
-            w_out[h * w_rows:(h + 1) * w_rows].reshape(w_rows, n_out, -1),
-            preferred_element_type=jnp.float32,
+        term = jnp.dot(
+            head_group, w_out[h * w_rows:(h + 1) * w_rows], preferred_element_type=jnp.float32
         )
         terms = term if terms is None else terms + term
+    terms = terms.reshape(n_tok, tokens // n_tok, n_out, -1).transpose(0, 2, 1, 3)
     terms = terms.reshape(n_tok * n_out, tokens // n_tok, -1)
     summed = lax.psum_scatter(terms, ("tok", "out"), scatter_dimension=0, tiled=True)
     return summed[0] + b_out.astype(jnp.float32)

time: 551 us -> 581 us (1.054)
  waiting for transfers between devices: 411 us -> 424 us
  local copies, waits for them, and re-layouts: 41.3 us -> 54 us
    reshape x0 -> x1, local copies, waits for them, and re-layouts: none -> 16.8 us  [shards(): terms.reshape(n_tok, tokens // n_tok, n_out, -1).transpose(0, 2, 1, 3)]
    all_gather x2, waiting for transfers between devices: 28.8 us -> 42.1 us  [shards(): head_group = lax.all_gather(context, 'ka', axis=0, tiled=True)]
    transpose x0 -> x1, local copies, waits for them, and re-layouts: none -> 11.4 us  [shards(): terms.reshape(n_tok, tokens // n_tok, n_out, -1).transpose(0, 2, 1, 3)]
    unnamed x8 -> x6, local copies, waits for them, and re-layouts: 8.07 us -> 2.04 us
  transfers between devices with their start and end apart: 16 -> 16, of which waited for: 8 -> 9; matrix products, arithmetic and copies ran while one was open for 13% -> 10% of each run, Pallas kernels for 0% -> 0%
where the time goes in v13:
time: 581 us
  waiting for transfers between devices  424 us (73%)
  matrix products  63 us (11%)
  local copies, waits for them, and re-layouts  54 us (9%)
  starting transfers between devices  16 us (3%)
  between operations  13.7 us (2%)
  other arithmetic  9.86 us (2%)
    reduce_scatter x2, waiting for transfers between devices, shards(): slab_sum = lax.psum_scatter(part, 'tok', scatter_dimension=1, tiled=True)  217 us
    reduce_scatter x1, waiting for transfers between devices, shards(): lax.psum_scatter(terms, ('tok', 'out'), scatter_dimension=0, tiled=True)  90.2 us
    ppermute x6, waiting for transfers between devices, shards(): total = total + lax.ppermute(blocks[s], 'ka', pairs).astype(jnp.float32)  56.2 us
    all_gather x2, waiting for transfers between devices, shards(): head_group = lax.all_gather(context, 'ka', axis=0, tiled=True)  42.1 us
    dot_general x2, matrix products, shards(): value = jnp.dot(panel, w_h, preferred_element_type=jnp.float32)  35 us
    dot_general x2, matrix products, shards(): jnp.dot(head_group, w_out[h * w_rows:(h + 1) * w_rows], preferred_element...  24 us
    ppermute x3, waiting for transfers between devices, shards(): pieces[s] = lax.ppermute(owed, 'tok', [(i, i ^ s) for i in range(n_tok)])  17.4 us
    reshape x1, local copies, waits for them, and re-layouts, shards(): terms.reshape(n_tok, tokens // n_tok, n_out, -1).transpose(0, 2, 1, 3)  16.8 us
  transfers between devices with their start and end apart: 16, of which 9 were waited for; matrix products, arithmetic and copies ran while one was open for 10% of the time, Pallas kernels for 0%

profile of v13, /device:TPU:0, one launch (start us, length us, event | category | flops | bytes accessed | tf_op | source)
XLA Modules:
  0.0 580.6 jit_solution(13453984018584860924)
XLA Ops:
  8.2 13.5 %fusion.47 = (bf16[768,1536]{1,0:T(8,128)(2,1)}, bf16[768,1536]{1,0:T(8,128)(2,1)}, bf16[768,1536]{1,0:T(8,128)(2,1)}, bf16[768,1536]{1,0:T(8,128)(2,1)}, bf16[7...) fusion(bf16[768,12288]{1,0:T(8,128)(2,1)} %param.10), kind=kLoop, calls=%fused_computation.90 | loop fusion | bytes 37748736 | tf_op jit(solution)/shard_map/slice | solution.py:91
  21.7 1.5 dynamic-slice_bitcast_fusion
  23.2 3.1 collective-permute-start
  26.3 1.5 collective-permute-start.1
  27.8 8.4 %collective-permute-done = bf16[256,768]{1,0:T(8,128)(2,1)S(1)} collective-permute-done((bf16[256,768]{1,0:T(8,128)(2,1)S(1)}, bf16[256,768]{1,0:T(8,128)(2,1)S(1)}, u32[]{:S(2)}, u32[]{:S(2)}) %collective-permute-start) | collective-permute-done | bytes 393248 | tf_op jit(solution)/shard_map/ppermute | solution.py:53
  36.2 9.0 %collective-permute-done.1 = bf16[256,768]{1,0:T(8,128)(2,1)S(1)} collective-permute-done((bf16[256,768]{1,0:T(8,128)(2,1)S(1)}, bf16[256,768]{1,0:T(8,128)(2,1)S(1)}, u32[]{:S(2)}, u32[]{:S(2)}) %collective-permute-start.1) | collective-permute-done | bytes 393248 | tf_op jit(solution)/shard_map/ppermute | solution.py:53
  46.1 1.4 broadcast_select_fusion.1
  47.4 2.1 gather_fusion.1
  49.7 18.0 %fusion.3 = bf16[1024,6144]{1,0:T(8,128)(2,1)} fusion(bf16[1024,768]{1,0:T(8,128)(2,1)S(1)} %bitcast.79, f32[6144]{0:T(1024)S(1)} %broadcast_in_dim.64, pred[6144]{0:T(1024)(128)(4,1)S(1)} %fusion.30, pred[1024]{0:T(1024)(128)(4,1)S(1)} %fusion.35, bf16[768,1536]{1,0:T(8,128)(2,1)} %get-tuple-element.8, bf16[768,1536]{1,0:T(8,128)(2,1)} %get-tuple-element.9, ...), kind=kOutput, calls=%fused_computation.7 | convolution fusion | flops 9726590976 | bytes 23624704 | tf_op jit(solution)/shard_map/dot_general | solution.py:93
  68.0 1.4 copy-done
  69.4 17.0 %fusion.5 = bf16[1024,6144]{1,0:T(8,128)(2,1)} fusion(bf16[1024,768]{1,0:T(8,128)(2,1)} %bitcast.80, f32[6144]{0:T(1024)S(1)} %broadcast_in_dim.69, pred[6144]{0:T(1024)(128)(4,1)S(1)} %fusion.30, pred[1024]{0:T(1024)(128)(4,1)S(1)} %fusion.35, bf16[768,1536]{1,0:T(8,128)(2,1)} %get-tuple-element.12, bf16[768,1536]{1,0:T(8,128)(2,1)} %get-tuple-element.13, ...), kind=kOutput, calls=%fused_computation.9 | convolution fusion | flops 9726590976 | bytes 23624704 | tf_op jit(solution)/shard_map/dot_general | solution.py:93
  86.5 1.9 collective-permute-start.6
  88.4 100.7 %reduce-scatter.4.cloned.1.call-done = bf16[1024,1536]{1,0:T(8,128)(2,1)} async-done(((bf16[1024,6144]{1,0:T(8,128)(2,1)}), bf16[1024,1536]{1,0:T(8,128)(2,1)}) %reduce-scatter.4.cloned.1.call-update) | async-done | bytes 3145744 | tf_op jit(solution)/shard_map/reduce_scatter | solution.py:96
  189.0 1.8 fusion.49
  190.8 1.5 collective-permute-start.3
  192.3 2.4 collective-permute-start.4
  196.1 116.8 %reduce-scatter.6.cloned.1.call-done = bf16[1024,1536]{1,0:T(8,128)(2,1)} async-done(((bf16[1024,6144]{1,0:T(8,128)(2,1)}), bf16[1024,1536]{1,0:T(8,128)(2,1)}) %reduce-scatter.6.cloned.1.call-update) | async-done | bytes 3145744 | tf_op jit(solution)/shard_map/reduce_scatter | solution.py:96
  312.9 3.0 fusion.48
  315.9 1.5 collective-permute-start.7
  317.3 2.4 collective-permute-start.8
  320.3 2.2 add_convert_fusion.1
  324.9 38.1 %collective-permute-done.7 = bf16[256,1536]{1,0:T(8,128)(2,1)} collective-permute-done((bf16[256,1536]{1,0:T(8,128)(2,1)}, bf16[256,1536]{1,0:T(8,128)(2,1)}, u32[]{:S(2)}, u32[]{:S(2)}) %collective-permute-start.7) | collective-permute-done | bytes 786464 | tf_op jit(solution)/shard_map/ppermute | solution.py:102
  363.0 18.0 %collective-permute-done.8 = bf16[256,1536]{1,0:T(8,128)(2,1)} collective-permute-done((bf16[256,1536]{1,0:T(8,128)(2,1)}, bf16[256,1536]{1,0:T(8,128)(2,1)}, u32[]{:S(2)}, u32[]{:S(2)}) %collective-permute-start.8) | collective-permute-done | bytes 786464 | tf_op jit(solution)/shard_map/ppermute | solution.py:102
  381.0 2.3 add_convert_fusion
  385.9 9.8 %all-gather.6.cloned.1.call-done = bf16[1024,512]{0,1:T(8,128)(2,1)} async-done(((bf16[256,512]{0,1:T(8,128)(2,1)}), bf16[1024,512]{0,1:T(8,128)(2,1)}) %all-gather.6.cloned.1.call-update) | async-done | bytes 1048592 | tf_op jit(solution)/shard_map/all_gather | solution.py:107
  395.7 10.2 %fusion.21 = f32[1024,3072]{1,0:T(8,128)} fusion(bf16[1024,512]{0,1:T(8,128)(2,1)} %all-gather.6.cloned.1.call-done, bf16[1024,3072]{1,0:T(8,128)(2,1)} %param.12), kind=kOutput, calls=%fused_computation.26 | convolution fusion | flops 3221225472 | bytes 16777216 | tf_op jit(solution)/shard_map/dot_general | solution.py:108
  405.9 32.2 %all-gather.8.cloned.1.call-done = bf16[1024,512]{0,1:T(8,128)(2,1)} async-done(((bf16[256,512]{0,1:T(8,128)(2,1)}), bf16[1024,512]{0,1:T(8,128)(2,1)}) %all-gather.8.cloned.1.call-update) | async-done | bytes 1048592 | tf_op jit(solution)/shard_map/all_gather | solution.py:107
  438.1 13.8 %convolution_add_fusion = f32[1024,3072]{1,0:T(8,128)} fusion(f32[1024,3072]{1,0:T(8,128)} %fusion.21, bf16[1024,512]{0,1:T(8,128)(2,1)} %all-gather.8.cloned.1.call-done, bf16[1024,3072]{1,0:T(8,128)(2,1)} %param.12), kind=kOutput, calls=%fused_computation.24 | convolution fusion | flops 3224371200 | bytes 29360128 | tf_op jit(solution)/shard_map/dot_general | solution.py:108
  451.9 16.8 %reshape.233 = f32[4,256,2,1536]{3,2,1,0:T(2,128)} reshape(f32[1024,3072]{1,0:T(8,128)} %convolution_add_fusion) | data formatting | bytes 25165824 | tf_op jit(solution)/shard_map/reshape | solution.py:112
  468.8 11.4 %copy.26 = f32[4,2,256,1536]{3,2,1,0:T(8,128)} copy(f32[4,2,256,1536]{3,1,2,0:T(2,128)} %bitcast.72) | data formatting | bytes 25165824 | tf_op jit(solution)/shard_map/transpose | solution.py:112
  480.8 90.2 %reduce-scatter.8.cloned.1.call-done = f32[1,256,1536]{2,1,0:T(8,128)} async-done(((f32[8,256,1536]{2,1,0:T(8,128)}), f32[1,256,1536]{2,1,0:T(8,128)}) %reduce-scatter.8.cloned.1.call-update) | async-done | bytes 1572880 | tf_op jit(solution)/shard_map/reduce_scatter | solution.py:114
  571.0 2.7 bitcast_add_fusion
  (53 shorter events, 10.5 us)
Async XLA Ops:
  6.5 15.2 %all-gather.4.cloned.1.call-start = ((), (), s32[]{:S(2)}) async-start(), calls=%async_computation.3 | async-start | bytes 2359296 | tf_op jit(solution)/shard_map/all_gather | solution.py:46
  7.3 181.8 %reduce-scatter.4.cloned.1.call-start = ((), (), s32[]{:S(2)}) async-start(), calls=%async_computation.4 | async-start | bytes 15728640 | tf_op jit(solution)/shard_map/reduce_scatter | solution.py:96
  23.2 13.0 %collective-permute-start = (bf16[256,768]{1,0:T(8,128)(2,1)S(1)}, bf16[256,768]{1,0:T(8,128)(2,1)S(1)}, u32[]{:S(2)}, u32[]{:S(2)}) collective-permute-start(bf16[256,768]{1,0:T(8,128)(2,1)S(1)} %get-tuple-element.23), channel_id=1, source_target_pairs={{0,8},{8,0},{16,24},{24,16},{1,9},{9,1},{17,25},{25,17},{2,10},{10... | collective-permute-start | bytes 1179656 | tf_op jit(solution)/shard_map/ppermute | solution.py:53
  26.3 19.0 %collective-permute-start.1 = (bf16[256,768]{1,0:T(8,128)(2,1)S(1)}, bf16[256,768]{1,0:T(8,128)(2,1)S(1)}, u32[]{:S(2)}, u32[]{:S(2)}) collective-permute-start(bf16[256,768]{1,0:T(8,128)(2,1)S(1)} %get-tuple-element.22), channel_id=1, source_target_pairs={{0,16},{8,24},{16,0},{24,8},{1,17},{9,25},{17,1},{25,9},{2,18},{10... | collective-permute-start | bytes 1179656 | tf_op jit(solution)/shard_map/ppermute | solution.py:53
  27.8 17.4 %collective-permute-start.2 = (bf16[256,768]{1,0:T(8,128)(2,1)S(1)}, bf16[256,768]{1,0:T(8,128)(2,1)S(1)}, u32[]{:S(2)}, u32[]{:S(2)}) collective-permute-start(bf16[256,768]{1,0:T(8,128)(2,1)S(1)} %get-tuple-element.21), channel_id=1, source_target_pairs={{0,24},{8,16},{16,8},{24,0},{1,25},{9,17},{17,9},{25,1},{2,26},{10... | collective-permute-start | bytes 1179656 | tf_op jit(solution)/shard_map/ppermute | solution.py:53
  49.7 18.0 %copy-start.1 = (bf16[4,256,768]{2,1,0:T(8,128)(2,1)}, bf16[4,256,768]{2,1,0:T(8,128)(2,1)S(1)}, u32[]{:S(2)}) copy-start(bf16[4,256,768]{2,1,0:T(8,128)(2,1)S(1)} %broadcast_select_fusion) | copy-start | bytes 4718596
  67.7 1.7 copy-start
  67.8 245.1 %reduce-scatter.6.cloned.1.call-start = ((), (), s32[]{:S(2)}) async-start(), calls=%async_computation.6 | async-start | bytes 15728640 | tf_op jit(solution)/shard_map/reduce_scatter | solution.py:96
  86.4 309.3 %all-gather.6.cloned.1.call-start = ((), (), s32[]{:S(2)}) async-start(), calls=%async_computation.5 | async-start | bytes 1310720 | tf_op jit(solution)/shard_map/all_gather | solution.py:107
  86.5 108.8 %collective-permute-start.6 = (s32[1]{0:T(128)}, s32[1]{0:T(128)}, u32[]{:S(2)}, u32[]{:S(2)}) collective-permute-start(s32[1]{0:T(128)} %param.9), channel_id=1, source_target_pairs={{0,0},{2,8},{4,16},{6,24},{8,2},{10,10},{12,18},{14,26},{16,4},{18... | collective-permute-start | bytes 20 | tf_op jit(solution)/shard_map/ppermute | solution.py:73
  190.8 128.9 %collective-permute-start.3 = (bf16[256,1536]{1,0:T(8,128)(2,1)S(1)}, bf16[256,1536]{1,0:T(8,128)(2,1)}, u32[]{:S(2)}, u32[]{:S(2)}) collective-permute-start(bf16[256,1536]{1,0:T(8,128)(2,1)S(1)} %get-tuple-element.17), channel_id=1, source_target_pairs={{0,2},{2,0},{4,6},{6,4},{1,3},{3,1},{5,7},{7,5},{8,10},{10,8},{12,... | collective-permute-start | bytes 2359304 | tf_op jit(solution)/shard_map/ppermute | solution.py:102
  192.3 127.9 %collective-permute-start.4 = (bf16[256,1536]{1,0:T(8,128)(2,1)S(1)}, bf16[256,1536]{1,0:T(8,128)(2,1)}, u32[]{:S(2)}, u32[]{:S(2)}) collective-permute-start(bf16[256,1536]{1,0:T(8,128)(2,1)S(1)} %get-tuple-element.19), channel_id=1, source_target_pairs={{0,4},{2,6},{4,0},{6,2},{1,5},{3,7},{5,1},{7,3},{8,12},{10,14},{12... | collective-permute-start | bytes 2359304 | tf_op jit(solution)/shard_map/ppermute | solution.py:102
  194.7 125.5 %collective-permute-start.5 = (bf16[256,1536]{1,0:T(8,128)(2,1)S(1)}, bf16[256,1536]{1,0:T(8,128)(2,1)}, u32[]{:S(2)}, u32[]{:S(2)}) collective-permute-start(bf16[256,1536]{1,0:T(8,128)(2,1)S(1)} %get-tuple-element.18), channel_id=1, source_target_pairs={{0,6},{2,4},{4,2},{6,0},{1,7},{3,5},{5,3},{7,1},{8,14},{10,12},{12... | collective-permute-start | bytes 2359304 | tf_op jit(solution)/shard_map/ppermute | solution.py:102
  315.9 47.2 %collective-permute-start.7 = (bf16[256,1536]{1,0:T(8,128)(2,1)}, bf16[256,1536]{1,0:T(8,128)(2,1)}, u32[]{:S(2)}, u32[]{:S(2)}) collective-permute-start(bf16[256,1536]{1,0:T(8,128)(2,1)} %get-tuple-element.14), channel_id=1, source_target_pairs={{0,2},{2,0},{4,6},{6,4},{1,3},{3,1},{5,7},{7,5},{8,10},{10,8},{12,... | collective-permute-start | bytes 2359304 | tf_op jit(solution)/shard_map/ppermute | solution.py:102
  317.3 63.7 %collective-permute-start.8 = (bf16[256,1536]{1,0:T(8,128)(2,1)}, bf16[256,1536]{1,0:T(8,128)(2,1)}, u32[]{:S(2)}, u32[]{:S(2)}) collective-permute-start(bf16[256,1536]{1,0:T(8,128)(2,1)} %get-tuple-element.16), channel_id=1, source_target_pairs={{0,4},{2,6},{4,0},{6,2},{1,5},{3,7},{5,1},{7,3},{8,12},{10,14},{12... | collective-permute-start | bytes 2359304 | tf_op jit(solution)/shard_map/ppermute | solution.py:102
  319.7 61.3 %collective-permute-start.9 = (bf16[256,1536]{1,0:T(8,128)(2,1)S(1)}, bf16[256,1536]{1,0:T(8,128)(2,1)}, u32[]{:S(2)}, u32[]{:S(2)}) collective-permute-start(bf16[256,1536]{1,0:T(8,128)(2,1)S(1)} %get-tuple-element.15), channel_id=1, source_target_pairs={{0,6},{2,4},{4,2},{6,0},{1,7},{3,5},{5,3},{7,1},{8,14},{10,12},{12... | collective-permute-start | bytes 2359304 | tf_op jit(solution)/shard_map/ppermute | solution.py:102
  324.8 113.3 %all-gather.8.cloned.1.call-start = ((), (), s32[]{:S(2)}) async-start(), calls=%async_computation.7 | async-start | bytes 1310720 | tf_op jit(solution)/shard_map/all_gather | solution.py:107
  385.6 185.4 %reduce-scatter.8.cloned.1.call-start = ((), (), s32[]{:S(2)}) async-start(), calls=%async_computation.8 | async-start | bytes 14155776 | tf_op jit(solution)/shard_map/reduce_scatter | solution.py:114
  480.1 0.7 copy-start.2
Sparse Core Ops, SparseCore 0:
  8.9 12.4 all-gather.3
  67.9 121.1 reduce-scatter.3
  192.1 120.7 reduce-scatter.5
  325.0 70.7 all-gather.5
  397.1 40.9 all-gather.7
  480.3 90.6 reduce-scatter.7

commit v14 on v10

--- a/solution.py
+++ b/solution.py
@@ -96,10 +96,12 @@
         slab_sum = lax.psum_scatter(part, "tok", scatter_dimension=1, tiled=True)
         if by_xor:
             blocks = slab_sum.reshape(n_blocks, rows_dev, piece)
+            got = {}
+            for s in range(n_ka - 1, 0, -1):
+                got[s] = lax.ppermute(blocks[s], "ka", [(i, i ^ s) for i in range(n_ka)])
             total = blocks[0].astype(jnp.float32)
             for s in range(1, n_ka):
-                pairs = [(i, i ^ s) for i in range(n_ka)]
-                total = total + lax.ppermute(blocks[s], "ka", pairs).astype(jnp.float32)
+                total = total + got[s].astype(jnp.float32)
             qkv_held = total.astype(jnp.bfloat16)
         else:
             qkv_held = lax.psum_scatter(slab_sum, "ka", scatter_dimension=0, tiled=True)

time: 551 us -> 551 us (level)
  no operation moved by 1% of the time
where the time goes in v14:
time: 551 us; the launch traced here: 550 us
  waiting for transfers between devices  411 us (75%)
  matrix products  58.7 us (11%)
  local copies, waits for them, and re-layouts  41.3 us (7%)
  starting transfers between devices  15.9 us (3%)
  between operations  13.7 us (2%)
  other arithmetic  9.85 us (2%)
    reduce_scatter x2, waiting for transfers between devices, shards(): slab_sum = lax.psum_scatter(part, 'tok', scatter_dimension=1, tiled=True)  217 us
    reduce_scatter x1, waiting for transfers between devices, shards(): lax.psum_scatter(terms, ('tok', 'out'), scatter_dimension=0, tiled=True)  90.2 us
    ppermute x6, waiting for transfers between devices, shards(): got[s] = lax.ppermute(blocks[s], 'ka', [(i, i ^ s) for i in range(n_ka)])  56.1 us
    dot_general x2, matrix products, shards(): value = jnp.dot(panel, w_h, preferred_element_type=jnp.float32)  35 us
    all_gather x2, waiting for transfers between devices, shards(): head_group = lax.all_gather(context, 'ka', axis=0, tiled=True)  28.8 us
    dot_general x2, matrix products, shards(): jnp.einsum('tsd,doc->tosc', head_group.reshape(n_tok, tokens // n_tok, -1...  19.7 us
    ppermute x3, waiting for transfers between devices, shards(): pieces[s] = lax.ppermute(owed, 'tok', [(i, i ^ s) for i in range(n_tok)])  17.4 us
    slice x1, local copies, waits for them, and re-layouts, shards(): w_qkv[:, c * width + h * piece:c * width + (h + 1) * piece]  13.5 us
  transfers between devices with their start and end apart: 16, of which 8 were waited for; matrix products, arithmetic and copies ran while one was open for 13% of the time, Pallas kernels for 0%

profile of v14, /device:TPU:0, one launch (start us, length us, event | category | flops | bytes accessed | tf_op | source)
XLA Modules:
  0.0 550.3 jit_solution(7277942607117833040)
XLA Ops:
  8.2 13.5 %fusion.44 = (bf16[768,1536]{1,0:T(8,128)(2,1)}, bf16[768,1536]{1,0:T(8,128)(2,1)}, bf16[768,1536]{1,0:T(8,128)(2,1)}, bf16[768,1536]{1,0:T(8,128)(2,1)}, bf16[7...) fusion(bf16[768,12288]{1,0:T(8,128)(2,1)} %param.10), kind=kLoop, calls=%fused_computation.87 | loop fusion | bytes 37748736 | tf_op jit(solution)/shard_map/slice | solution.py:91
  21.7 1.5 dynamic-slice_bitcast_fusion
  23.2 3.0 collective-permute-start
  26.2 1.5 collective-permute-start.1
  27.8 8.4 %collective-permute-done = bf16[256,768]{1,0:T(8,128)(2,1)S(1)} collective-permute-done((bf16[256,768]{1,0:T(8,128)(2,1)S(1)}, bf16[256,768]{1,0:T(8,128)(2,1)S(1)}, u32[]{:S(2)}, u32[]{:S(2)}) %collective-permute-start) | collective-permute-done | bytes 393248 | tf_op jit(solution)/shard_map/ppermute | solution.py:53
  36.2 9.0 %collective-permute-done.1 = bf16[256,768]{1,0:T(8,128)(2,1)S(1)} collective-permute-done((bf16[256,768]{1,0:T(8,128)(2,1)S(1)}, bf16[256,768]{1,0:T(8,128)(2,1)S(1)}, u32[]{:S(2)}, u32[]{:S(2)}) %collective-permute-start.1) | collective-permute-done | bytes 393248 | tf_op jit(solution)/shard_map/ppermute | solution.py:53
  47.4 2.1 gather_fusion.1
  49.7 17.9 %fusion.3 = bf16[1024,6144]{1,0:T(8,128)(2,1)} fusion(bf16[1024,768]{1,0:T(8,128)(2,1)S(1)} %bitcast.100, f32[6144]{0:T(1024)S(1)} %broadcast_in_dim.64, pred[6144]{0:T(1024)(128)(4,1)S(1)} %fusion.27, pred[1024]{0:T(1024)(128)(4,1)S(1)} %fusion.32, bf16[768,1536]{1,0:T(8,128)(2,1)} %get-tuple-element.8, bf16[768,1536]{1,0:T(8,128)(2,1)} %get-tuple-element.9, ...), kind=kOutput, calls=%fused_computation.7 | convolution fusion | flops 9726590976 | bytes 23624704 | tf_op jit(solution)/shard_map/dot_general | solution.py:93
  69.3 17.1 %fusion.5 = bf16[1024,6144]{1,0:T(8,128)(2,1)} fusion(bf16[1024,768]{1,0:T(8,128)(2,1)} %bitcast.101, f32[6144]{0:T(1024)S(1)} %broadcast_in_dim.69, pred[6144]{0:T(1024)(128)(4,1)S(1)} %fusion.27, pred[1024]{0:T(1024)(128)(4,1)S(1)} %fusion.32, bf16[768,1536]{1,0:T(8,128)(2,1)} %get-tuple-element.12, bf16[768,1536]{1,0:T(8,128)(2,1)} %get-tuple-element.13, ...), kind=kOutput, calls=%fused_computation.9 | convolution fusion | flops 9726590976 | bytes 23624704 | tf_op jit(solution)/shard_map/dot_general | solution.py:93
  86.5 1.9 collective-permute-start.6
  88.4 100.6 %reduce-scatter.4.cloned.1.call-done = bf16[1024,1536]{1,0:T(8,128)(2,1)} async-done(((bf16[1024,6144]{1,0:T(8,128)(2,1)}), bf16[1024,1536]{1,0:T(8,128)(2,1)}) %reduce-scatter.4.cloned.1.call-update) | async-done | bytes 3145744 | tf_op jit(solution)/shard_map/reduce_scatter | solution.py:96
  188.9 1.8 fusion.47
  190.7 1.5 collective-permute-start.3
  192.2 2.4 collective-permute-start.4
  196.0 116.8 %reduce-scatter.6.cloned.1.call-done = bf16[1024,1536]{1,0:T(8,128)(2,1)} async-done(((bf16[1024,6144]{1,0:T(8,128)(2,1)}), bf16[1024,1536]{1,0:T(8,128)(2,1)}) %reduce-scatter.6.cloned.1.call-update) | async-done | bytes 3145744 | tf_op jit(solution)/shard_map/reduce_scatter | solution.py:96
  312.8 3.0 fusion.46
  315.8 1.5 collective-permute-start.7
  317.2 2.4 collective-permute-start.8
  320.2 2.2 add_convert_fusion.1
  324.8 38.2 %collective-permute-done.7 = bf16[256,1536]{1,0:T(8,128)(2,1)} collective-permute-done((bf16[256,1536]{1,0:T(8,128)(2,1)}, bf16[256,1536]{1,0:T(8,128)(2,1)}, u32[]{:S(2)}, u32[]{:S(2)}) %collective-permute-start.7) | collective-permute-done | bytes 786464 | tf_op jit(solution)/shard_map/ppermute | solution.py:101
  362.9 18.0 %collective-permute-done.8 = bf16[256,1536]{1,0:T(8,128)(2,1)} collective-permute-done((bf16[256,1536]{1,0:T(8,128)(2,1)}, bf16[256,1536]{1,0:T(8,128)(2,1)}, u32[]{:S(2)}, u32[]{:S(2)}) %collective-permute-start.8) | collective-permute-done | bytes 786464 | tf_op jit(solution)/shard_map/ppermute | solution.py:101
  380.9 2.3 add_convert_fusion
  385.8 4.9 fusion.45
  390.7 2.8 copy.44
  393.5 3.2 copy.48
  396.7 2.3 copy.22
  399.0 10.2 %fusion.51 = f32[4,256,2,1536]{3,1,2,0:T(8,128)} fusion(bf16[4,256,512,1]{2,1,3,0:T(8,128)(2,1)} %bitcast.102, bf16[512,2,1536,1]{0,2,1,3:T(8,128)(2,1)} %bitcast.93), kind=kOutput, calls=%fused_computation.94 | convolution fusion | flops 3221225472 | bytes 16777216 | tf_op jit(solution)/shard_map/tsd,doc->tosc/dot_general | solution.py:110
  409.2 28.8 %all-gather.8.cloned.1.call-done = bf16[1024,512]{0,1:T(8,128)(2,1)} async-done(((bf16[256,512]{0,1:T(8,128)(2,1)}), bf16[1024,512]{0,1:T(8,128)(2,1)}) %all-gather.8.cloned.1.call-update) | async-done | bytes 1048592 | tf_op jit(solution)/shard_map/all_gather | solution.py:109
  438.0 2.3 copy.30
  440.3 9.5 %convolution_add_fusion = f32[4,256,2,1536]{3,1,2,0:T(8,128)} fusion(f32[4,256,2,1536]{3,1,2,0:T(8,128)} %fusion.51, bf16[4,256,512,1]{2,1,3,0:T(8,128)(2,1)} %bitcast.92, bf16[512,2,1536,1]{0,2,1,3:T(8,128)(2,1)S(1)} %bitcast.91), kind=kOutput, calls=%fused_computation.24 | convolution fusion | flops 3224371200 | bytes 29360128 | tf_op jit(solution)/shard_map/tsd,doc->tosc/dot_general | solution.py:110
  450.5 90.2 %reduce-scatter.8.cloned.1.call-done = f32[1,256,1536]{2,1,0:T(8,128)} async-done(((f32[8,256,1536]{2,1,0:T(8,128)}), f32[1,256,1536]{2,1,0:T(8,128)}) %reduce-scatter.8.cloned.1.call-update) | async-done | bytes 1572880 | tf_op jit(solution)/shard_map/reduce_scatter | solution.py:118
  540.7 2.7 bitcast_add_fusion
  (56 shorter events, 13.1 us)
Async XLA Ops:
  6.5 15.2 %all-gather.4.cloned.1.call-start = ((), (), s32[]{:S(2)}) async-start(), calls=%async_computation.3 | async-start | bytes 2359296 | tf_op jit(solution)/shard_map/all_gather | solution.py:46
  7.3 181.7 %reduce-scatter.4.cloned.1.call-start = ((), (), s32[]{:S(2)}) async-start(), calls=%async_computation.4 | async-start | bytes 15728640 | tf_op jit(solution)/shard_map/reduce_scatter | solution.py:96
  23.2 13.0 %collective-permute-start = (bf16[256,768]{1,0:T(8,128)(2,1)S(1)}, bf16[256,768]{1,0:T(8,128)(2,1)S(1)}, u32[]{:S(2)}, u32[]{:S(2)}) collective-permute-start(bf16[256,768]{1,0:T(8,128)(2,1)S(1)} %get-tuple-element.25), channel_id=1, source_target_pairs={{0,8},{8,0},{16,24},{24,16},{1,9},{9,1},{17,25},{25,17},{2,10},{10... | collective-permute-start | bytes 1179656 | tf_op jit(solution)/shard_map/ppermute | solution.py:53
  26.2 19.0 %collective-permute-start.1 = (bf16[256,768]{1,0:T(8,128)(2,1)S(1)}, bf16[256,768]{1,0:T(8,128)(2,1)S(1)}, u32[]{:S(2)}, u32[]{:S(2)}) collective-permute-start(bf16[256,768]{1,0:T(8,128)(2,1)S(1)} %get-tuple-element.24), channel_id=1, source_target_pairs={{0,16},{8,24},{16,0},{24,8},{1,17},{9,25},{17,1},{25,9},{2,18},{10... | collective-permute-start | bytes 1179656 | tf_op jit(solution)/shard_map/ppermute | solution.py:53
  27.8 17.5 %collective-permute-start.2 = (bf16[256,768]{1,0:T(8,128)(2,1)S(1)}, bf16[256,768]{1,0:T(8,128)(2,1)S(1)}, u32[]{:S(2)}, u32[]{:S(2)}) collective-permute-start(bf16[256,768]{1,0:T(8,128)(2,1)S(1)} %get-tuple-element.23), channel_id=1, source_target_pairs={{0,24},{8,16},{16,8},{24,0},{1,25},{9,17},{17,9},{25,1},{2,26},{10... | collective-permute-start | bytes 1179656 | tf_op jit(solution)/shard_map/ppermute | solution.py:53
  49.7 17.9 %copy-start.1 = (bf16[4,256,768]{2,1,0:T(8,128)(2,1)}, bf16[4,256,768]{2,1,0:T(8,128)(2,1)S(1)}, u32[]{:S(2)}) copy-start(bf16[4,256,768]{2,1,0:T(8,128)(2,1)S(1)} %broadcast_select_fusion) | copy-start | bytes 4718596
  67.7 1.7 copy-start
  67.7 245.1 %reduce-scatter.6.cloned.1.call-start = ((), (), s32[]{:S(2)}) async-start(), calls=%async_computation.6 | async-start | bytes 15728640 | tf_op jit(solution)/shard_map/reduce_scatter | solution.py:96
  86.4 310.3 %all-gather.6.cloned.1.call-start = ((), (), s32[]{:S(2)}) async-start(), calls=%async_computation.5 | async-start | bytes 1310720 | tf_op jit(solution)/shard_map/all_gather | solution.py:109
  86.5 108.7 %collective-permute-start.6 = (s32[1]{0:T(128)}, s32[1]{0:T(128)}, u32[]{:S(2)}, u32[]{:S(2)}) collective-permute-start(s32[1]{0:T(128)} %param.9), channel_id=1, source_target_pairs={{0,0},{2,8},{4,16},{6,24},{8,2},{10,10},{12,18},{14,26},{16,4},{18... | collective-permute-start | bytes 20 | tf_op jit(solution)/shard_map/ppermute | solution.py:73
  190.7 129.0 %collective-permute-start.3 = (bf16[256,1536]{1,0:T(8,128)(2,1)S(1)}, bf16[256,1536]{1,0:T(8,128)(2,1)}, u32[]{:S(2)}, u32[]{:S(2)}) collective-permute-start(bf16[256,1536]{1,0:T(8,128)(2,1)S(1)} %get-tuple-element.19), channel_id=1, source_target_pairs={{0,2},{2,0},{4,6},{6,4},{1,3},{3,1},{5,7},{7,5},{8,10},{10,8},{12,... | collective-permute-start | bytes 2359304 | tf_op jit(solution)/shard_map/ppermute | solution.py:101
  192.2 127.9 %collective-permute-start.4 = (bf16[256,1536]{1,0:T(8,128)(2,1)S(1)}, bf16[256,1536]{1,0:T(8,128)(2,1)}, u32[]{:S(2)}, u32[]{:S(2)}) collective-permute-start(bf16[256,1536]{1,0:T(8,128)(2,1)S(1)} %get-tuple-element.21), channel_id=1, source_target_pairs={{0,4},{2,6},{4,0},{6,2},{1,5},{3,7},{5,1},{7,3},{8,12},{10,14},{12... | collective-permute-start | bytes 2359304 | tf_op jit(solution)/shard_map/ppermute | solution.py:101
  194.7 125.5 %collective-permute-start.5 = (bf16[256,1536]{1,0:T(8,128)(2,1)S(1)}, bf16[256,1536]{1,0:T(8,128)(2,1)}, u32[]{:S(2)}, u32[]{:S(2)}) collective-permute-start(bf16[256,1536]{1,0:T(8,128)(2,1)S(1)} %get-tuple-element.20), channel_id=1, source_target_pairs={{0,6},{2,4},{4,2},{6,0},{1,7},{3,5},{5,3},{7,1},{8,14},{10,12},{12... | collective-permute-start | bytes 2359304 | tf_op jit(solution)/shard_map/ppermute | solution.py:101
  315.8 47.2 %collective-permute-start.7 = (bf16[256,1536]{1,0:T(8,128)(2,1)}, bf16[256,1536]{1,0:T(8,128)(2,1)}, u32[]{:S(2)}, u32[]{:S(2)}) collective-permute-start(bf16[256,1536]{1,0:T(8,128)(2,1)} %get-tuple-element.16), channel_id=1, source_target_pairs={{0,2},{2,0},{4,6},{6,4},{1,3},{3,1},{5,7},{7,5},{8,10},{10,8},{12,... | collective-permute-start | bytes 2359304 | tf_op jit(solution)/shard_map/ppermute | solution.py:101
  317.2 63.7 %collective-permute-start.8 = (bf16[256,1536]{1,0:T(8,128)(2,1)}, bf16[256,1536]{1,0:T(8,128)(2,1)}, u32[]{:S(2)}, u32[]{:S(2)}) collective-permute-start(bf16[256,1536]{1,0:T(8,128)(2,1)} %get-tuple-element.18), channel_id=1, source_target_pairs={{0,4},{2,6},{4,0},{6,2},{1,5},{3,7},{5,1},{7,3},{8,12},{10,14},{12... | collective-permute-start | bytes 2359304 | tf_op jit(solution)/shard_map/ppermute | solution.py:101
  319.7 61.2 %collective-permute-start.9 = (bf16[256,1536]{1,0:T(8,128)(2,1)S(1)}, bf16[256,1536]{1,0:T(8,128)(2,1)}, u32[]{:S(2)}, u32[]{:S(2)}) collective-permute-start(bf16[256,1536]{1,0:T(8,128)(2,1)S(1)} %get-tuple-element.17), channel_id=1, source_target_pairs={{0,6},{2,4},{4,2},{6,0},{1,7},{3,5},{5,3},{7,1},{8,14},{10,12},{12... | collective-permute-start | bytes 2359304 | tf_op jit(solution)/shard_map/ppermute | solution.py:101
  324.7 113.3 %all-gather.8.cloned.1.call-start = ((), (), s32[]{:S(2)}) async-start(), calls=%async_computation.7 | async-start | bytes 1310720 | tf_op jit(solution)/shard_map/all_gather | solution.py:109
  385.5 155.2 %reduce-scatter.8.cloned.1.call-start = ((), (), s32[]{:S(2)}) async-start(), calls=%async_computation.8 | async-start | bytes 14155776 | tf_op jit(solution)/shard_map/reduce_scatter | solution.py:118
  449.8 0.7 copy-start.2
Sparse Core Ops, SparseCore 0:
  8.9 12.4 all-gather.3
  67.8 121.0 reduce-scatter.3
  192.0 120.7 reduce-scatter.5
  324.8 70.7 all-gather.5
  397.0 40.9 all-gather.7
  450.0 90.7 reduce-scatter.7

commit v15 on v14

--- a/solution.py
+++ b/solution.py
@@ -76,22 +76,23 @@
         per = all_lengths.shape[0] // n_ka
         own_lengths = lax.dynamic_slice_in_dim(all_lengths, k * per, per)
     heads_block = width // (3 * HD)
-    n_streams = 2 if heads_block % 2 == 0 else 1
-    piece = width // n_streams
+    first = (heads_block * 5) // 8
+    counts = [first, heads_block - first] if 0 < first < heads_block else [heads_block]
+    n_streams = len(counts)
+    starts = [sum(counts[:i]) for i in range(n_streams)]
     own_rows = prompt_of == t
     bias = b_qkv.astype(jnp.float32)
-    w_rows = w_out.shape[0] // n_streams
-
-    col_block = lax.broadcasted_iota(jnp.int32, (1, n_tok * piece), 1) // piece
-    here = own_rows & (col_block == k)
 
     terms = None
     for h in range(n_streams):
+        lo, piece = starts[h] * 3 * HD, counts[h] * 3 * HD
         w_h = jnp.concatenate(
-            [w_qkv[:, c * width + h * piece:c * width + (h + 1) * piece] for c in range(n_tok)], axis=1
+            [w_qkv[:, c * width + lo:c * width + lo + piece] for c in range(n_tok)], axis=1
         )
         value = jnp.dot(panel, w_h, preferred_element_type=jnp.float32)
-        bias_row = jnp.tile(bias[h * piece:(h + 1) * piece], n_tok)[None, :]
+        col_block = lax.broadcasted_iota(jnp.int32, (1, n_tok * piece), 1) // piece
+        here = own_rows & (col_block == k)
+        bias_row = jnp.tile(bias[lo:lo + piece], n_tok)[None, :]
         part = (value + jnp.where(here, bias_row, 0.0)).astype(jnp.bfloat16)
         slab_sum = lax.psum_scatter(part, "tok", scatter_dimension=1, tiled=True)
         if by_xor:
@@ -110,7 +111,7 @@
         term = jnp.einsum(
             "tsd,doc->tosc",
             head_group.reshape(n_tok, tokens // n_tok, -1),
-            w_out[h * w_rows:(h + 1) * w_rows].reshape(w_rows, n_out, -1),
+            w_out[starts[h] * HD:(starts[h] + counts[h]) * HD].reshape(counts[h] * HD, n_out, -1),
             preferred_element_type=jnp.float32,
         )
         terms = term if terms is None else terms + term

time: 551 us -> 559 us (1.015)
  waiting for transfers between devices: 411 us -> 342 us
  blocking collectives: 0 us -> 41.2 us
  local copies, waits for them, and re-layouts: 41.3 us -> 78.4 us
    reduce_scatter x2 -> x0, waiting for transfers between devices: 217 us -> none  [shards(): slab_sum = lax.psum_scatter(part, 'tok', scatter_dimension=1, tiled=True)]
    unnamed x6 -> x7, waiting for transfers between devices: 0.79 us -> 206 us
    all_gather x0 -> x1, blocking collectives: none -> 41.2 us  [shards(): head_group = lax.all_gather(context, 'ka', axis=0, tiled=True)]
    unnamed x8 -> x10, local copies, waits for them, and re-layouts: 8.07 us -> 43.6 us
    ppermute x6, waiting for transfers between devices: 56.1 us -> 25.1 us  [shards(): got[s] = lax.ppermute(blocks[s], 'ka', [(i, i ^ s) for i in range(n_ka)])]
    all_gather x2 -> x1, waiting for transfers between devices: 28.8 us -> 0.02 us  [shards(): head_group = lax.all_gather(context, 'ka', axis=0, tiled=True)]
    slice x3 -> x6, local copies, waits for them, and re-layouts: 19.2 us -> 20.5 us  [the longest x2 12.3 us: shards(): w_qkv[:, c * width + lo:c * width + lo + piece]]
  transfers between devices with their start and end apart: 16 -> 15, of which waited for: 8 -> 9; matrix products, arithmetic and copies ran while one was open for 13% -> 14% of each run, Pallas kernels for 0% -> 0%
where the time goes in v15:
time: 559 us; the launch traced here: 557 us
  waiting for transfers between devices  342 us (61%)
  local copies, waits for them, and re-layouts  78.4 us (14%)
  matrix products  56.6 us (10%)
  blocking collectives  41.2 us (7%)
  starting transfers between devices  14.6 us (3%)
  between operations  13.3 us (2%)
  other arithmetic  10.5 us (2%)
    unnamed x7, waiting for transfers between devices  206 us
    reduce_scatter x1, waiting for transfers between devices, shards(): lax.psum_scatter(terms, ('tok', 'out'), scatter_dimension=0, tiled=True)  89.5 us
    unnamed x10, local copies, waits for them, and re-layouts  43.6 us
    all_gather x1, blocking collectives, shards(): head_group = lax.all_gather(context, 'ka', axis=0, tiled=True)  41.2 us
    dot_general x2, matrix products, shards(): value = jnp.dot(panel, w_h, preferred_element_type=jnp.float32)  33 us
    ppermute x6, waiting for transfers between devices, shards(): got[s] = lax.ppermute(blocks[s], 'ka', [(i, i ^ s) for i in range(n_ka)])  25.1 us
    ppermute x3, waiting for transfers between devices, shards(): pieces[s] = lax.ppermute(owed, 'tok', [(i, i ^ s) for i in range(n_tok)])  17.7 us
    dot_general x2, matrix products, shards(): jnp.einsum('tsd,doc->tosc', head_group.reshape(n_tok, tokens // n_tok, -1...  14.2 us
  transfers between devices with their start and end apart: 15, of which 9 were waited for; matrix products, arithmetic and copies ran while one was open for 14% of the time, Pallas kernels for 0%

profile of v15, /device:TPU:0, one launch (start us, length us, event | category | flops | bytes accessed | tf_op | source)
XLA Modules:
  0.0 556.9 jit_solution(15615757929556096957)
XLA Ops:
  8.1 8.7 %fusion.50 = (bf16[768,1920]{1,0:T(8,128)(2,1)}, bf16[768,1920]{1,0:T(8,128)(2,1)}, bf16[768,1920]{1,0:T(8,128)(2,1)}, bf16[768,1920]{1,0:T(8,128)(2,1)}) fusion(bf16[768,12288]{1,0:T(8,128)(2,1)} %param.10), kind=kLoop, calls=%fused_computation.95 | loop fusion | bytes 23592960 | tf_op jit(solution)/shard_map/slice | solution.py:90
  16.8 4.7 all-gather.3.cloned.1.call-done
  26.5 8.4 %collective-permute-done = bf16[256,768]{1,0:T(8,128)(2,1)S(1)} collective-permute-done((bf16[256,768]{1,0:T(8,128)(2,1)S(1)}, bf16[256,768]{1,0:T(8,128)(2,1)S(1)}, u32[]{:S(2)}, u32[]{:S(2)}) %collective-permute-start) | collective-permute-done | bytes 393248 | tf_op jit(solution)/shard_map/ppermute | solution.py:53
  34.9 9.2 %collective-permute-done.1 = bf16[256,768]{1,0:T(8,128)(2,1)S(1)} collective-permute-done((bf16[256,768]{1,0:T(8,128)(2,1)S(1)}, bf16[256,768]{1,0:T(8,128)(2,1)S(1)}, u32[]{:S(2)}, u32[]{:S(2)}) %collective-permute-start.1) | collective-permute-done | bytes 393248 | tf_op jit(solution)/shard_map/ppermute | solution.py:53
  46.4 2.1 gather_fusion.1
  48.7 21.3 %add_convert_fusion = bf16[1024,7680]{1,0:T(8,128)(2,1)} fusion(bf16[1024,768]{1,0:T(8,128)(2,1)S(1)} %bitcast.118, f32[7680]{0:T(1024)S(1)} %broadcast_in_dim.78, pred[7680]{0:T(1024)(128)(4,1)S(1)} %fusion.23, pred[1024]{0:T(1024)(128)(4,1)S(1)} %fusion.32, bf16[768,1920]{1,0:T(8,128)(2,1)} %get-tuple-element.11, bf16[768,1920]{1,0:T(8,128)(2,1)} %get-tuple-element.12, ...), kind=kOutput, calls=%fused_computation.4 | convolution fusion | flops 12158238720 | bytes 29137408 | tf_op jit(solution)/shard_map/dot_general | solution.py:92
  69.9 20.6 %copy.63 = bf16[1024,7680]{0,1:T(8,128)(2,1)} copy(bf16[1024,7680]{1,0:T(8,128)(2,1)} %add_convert_fusion) | data formatting | bytes 31457280
  91.3 3.6 fusion.49
  94.9 11.8 %add_convert_fusion.1 = bf16[1024,4608]{1,0:T(8,128)(2,1)} fusion(bf16[1024,768]{1,0:T(8,128)(2,1)S(1)} %bitcast.119, f32[4608]{0:T(1024)S(1)} %broadcast_in_dim.83, pred[4608]{0:T(1024)(128)(4,1)S(1)} %fusion.27, pred[1024]{0:T(1024)(128)(4,1)S(1)} %fusion.32, bf16[768,1152]{1,0:T(8,128)(2,1)S(1)} %get-tuple-element.8, ...), kind=kOutput, calls=%fused_computation.5 | convolution fusion | flops 7294943232 | bytes 18112000 | tf_op jit(solution)/shard_map/dot_general | solution.py:92
  106.7 12.7 %copy.65 = bf16[1024,4608]{0,1:T(8,128)(2,1)} copy(bf16[1024,4608]{1,0:T(8,128)(2,1)} %add_convert_fusion.1) | data formatting | bytes 18874368
  119.4 117.8 %reduce-scatter.10.cloned.1.call-done = bf16[1920,1024]{1,0:T(8,128)(2,1)} async-done(((bf16[7680,1024]{1,0:T(8,128)(2,1)}), bf16[1920,1024]{1,0:T(8,128)(2,1)}) %reduce-scatter.10.cloned.1.call-update) | async-done | bytes 3932176
  237.2 3.5 fusion.51
  242.2 2.4 collective-permute-start.4
  248.4 87.0 %reduce-scatter.12.cloned.1.call-done = bf16[1152,1024]{1,0:T(8,128)(2,1)} async-done(((bf16[4608,1024]{1,0:T(8,128)(2,1)}), bf16[1152,1024]{1,0:T(8,128)(2,1)}) %reduce-scatter.12.cloned.1.call-update) | async-done | bytes 2359312
  335.4 2.6 fusion.52
  339.5 2.4 collective-permute-start.8
  342.4 2.6 add_convert_fusion.2
  346.8 2.4 convolution_convert_fusion
  349.3 4.3 slice.98
  353.5 3.3 slice.111
  356.8 6.2 %copy.70 = bf16[640,3072]{0,1:T(8,128)(2,1)} copy(bf16[640,3072]{1,0:T(8,128)(2,1)} %slice.98) | data formatting | bytes 7864320
  363.1 3.0 copy.74
  366.1 2.6 collective-permute-done.7
  368.6 6.6 %collective-permute-done.8 = bf16[256,1152]{0,1:T(8,128)(2,1)} collective-permute-done((bf16[256,1152]{0,1:T(8,128)(2,1)}, bf16[256,1152]{0,1:T(8,128)(2,1)}, u32[]{:S(2)}, u32[]{:S(2)}) %collective-permute-start.8) | collective-permute-done | bytes 589856 | tf_op jit(solution)/shard_map/ppermute | solution.py:102
  375.3 15.8 %collective-permute-done.9 = bf16[256,1152]{0,1:T(8,128)(2,1)} collective-permute-done((bf16[256,1152]{0,1:T(8,128)(2,1)S(1)}, bf16[256,1152]{0,1:T(8,128)(2,1)}, u32[]{:S(2)}, u32[]{:S(2)}) %collective-permute-start.9) | collective-permute-done | bytes 589856 | tf_op jit(solution)/shard_map/ppermute | solution.py:102
  394.3 2.0 fusion.21
  398.2 41.2 %all_gather.11 = bf16[1024,384]{0,1:T(8,128)(2,1)} all-gather(bf16[256,384]{0,1:T(8,128)(2,1)S(1)} %bitcast.127), channel_id=1, replica_groups=mesh['tok'=4,'ka'=4,'out'=2] {'ka'}, dimensions={0}, use_global_device_ids=true | all-gather | bytes 983040 | tf_op jit(solution)/shard_map/all_gather | solution.py:110
  440.9 2.4 copy.41
  443.3 7.6 %fusion.55 = f32[4,256,2,1536]{3,1,2,0:T(8,128)S(1)} fusion(bf16[4,256,640,1]{2,1,3,0:T(8,128)(2,1)} %bitcast.120, bf16[640,2,1536,1]{0,2,1,3:T(8,128)(2,1)} %bitcast.111), kind=kOutput, calls=%fused_computation.100 | convolution fusion | flops 4026531840 | bytes 17825792 | tf_op jit(solution)/shard_map/tsd,doc->tosc/dot_general | solution.py:111
  450.9 6.6 %convolution_add_fusion = f32[4,256,2,1536]{3,1,2,0:T(8,128)} fusion(f32[4,256,2,1536]{3,1,2,0:T(8,128)S(1)} %fusion.55, bf16[4,256,384,1]{2,1,3,0:T(8,128)(2,1)S(1)} %bitcast.112, bf16[384,2,1536,1]{0,2,1,3:T(8,128)(2,1)S(1)} %bitcast.108), kind=kOutput, calls=%fused_computation.20 | convolution fusion | flops 2419064832 | bytes 28311552 | tf_op jit(solution)/shard_map/tsd,doc->tosc/dot_general | solution.py:111
  458.2 89.5 %reduce-scatter.8.cloned.1.call-done = f32[1,256,1536]{2,1,0:T(8,128)} async-done(((f32[8,256,1536]{2,1,0:T(8,128)}), f32[1,256,1536]{2,1,0:T(8,128)}) %reduce-scatter.8.cloned.1.call-update) | async-done | bytes 1572880 | tf_op jit(solution)/shard_map/reduce_scatter | solution.py:119
  547.7 2.7 bitcast_add_fusion
  (57 shorter events, 26.0 us)
Async XLA Ops:
  6.5 14.9 %all-gather.3.cloned.1.call-start = ((), (), s32[]{:S(2)}) async-start(), calls=%async_computation.3 | async-start | bytes 2359296 | tf_op jit(solution)/shard_map/all_gather | solution.py:46
  7.3 230.0 %reduce-scatter.10.cloned.1.call-start = ((), (), s32[]{:S(2)}) async-start(), calls=%async_computation.6 | async-start | bytes 19660800
  22.9 12.0 %collective-permute-start = (bf16[256,768]{1,0:T(8,128)(2,1)S(1)}, bf16[256,768]{1,0:T(8,128)(2,1)S(1)}, u32[]{:S(2)}, u32[]{:S(2)}) collective-permute-start(bf16[256,768]{1,0:T(8,128)(2,1)S(1)} %get-tuple-element.23), channel_id=1, source_target_pairs={{0,8},{8,0},{16,24},{24,16},{1,9},{9,1},{17,25},{25,17},{2,10},{10... | collective-permute-start | bytes 1179656 | tf_op jit(solution)/shard_map/ppermute | solution.py:53
  24.7 19.5 %collective-permute-start.1 = (bf16[256,768]{1,0:T(8,128)(2,1)S(1)}, bf16[256,768]{1,0:T(8,128)(2,1)S(1)}, u32[]{:S(2)}, u32[]{:S(2)}) collective-permute-start(bf16[256,768]{1,0:T(8,128)(2,1)S(1)} %get-tuple-element.22), channel_id=1, source_target_pairs={{0,16},{8,24},{16,0},{24,8},{1,17},{9,25},{17,1},{25,9},{2,18},{10... | collective-permute-start | bytes 1179656 | tf_op jit(solution)/shard_map/ppermute | solution.py:53
  26.2 18.0 %collective-permute-start.2 = (bf16[256,768]{1,0:T(8,128)(2,1)S(1)}, bf16[256,768]{1,0:T(8,128)(2,1)S(1)}, u32[]{:S(2)}, u32[]{:S(2)}) collective-permute-start(bf16[256,768]{1,0:T(8,128)(2,1)S(1)} %get-tuple-element.21), channel_id=1, source_target_pairs={{0,24},{8,16},{16,8},{24,0},{1,25},{9,17},{17,9},{25,1},{2,26},{10... | collective-permute-start | bytes 1179656 | tf_op jit(solution)/shard_map/ppermute | solution.py:53
  90.5 0.7 copy-start.1
  90.6 244.9 %reduce-scatter.12.cloned.1.call-start = ((), (), s32[]{:S(2)}) async-start(), calls=%async_computation.7 | async-start | bytes 11796480
  119.4 321.5 %all-gather.5.cloned.1.call-start = ((), (), s32[]{:S(2)}) async-start(), calls=%async_computation.4 | async-start | bytes 1638400 | tf_op jit(solution)/shard_map/all_gather | solution.py:110
  240.7 101.2 %collective-permute-start.3 = (bf16[256,1920]{0,1:T(8,128)(2,1)}, bf16[256,1920]{0,1:T(8,128)(2,1)S(1)}, u32[]{:S(2)}, u32[]{:S(2)}) collective-permute-start(bf16[256,1920]{0,1:T(8,128)(2,1)} %get-tuple-element.14), channel_id=1, source_target_pairs={{0,2},{2,0},{4,6},{6,4},{1,3},{3,1},{5,7},{7,5},{8,10},{10,8},{12,... | collective-permute-start | bytes 2949128 | tf_op jit(solution)/shard_map/ppermute | solution.py:102
  242.2 100.2 %collective-permute-start.4 = (bf16[256,1920]{0,1:T(8,128)(2,1)}, bf16[256,1920]{0,1:T(8,128)(2,1)S(1)}, u32[]{:S(2)}, u32[]{:S(2)}) collective-permute-start(bf16[256,1920]{0,1:T(8,128)(2,1)} %get-tuple-element.15), channel_id=1, source_target_pairs={{0,4},{2,6},{4,0},{6,2},{1,5},{3,7},{5,1},{7,3},{8,12},{10,14},{12... | collective-permute-start | bytes 2949128 | tf_op jit(solution)/shard_map/ppermute | solution.py:102
  244.6 97.8 %collective-permute-start.5 = (bf16[256,1920]{0,1:T(8,128)(2,1)}, bf16[256,1920]{0,1:T(8,128)(2,1)S(1)}, u32[]{:S(2)}, u32[]{:S(2)}) collective-permute-start(bf16[256,1920]{0,1:T(8,128)(2,1)} %get-tuple-element.16), channel_id=1, source_target_pairs={{0,6},{2,4},{4,2},{6,0},{1,7},{3,5},{5,3},{7,1},{8,14},{10,12},{12... | collective-permute-start | bytes 2949128 | tf_op jit(solution)/shard_map/ppermute | solution.py:102
  245.1 1.9 collective-permute-start.6
  338.0 30.6 %collective-permute-start.7 = (bf16[256,1152]{0,1:T(8,128)(2,1)}, bf16[256,1152]{0,1:T(8,128)(2,1)}, u32[]{:S(2)}, u32[]{:S(2)}) collective-permute-start(bf16[256,1152]{0,1:T(8,128)(2,1)} %get-tuple-element.17), channel_id=1, source_target_pairs={{0,2},{2,0},{4,6},{6,4},{1,3},{3,1},{5,7},{7,5},{8,10},{10,8},{12,... | collective-permute-start | bytes 1769480 | tf_op jit(solution)/shard_map/ppermute | solution.py:102
  339.5 35.8 %collective-permute-start.8 = (bf16[256,1152]{0,1:T(8,128)(2,1)}, bf16[256,1152]{0,1:T(8,128)(2,1)}, u32[]{:S(2)}, u32[]{:S(2)}) collective-permute-start(bf16[256,1152]{0,1:T(8,128)(2,1)} %get-tuple-element.18), channel_id=1, source_target_pairs={{0,4},{2,6},{4,0},{6,2},{1,5},{3,7},{5,1},{7,3},{8,12},{10,14},{12... | collective-permute-start | bytes 1769480 | tf_op jit(solution)/shard_map/ppermute | solution.py:102
  341.9 49.2 %collective-permute-start.9 = (bf16[256,1152]{0,1:T(8,128)(2,1)S(1)}, bf16[256,1152]{0,1:T(8,128)(2,1)}, u32[]{:S(2)}, u32[]{:S(2)}) collective-permute-start(bf16[256,1152]{0,1:T(8,128)(2,1)S(1)} %get-tuple-element.19), channel_id=1, source_target_pairs={{0,6},{2,4},{4,2},{6,0},{1,7},{3,5},{5,3},{7,1},{8,14},{10,12},{12... | collective-permute-start | bytes 1769480 | tf_op jit(solution)/shard_map/ppermute | solution.py:102
  345.0 1.8 copy-start
  349.2 198.5 %reduce-scatter.8.cloned.1.call-start = ((), (), s32[]{:S(2)}) async-start(), calls=%async_computation.5 | async-start | bytes 14155776 | tf_op jit(solution)/shard_map/reduce_scatter | solution.py:119
  457.5 0.7 copy-start.2
Sparse Core Ops, SparseCore 0:
  8.9 12.4 all-gather.2
  90.7 146.5 reduce-scatter.9
  240.3 95.0 reduce-scatter.11
  349.3 63.0 all-gather.4
  457.7 89.9 reduce-scatter.7

commit v16 on v14

--- a/solution.py
+++ b/solution.py
@@ -85,6 +85,11 @@
     col_block = lax.broadcasted_iota(jnp.int32, (1, n_tok * piece), 1) // piece
     here = own_rows & (col_block == k)
 
+    w_out_t = [
+        jnp.transpose(w_out[h * w_rows:(h + 1) * w_rows].reshape(w_rows, n_out, -1), (1, 2, 0))
+        for h in range(n_streams)
+    ]
+    w_out_t, panel = lax.optimization_barrier((w_out_t, panel))
     terms = None
     for h in range(n_streams):
         w_h = jnp.concatenate(
@@ -108,9 +113,9 @@
         context = attention(qkv_held, own_lengths)
         head_group = lax.all_gather(context, "ka", axis=0, tiled=True)
         term = jnp.einsum(
-            "tsd,doc->tosc",
+            "tsd,ocd->tosc",
             head_group.reshape(n_tok, tokens // n_tok, -1),
-            w_out[h * w_rows:(h + 1) * w_rows].reshape(w_rows, n_out, -1),
+            w_out_t[h],
             preferred_element_type=jnp.float32,
         )
         terms = term if terms is None else terms + term

time: 551 us -> 590 us (1.071)
  local copies, waits for them, and re-layouts: 41.3 us -> 61.3 us
  matrix products: 58.7 us -> 68.6 us
  other arithmetic: 9.85 us -> 16.7 us
    add x0 -> x1, local copies, waits for them, and re-layouts: none -> 12.6 us  [shards(): terms = term if terms is None else terms + term]
    all_gather x2, waiting for transfers between devices: 28.8 us -> 40.9 us  [shards(): head_group = lax.all_gather(context, 'ka', axis=0, tiled=True)]
    ppermute x6, waiting for transfers between devices: 56.1 us -> 47.5 us  [shards(): got[s] = lax.ppermute(blocks[s], 'ka', [(i, i ^ s) for i in range(n_ka)])]
    unnamed x8 -> x4, local copies, waits for them, and re-layouts: 8.07 us -> 0.67 us
    reshape x0 -> x2, local copies, waits for them, and re-layouts: none -> 6.11 us  [shards(): w_out[h * w_rows:(h + 1) * w_rows].reshape(w_rows, n_out, -1)]
  transfers between devices with their start and end apart: 16 -> 16, of which waited for: 8 -> 9; matrix products, arithmetic and copies ran while one was open for 13% -> 15% of each run, Pallas kernels for 0% -> 0%
where the time goes in v16:
time: 590 us; the launch traced here: 589 us
  waiting for transfers between devices  413 us (70%)
  matrix products  68.6 us (12%)
  local copies, waits for them, and re-layouts  61.3 us (10%)
  other arithmetic  16.7 us (3%)
  starting transfers between devices  15.5 us (3%)
  between operations  13.6 us (2%)
    reduce_scatter x2, waiting for transfers between devices, shards(): slab_sum = lax.psum_scatter(part, 'tok', scatter_dimension=1, tiled=True)  216 us
    reduce_scatter x1, waiting for transfers between devices, shards(): lax.psum_scatter(terms, ('tok', 'out'), scatter_dimension=0, tiled=True)  90.2 us
    ppermute x6, waiting for transfers between devices, shards(): got[s] = lax.ppermute(blocks[s], 'ka', [(i, i ^ s) for i in range(n_ka)])  47.5 us
    all_gather x2, waiting for transfers between devices, shards(): head_group = lax.all_gather(context, 'ka', axis=0, tiled=True)  40.9 us
    dot_general x2, matrix products, shards(): value = jnp.dot(panel, w_h, preferred_element_type=jnp.float32)  35.7 us
    dot_general x2, matrix products, shards(): jnp.einsum('tsd,ocd->tosc', head_group.reshape(n_tok, tokens // n_tok, -1...  19.6 us
    ppermute x3, waiting for transfers between devices, shards(): pieces[s] = lax.ppermute(owed, 'tok', [(i, i ^ s) for i in range(n_tok)])  17.6 us
    slice x1, local copies, waits for them, and re-layouts, shards(): w_qkv[:, c * width + h * piece:c * width + (h + 1) * piece]  13.7 us
  transfers between devices with their start and end apart: 16, of which 9 were waited for; matrix products, arithmetic and copies ran while one was open for 15% of the time, Pallas kernels for 0%

profile of v16, /device:TPU:0, one launch (start us, length us, event | category | flops | bytes accessed | tf_op | source)
XLA Modules:
  0.0 589.2 jit_solution(17256294451777854332)
XLA Ops:
  7.3 4.9 fusion.48
  12.2 2.9 copy.38
  15.1 3.3 copy.39
  18.5 13.7 %fusion.47 = (bf16[768,1536]{1,0:T(8,128)(2,1)}, bf16[768,1536]{1,0:T(8,128)(2,1)}, bf16[768,1536]{1,0:T(8,128)(2,1)}, bf16[768,1536]{1,0:T(8,128)(2,1)}, bf16[7...) fusion(bf16[768,12288]{1,0:T(8,128)(2,1)} %param.10), kind=kLoop, calls=%fused_computation.90 | loop fusion | bytes 37748736 | tf_op jit(solution)/shard_map/slice | solution.py:96
  33.7 2.7 collective-permute-start
  37.9 8.3 %collective-permute-done = bf16[256,768]{1,0:T(8,128)(2,1)S(1)} collective-permute-done((bf16[256,768]{1,0:T(8,128)(2,1)S(1)}, bf16[256,768]{1,0:T(8,128)(2,1)S(1)}, u32[]{:S(2)}, u32[]{:S(2)}) %collective-permute-start) | collective-permute-done | bytes 393248 | tf_op jit(solution)/shard_map/ppermute | solution.py:53
  46.3 9.3 %collective-permute-done.1 = bf16[256,768]{1,0:T(8,128)(2,1)S(1)} collective-permute-done((bf16[256,768]{1,0:T(8,128)(2,1)S(1)}, bf16[256,768]{1,0:T(8,128)(2,1)S(1)}, u32[]{:S(2)}, u32[]{:S(2)}) %collective-permute-start.1) | collective-permute-done | bytes 393248 | tf_op jit(solution)/shard_map/ppermute | solution.py:53
  56.9 3.2 gather_fusion
  60.1 2.8 broadcast_select_fusion.1
  62.8 3.2 gather_fusion.1
  66.1 2.8 broadcast_select_fusion
  68.8 17.8 %fusion.3 = bf16[1024,6144]{1,0:T(8,128)(2,1)} fusion(bf16[1024,768]{1,0:T(8,128)(2,1)} %bitcast.104, f32[6144]{0:T(1024)S(1)} %broadcast_in_dim.64, pred[6144]{0:T(1024)(128)(4,1)S(1)} %fusion.30, pred[1024]{0:T(1024)(128)(4,1)S(1)} %fusion.35, bf16[768,1536]{1,0:T(8,128)(2,1)} %get-tuple-element.14, bf16[768,1536]{1,0:T(8,128)(2,1)} %get-tuple-element.15, ...), kind=kOutput, calls=%fused_computation.7 | convolution fusion | flops 9726590976 | bytes 23624704 | tf_op jit(solution)/shard_map/dot_general | solution.py:98
  86.9 17.9 %fusion.5 = bf16[1024,6144]{1,0:T(8,128)(2,1)} fusion(bf16[1024,768]{1,0:T(8,128)(2,1)} %bitcast.105, f32[6144]{0:T(1024)S(1)} %broadcast_in_dim.69, pred[6144]{0:T(1024)(128)(4,1)S(1)} %fusion.30, pred[1024]{0:T(1024)(128)(4,1)S(1)} %fusion.35, bf16[768,1536]{1,0:T(8,128)(2,1)} %get-tuple-element.18, bf16[768,1536]{1,0:T(8,128)(2,1)} %get-tuple-element.19, ...), kind=kOutput, calls=%fused_computation.9 | convolution fusion | flops 9726590976 | bytes 23624704 | tf_op jit(solution)/shard_map/dot_general | solution.py:98
  106.8 100.9 %reduce-scatter.4.cloned.1.call-done = bf16[1024,1536]{1,0:T(8,128)(2,1)} async-done(((bf16[1024,6144]{1,0:T(8,128)(2,1)}), bf16[1024,1536]{1,0:T(8,128)(2,1)}) %reduce-scatter.4.cloned.1.call-update) | async-done | bytes 3145744 | tf_op jit(solution)/shard_map/reduce_scatter | solution.py:101
  207.7 3.1 fusion.50
  212.2 2.4 collective-permute-start.4
  216.0 115.6 %reduce-scatter.6.cloned.1.call-done = bf16[1024,1536]{1,0:T(8,128)(2,1)} async-done(((bf16[1024,6144]{1,0:T(8,128)(2,1)}), bf16[1024,1536]{1,0:T(8,128)(2,1)}) %reduce-scatter.6.cloned.1.call-update) | async-done | bytes 3145744 | tf_op jit(solution)/shard_map/reduce_scatter | solution.py:101
  331.5 3.1 fusion.49
  336.1 2.4 collective-permute-start.8
  339.0 3.1 add_convert_fusion.1
  348.3 2.8 convolution_convert_fusion.1
  351.2 26.7 %collective-permute-done.7 = bf16[256,1536]{1,0:T(8,128)(2,1)} collective-permute-done((bf16[256,1536]{1,0:T(8,128)(2,1)}, bf16[256,1536]{1,0:T(8,128)(2,1)}, u32[]{:S(2)}, u32[]{:S(2)}) %collective-permute-start.7) | collective-permute-done | bytes 786464 | tf_op jit(solution)/shard_map/ppermute | solution.py:106
  377.9 20.7 %collective-permute-done.8 = bf16[256,1536]{1,0:T(8,128)(2,1)} collective-permute-done((bf16[256,1536]{1,0:T(8,128)(2,1)}, bf16[256,1536]{1,0:T(8,128)(2,1)}, u32[]{:S(2)}, u32[]{:S(2)}) %collective-permute-start.8) | collective-permute-done | bytes 786464 | tf_op jit(solution)/shard_map/ppermute | solution.py:106
  398.6 3.1 add_convert_fusion
  408.0 2.8 convolution_convert_fusion
  411.1 4.5 all-gather.6.cloned.1.call-done
  417.9 10.2 %fusion.21 = f32[2,1536,4,256]{3,1,2,0:T(8,128)} fusion(bf16[4,256,512,1]{2,1,0,3:T(8,128)(2,1)} %bitcast.106, bf16[2,1536,512]{2,1,0:T(8,128)(2,1)} %bitcast.97), kind=kOutput, calls=%fused_computation.26 | convolution fusion | flops 3221225472 | bytes 16777216 | tf_op jit(solution)/shard_map/tsd,ocd->tosc/dot_general | solution.py:115
  428.1 36.4 %all-gather.8.cloned.1.call-done = bf16[1024,512]{0,1:T(8,128)(2,1)} async-done(((bf16[256,512]{0,1:T(8,128)(2,1)}), bf16[1024,512]{0,1:T(8,128)(2,1)}) %all-gather.8.cloned.1.call-update) | async-done | bytes 1048592 | tf_op jit(solution)/shard_map/all_gather | solution.py:114
  466.7 9.4 %add_bitcast_fusion = f32[4,2,256,1536]{2,3,0,1:T(8,128)} fusion(f32[2,1536,4,256]{3,1,2,0:T(8,128)} %fusion.21, bf16[4,256,512,1]{2,1,0,3:T(8,128)(2,1)} %bitcast.96, bf16[2,1536,512]{2,1,0:T(8,128)(2,1)S(1)} %bitcast.95), kind=kOutput, calls=%fused_computation.10 | convolution fusion | flops 3224371200 | bytes 29360128 | tf_op jit(solution)/shard_map/tsd,ocd->tosc/dot_general | solution.py:115
  476.2 12.6 %copy.33 = f32[4,2,256,1536]{3,2,1,0:T(8,128)} copy(f32[4,2,256,1536]{2,3,0,1:T(8,128)} %add_bitcast_fusion) | data formatting | bytes 25165824 | tf_op jit(solution)/shard_map/add | solution.py:121
  489.4 90.2 %reduce-scatter.8.cloned.1.call-done = f32[1,256,1536]{2,1,0:T(8,128)} async-done(((f32[8,256,1536]{2,1,0:T(8,128)}), f32[1,256,1536]{2,1,0:T(8,128)}) %reduce-scatter.8.cloned.1.call-update) | async-done | bytes 1572880 | tf_op jit(solution)/shard_map/reduce_scatter | solution.py:123
  579.6 2.7 bitcast_add_fusion
  (55 shorter events, 30.3 us)
Async XLA Ops:
  6.5 25.6 %all-gather.4.cloned.1.call-start = ((), (), s32[]{:S(2)}) async-start(), calls=%async_computation.3 | async-start | bytes 2359296 | tf_op jit(solution)/shard_map/all_gather | solution.py:46
  7.3 5.0 copy-start
  7.3 200.4 %reduce-scatter.4.cloned.1.call-start = ((), (), s32[]{:S(2)}) async-start(), calls=%async_computation.4 | async-start | bytes 15728640 | tf_op jit(solution)/shard_map/reduce_scatter | solution.py:101
  33.7 12.6 %collective-permute-start = (bf16[256,768]{1,0:T(8,128)(2,1)S(1)}, bf16[256,768]{1,0:T(8,128)(2,1)S(1)}, u32[]{:S(2)}, u32[]{:S(2)}) collective-permute-start(bf16[256,768]{1,0:T(8,128)(2,1)S(1)} %get-tuple-element.31), channel_id=1, source_target_pairs={{0,8},{8,0},{16,24},{24,16},{1,9},{9,1},{17,25},{25,17},{2,10},{10... | collective-permute-start | bytes 1179656 | tf_op jit(solution)/shard_map/ppermute | solution.py:53
  36.3 19.2 %collective-permute-start.1 = (bf16[256,768]{1,0:T(8,128)(2,1)S(1)}, bf16[256,768]{1,0:T(8,128)(2,1)S(1)}, u32[]{:S(2)}, u32[]{:S(2)}) collective-permute-start(bf16[256,768]{1,0:T(8,128)(2,1)S(1)} %get-tuple-element.30), channel_id=1, source_target_pairs={{0,16},{8,24},{16,0},{24,8},{1,17},{9,25},{17,1},{25,9},{2,18},{10... | collective-permute-start | bytes 1179656 | tf_op jit(solution)/shard_map/ppermute | solution.py:53
  37.9 17.6 %collective-permute-start.2 = (bf16[256,768]{1,0:T(8,128)(2,1)S(1)}, bf16[256,768]{1,0:T(8,128)(2,1)S(1)}, u32[]{:S(2)}, u32[]{:S(2)}) collective-permute-start(bf16[256,768]{1,0:T(8,128)(2,1)S(1)} %get-tuple-element.29), channel_id=1, source_target_pairs={{0,24},{8,16},{16,8},{24,0},{1,25},{9,17},{17,9},{25,1},{2,26},{10... | collective-permute-start | bytes 1179656 | tf_op jit(solution)/shard_map/ppermute | solution.py:53
  86.6 244.9 %reduce-scatter.6.cloned.1.call-start = ((), (), s32[]{:S(2)}) async-start(), calls=%async_computation.6 | async-start | bytes 15728640 | tf_op jit(solution)/shard_map/reduce_scatter | solution.py:101
  104.8 310.8 %all-gather.6.cloned.1.call-start = ((), (), s32[]{:S(2)}) async-start(), calls=%async_computation.5 | async-start | bytes 1310720 | tf_op jit(solution)/shard_map/all_gather | solution.py:114
  104.8 110.3 %collective-permute-start.6 = (s32[1]{0:T(128)}, s32[1]{0:T(128)}, u32[]{:S(2)}, u32[]{:S(2)}) collective-permute-start(s32[1]{0:T(128)} %param.9), channel_id=1, source_target_pairs={{0,0},{2,8},{4,16},{6,24},{8,2},{10,10},{12,18},{14,26},{16,4},{18... | collective-permute-start | bytes 20 | tf_op jit(solution)/shard_map/ppermute | solution.py:73
  210.8 127.7 %collective-permute-start.3 = (bf16[256,1536]{1,0:T(8,128)(2,1)}, bf16[256,1536]{1,0:T(8,128)(2,1)}, u32[]{:S(2)}, u32[]{:S(2)}) collective-permute-start(bf16[256,1536]{1,0:T(8,128)(2,1)} %get-tuple-element.25), channel_id=1, source_target_pairs={{0,2},{2,0},{4,6},{6,4},{1,3},{3,1},{5,7},{7,5},{8,10},{10,8},{12,... | collective-permute-start | bytes 2359304 | tf_op jit(solution)/shard_map/ppermute | solution.py:106
  212.2 126.8 %collective-permute-start.4 = (bf16[256,1536]{1,0:T(8,128)(2,1)}, bf16[256,1536]{1,0:T(8,128)(2,1)}, u32[]{:S(2)}, u32[]{:S(2)}) collective-permute-start(bf16[256,1536]{1,0:T(8,128)(2,1)} %get-tuple-element.27), channel_id=1, source_target_pairs={{0,4},{2,6},{4,0},{6,2},{1,5},{3,7},{5,1},{7,3},{8,12},{10,14},{12... | collective-permute-start | bytes 2359304 | tf_op jit(solution)/shard_map/ppermute | solution.py:106
  214.6 124.4 %collective-permute-start.5 = (bf16[256,1536]{1,0:T(8,128)(2,1)}, bf16[256,1536]{1,0:T(8,128)(2,1)}, u32[]{:S(2)}, u32[]{:S(2)}) collective-permute-start(bf16[256,1536]{1,0:T(8,128)(2,1)} %get-tuple-element.26), channel_id=1, source_target_pairs={{0,6},{2,4},{4,2},{6,0},{1,7},{3,5},{5,3},{7,1},{8,14},{10,12},{12... | collective-permute-start | bytes 2359304 | tf_op jit(solution)/shard_map/ppermute | solution.py:106
  334.6 43.3 %collective-permute-start.7 = (bf16[256,1536]{1,0:T(8,128)(2,1)}, bf16[256,1536]{1,0:T(8,128)(2,1)}, u32[]{:S(2)}, u32[]{:S(2)}) collective-permute-start(bf16[256,1536]{1,0:T(8,128)(2,1)} %get-tuple-element.22), channel_id=1, source_target_pairs={{0,2},{2,0},{4,6},{6,4},{1,3},{3,1},{5,7},{7,5},{8,10},{10,8},{12,... | collective-permute-start | bytes 2359304 | tf_op jit(solution)/shard_map/ppermute | solution.py:106
  336.1 62.5 %collective-permute-start.8 = (bf16[256,1536]{1,0:T(8,128)(2,1)}, bf16[256,1536]{1,0:T(8,128)(2,1)}, u32[]{:S(2)}, u32[]{:S(2)}) collective-permute-start(bf16[256,1536]{1,0:T(8,128)(2,1)} %get-tuple-element.24), channel_id=1, source_target_pairs={{0,4},{2,6},{4,0},{6,2},{1,5},{3,7},{5,1},{7,3},{8,12},{10,14},{12... | collective-permute-start | bytes 2359304 | tf_op jit(solution)/shard_map/ppermute | solution.py:106
  338.5 60.1 %collective-permute-start.9 = (bf16[256,1536]{1,0:T(8,128)(2,1)}, bf16[256,1536]{1,0:T(8,128)(2,1)}, u32[]{:S(2)}, u32[]{:S(2)}) collective-permute-start(bf16[256,1536]{1,0:T(8,128)(2,1)} %get-tuple-element.23), channel_id=1, source_target_pairs={{0,6},{2,4},{4,2},{6,0},{1,7},{3,5},{5,3},{7,1},{8,14},{10,12},{12... | collective-permute-start | bytes 2359304 | tf_op jit(solution)/shard_map/ppermute | solution.py:106
  351.1 113.3 %all-gather.8.cloned.1.call-start = ((), (), s32[]{:S(2)}) async-start(), calls=%async_computation.7 | async-start | bytes 1310720 | tf_op jit(solution)/shard_map/all_gather | solution.py:114
  410.8 168.8 %reduce-scatter.8.cloned.1.call-start = ((), (), s32[]{:S(2)}) async-start(), calls=%async_computation.8 | async-start | bytes 14155776 | tf_op jit(solution)/shard_map/reduce_scatter | solution.py:123
  488.8 0.7 copy-start.1
Sparse Core Ops, SparseCore 0:
  8.9 12.4 all-gather.3
  86.7 120.8 reduce-scatter.3
  210.8 120.7 reduce-scatter.5
  351.2 64.3 all-gather.5
  417.0 47.4 all-gather.7
  488.9 90.6 reduce-scatter.7

commit v17 on v16

--- a/solution.py
+++ b/solution.py
@@ -89,7 +89,6 @@
         jnp.transpose(w_out[h * w_rows:(h + 1) * w_rows].reshape(w_rows, n_out, -1), (1, 2, 0))
         for h in range(n_streams)
     ]
-    w_out_t, panel = lax.optimization_barrier((w_out_t, panel))
     terms = None
     for h in range(n_streams):
         w_h = jnp.concatenate(
@@ -99,6 +98,8 @@
         bias_row = jnp.tile(bias[h * piece:(h + 1) * piece], n_tok)[None, :]
         part = (value + jnp.where(here, bias_row, 0.0)).astype(jnp.bfloat16)
         slab_sum = lax.psum_scatter(part, "tok", scatter_dimension=1, tiled=True)
+        if h == 0:
+            w_out_t, slab_sum = lax.optimization_barrier((w_out_t, slab_sum))
         if by_xor:
             blocks = slab_sum.reshape(n_blocks, rows_dev, piece)
             got = {}

time: 590 us -> 571 us (0.968)
  waiting for transfers between devices: 413 us -> 402 us
    reduce_scatter x2, waiting for transfers between devices: 216 us -> 205 us  [shards(): slab_sum = lax.psum_scatter(part, 'tok', scatter_dimension=1, tiled=True)]
where the time goes in v17:
time: 571 us
  waiting for transfers between devices  402 us (70%)
  matrix products  68.1 us (12%)
  local copies, waits for them, and re-layouts  59.6 us (10%)
  starting transfers between devices  15.8 us (3%)
  between operations  13.6 us (2%)
  other arithmetic  11.5 us (2%)
    reduce_scatter x2, waiting for transfers between devices, shards(): slab_sum = lax.psum_scatter(part, 'tok', scatter_dimension=1, tiled=True)  205 us
    reduce_scatter x1, waiting for transfers between devices, shards(): lax.psum_scatter(terms, ('tok', 'out'), scatter_dimension=0, tiled=True)  90.2 us
    ppermute x6, waiting for transfers between devices, shards(): got[s] = lax.ppermute(blocks[s], 'ka', [(i, i ^ s) for i in range(n_ka)])  47.4 us
    all_gather x2, waiting for transfers between devices, shards(): head_group = lax.all_gather(context, 'ka', axis=0, tiled=True)  40.9 us
    dot_general x2, matrix products, shards(): value = jnp.dot(panel, w_h, preferred_element_type=jnp.float32)  35 us
    dot_general x2, matrix products, shards(): jnp.einsum('tsd,ocd->tosc', head_group.reshape(n_tok, tokens // n_tok, -1...  19.5 us
    ppermute x3, waiting for transfers between devices, shards(): pieces[s] = lax.ppermute(owed, 'tok', [(i, i ^ s) for i in range(n_tok)])  17.4 us
    slice x1, local copies, waits for them, and re-layouts, shards(): w_qkv[:, c * width + h * piece:c * width + (h + 1) * piece]  13.5 us
  transfers between devices with their start and end apart: 16, of which 9 were waited for; matrix products, arithmetic and copies ran while one was open for 15% of the time, Pallas kernels for 0%

profile of v17, /device:TPU:0, one launch (start us, length us, event | category | flops | bytes accessed | tf_op | source)
XLA Modules:
  0.0 570.5 jit_solution(1344309124722890340)
XLA Ops:
  8.2 13.5 %fusion.47 = (bf16[768,1536]{1,0:T(8,128)(2,1)}, bf16[768,1536]{1,0:T(8,128)(2,1)}, bf16[768,1536]{1,0:T(8,128)(2,1)}, bf16[768,1536]{1,0:T(8,128)(2,1)}, bf16[7...) fusion(bf16[768,12288]{1,0:T(8,128)(2,1)} %param.10), kind=kLoop, calls=%fused_computation.90 | loop fusion | bytes 37748736 | tf_op jit(solution)/shard_map/slice | solution.py:95
  23.2 3.0 collective-permute-start
  27.8 8.4 %collective-permute-done = bf16[256,768]{1,0:T(8,128)(2,1)S(1)} collective-permute-done((bf16[256,768]{1,0:T(8,128)(2,1)S(1)}, bf16[256,768]{1,0:T(8,128)(2,1)S(1)}, u32[]{:S(2)}, u32[]{:S(2)}) %collective-permute-start) | collective-permute-done | bytes 393248 | tf_op jit(solution)/shard_map/ppermute | solution.py:53
  36.2 9.1 %collective-permute-done.1 = bf16[256,768]{1,0:T(8,128)(2,1)S(1)} collective-permute-done((bf16[256,768]{1,0:T(8,128)(2,1)S(1)}, bf16[256,768]{1,0:T(8,128)(2,1)S(1)}, u32[]{:S(2)}, u32[]{:S(2)}) %collective-permute-start.1) | collective-permute-done | bytes 393248 | tf_op jit(solution)/shard_map/ppermute | solution.py:53
  49.8 17.9 %fusion.3 = bf16[1024,6144]{1,0:T(8,128)(2,1)} fusion(bf16[1024,768]{1,0:T(8,128)(2,1)S(1)} %bitcast.104, f32[6144]{0:T(1024)S(1)} %broadcast_in_dim.64, pred[6144]{0:T(1024)(128)(4,1)S(1)} %fusion.30, pred[1024]{0:T(1024)(128)(4,1)S(1)} %fusion.35, bf16[768,1536]{1,0:T(8,128)(2,1)} %get-tuple-element.14, bf16[768,1536]{1,0:T(8,128)(2,1)} %get-tuple-element.15, ...), kind=kOutput, calls=%fused_computation.7 | convolution fusion | flops 9726590976 | bytes 23624704 | tf_op jit(solution)/shard_map/dot_general | solution.py:97
  69.4 17.1 %fusion.5 = bf16[1024,6144]{1,0:T(8,128)(2,1)} fusion(bf16[1024,768]{1,0:T(8,128)(2,1)} %bitcast.105, f32[6144]{0:T(1024)S(1)} %broadcast_in_dim.69, pred[6144]{0:T(1024)(128)(4,1)S(1)} %fusion.30, pred[1024]{0:T(1024)(128)(4,1)S(1)} %fusion.35, bf16[768,1536]{1,0:T(8,128)(2,1)} %get-tuple-element.18, bf16[768,1536]{1,0:T(8,128)(2,1)} %get-tuple-element.19, ...), kind=kOutput, calls=%fused_computation.9 | convolution fusion | flops 9726590976 | bytes 23624704 | tf_op jit(solution)/shard_map/dot_general | solution.py:97
  88.4 5.0 fusion.48
  93.4 2.9 copy.38
  96.3 3.2 copy.39
  99.5 89.4 %reduce-scatter.4.cloned.1.call-done = bf16[1024,1536]{1,0:T(8,128)(2,1)} async-done(((bf16[1024,6144]{1,0:T(8,128)(2,1)}), bf16[1024,1536]{1,0:T(8,128)(2,1)}) %reduce-scatter.4.cloned.1.call-update) | async-done | bytes 3145744 | tf_op jit(solution)/shard_map/reduce_scatter | solution.py:100
  188.9 3.1 fusion.50
  193.5 2.4 collective-permute-start.4
  197.1 115.6 %reduce-scatter.6.cloned.1.call-done = bf16[1024,1536]{1,0:T(8,128)(2,1)} async-done(((bf16[1024,6144]{1,0:T(8,128)(2,1)}), bf16[1024,1536]{1,0:T(8,128)(2,1)}) %reduce-scatter.6.cloned.1.call-update) | async-done | bytes 3145744 | tf_op jit(solution)/shard_map/reduce_scatter | solution.py:100
  312.8 3.1 fusion.49
  317.4 2.4 collective-permute-start.8
  320.3 3.1 add_convert_fusion.1
  323.4 2.3 copy.21
  327.2 2.4 fusion.28
  329.6 2.8 convolution_convert_fusion.1
  332.5 26.6 %collective-permute-done.7 = bf16[256,1536]{1,0:T(8,128)(2,1)} collective-permute-done((bf16[256,1536]{1,0:T(8,128)(2,1)}, bf16[256,1536]{1,0:T(8,128)(2,1)}, u32[]{:S(2)}, u32[]{:S(2)}) %collective-permute-start.7) | collective-permute-done | bytes 786464 | tf_op jit(solution)/shard_map/ppermute | solution.py:107
  359.1 20.7 %collective-permute-done.8 = bf16[256,1536]{1,0:T(8,128)(2,1)} collective-permute-done((bf16[256,1536]{1,0:T(8,128)(2,1)}, bf16[256,1536]{1,0:T(8,128)(2,1)}, u32[]{:S(2)}, u32[]{:S(2)}) %collective-permute-start.8) | collective-permute-done | bytes 786464 | tf_op jit(solution)/shard_map/ppermute | solution.py:107
  379.9 3.1 add_convert_fusion
  383.0 2.3 copy.27
  386.9 2.4 fusion.27
  389.3 2.9 convolution_convert_fusion
  392.4 4.4 all-gather.6.cloned.1.call-done
  399.1 10.2 %fusion.21 = f32[2,1536,4,256]{3,1,2,0:T(8,128)} fusion(bf16[4,256,512,1]{2,1,0,3:T(8,128)(2,1)} %bitcast.106, bf16[2,1536,512]{2,1,0:T(8,128)(2,1)} %bitcast.97), kind=kOutput, calls=%fused_computation.26 | convolution fusion | flops 3221225472 | bytes 16777216 | tf_op jit(solution)/shard_map/tsd,ocd->tosc/dot_general | solution.py:116
  409.3 36.5 %all-gather.8.cloned.1.call-done = bf16[1024,512]{0,1:T(8,128)(2,1)} async-done(((bf16[256,512]{0,1:T(8,128)(2,1)}), bf16[1024,512]{0,1:T(8,128)(2,1)}) %all-gather.8.cloned.1.call-update) | async-done | bytes 1048592 | tf_op jit(solution)/shard_map/all_gather | solution.py:115
  448.1 9.4 %add_bitcast_fusion = f32[4,2,256,1536]{2,3,0,1:T(8,128)} fusion(f32[2,1536,4,256]{3,1,2,0:T(8,128)} %fusion.21, bf16[4,256,512,1]{2,1,0,3:T(8,128)(2,1)} %bitcast.96, bf16[2,1536,512]{2,1,0:T(8,128)(2,1)S(1)} %bitcast.95), kind=kOutput, calls=%fused_computation.10 | convolution fusion | flops 3224371200 | bytes 29360128 | tf_op jit(solution)/shard_map/tsd,ocd->tosc/dot_general | solution.py:116
  457.5 12.6 %copy.33 = f32[4,2,256,1536]{3,2,1,0:T(8,128)} copy(f32[4,2,256,1536]{2,3,0,1:T(8,128)} %add_bitcast_fusion) | data formatting | bytes 25165824 | tf_op jit(solution)/shard_map/add | solution.py:122
  470.7 90.2 %reduce-scatter.8.cloned.1.call-done = f32[1,256,1536]{2,1,0:T(8,128)} async-done(((f32[8,256,1536]{2,1,0:T(8,128)}), f32[1,256,1536]{2,1,0:T(8,128)}) %reduce-scatter.8.cloned.1.call-update) | async-done | bytes 1572880 | tf_op jit(solution)/shard_map/reduce_scatter | solution.py:124
  560.9 2.7 bitcast_add_fusion
  (57 shorter events, 26.1 us)
Async XLA Ops:
  6.5 15.2 %all-gather.4.cloned.1.call-start = ((), (), s32[]{:S(2)}) async-start(), calls=%async_computation.3 | async-start | bytes 2359296 | tf_op jit(solution)/shard_map/all_gather | solution.py:46
  7.3 181.6 %reduce-scatter.4.cloned.1.call-start = ((), (), s32[]{:S(2)}) async-start(), calls=%async_computation.4 | async-start | bytes 15728640 | tf_op jit(solution)/shard_map/reduce_scatter | solution.py:100
  23.2 12.9 %collective-permute-start = (bf16[256,768]{1,0:T(8,128)(2,1)S(1)}, bf16[256,768]{1,0:T(8,128)(2,1)S(1)}, u32[]{:S(2)}, u32[]{:S(2)}) collective-permute-start(bf16[256,768]{1,0:T(8,128)(2,1)S(1)} %get-tuple-element.31), channel_id=1, source_target_pairs={{0,8},{8,0},{16,24},{24,16},{1,9},{9,1},{17,25},{25,17},{2,10},{10... | collective-permute-start | bytes 1179656 | tf_op jit(solution)/shard_map/ppermute | solution.py:53
  26.2 19.0 %collective-permute-start.1 = (bf16[256,768]{1,0:T(8,128)(2,1)S(1)}, bf16[256,768]{1,0:T(8,128)(2,1)S(1)}, u32[]{:S(2)}, u32[]{:S(2)}) collective-permute-start(bf16[256,768]{1,0:T(8,128)(2,1)S(1)} %get-tuple-element.30), channel_id=1, source_target_pairs={{0,16},{8,24},{16,0},{24,8},{1,17},{9,25},{17,1},{25,9},{2,18},{10... | collective-permute-start | bytes 1179656 | tf_op jit(solution)/shard_map/ppermute | solution.py:53
  27.7 17.5 %collective-permute-start.2 = (bf16[256,768]{1,0:T(8,128)(2,1)S(1)}, bf16[256,768]{1,0:T(8,128)(2,1)S(1)}, u32[]{:S(2)}, u32[]{:S(2)}) collective-permute-start(bf16[256,768]{1,0:T(8,128)(2,1)S(1)} %get-tuple-element.29), channel_id=1, source_target_pairs={{0,24},{8,16},{16,8},{24,0},{1,25},{9,17},{17,9},{25,1},{2,26},{10... | collective-permute-start | bytes 1179656 | tf_op jit(solution)/shard_map/ppermute | solution.py:53
  49.7 17.9 %copy-start.1 = (bf16[4,256,768]{2,1,0:T(8,128)(2,1)}, bf16[4,256,768]{2,1,0:T(8,128)(2,1)S(1)}, u32[]{:S(2)}) copy-start(bf16[4,256,768]{2,1,0:T(8,128)(2,1)S(1)} %broadcast_select_fusion) | copy-start | bytes 4718596
  67.7 1.7 copy-start
  67.7 245.1 %reduce-scatter.6.cloned.1.call-start = ((), (), s32[]{:S(2)}) async-start(), calls=%async_computation.6 | async-start | bytes 15728640 | tf_op jit(solution)/shard_map/reduce_scatter | solution.py:100
  86.4 310.4 %all-gather.6.cloned.1.call-start = ((), (), s32[]{:S(2)}) async-start(), calls=%async_computation.5 | async-start | bytes 1310720 | tf_op jit(solution)/shard_map/all_gather | solution.py:115
  86.5 109.9 %collective-permute-start.6 = (s32[1]{0:T(128)}, s32[1]{0:T(128)}, u32[]{:S(2)}, u32[]{:S(2)}) collective-permute-start(s32[1]{0:T(128)} %param.9), channel_id=1, source_target_pairs={{0,0},{2,8},{4,16},{6,24},{8,2},{10,10},{12,18},{14,26},{16,4},{18... | collective-permute-start | bytes 20 | tf_op jit(solution)/shard_map/ppermute | solution.py:73
  192.0 127.8 %collective-permute-start.3 = (bf16[256,1536]{1,0:T(8,128)(2,1)}, bf16[256,1536]{1,0:T(8,128)(2,1)}, u32[]{:S(2)}, u32[]{:S(2)}) collective-permute-start(bf16[256,1536]{1,0:T(8,128)(2,1)} %get-tuple-element.25), channel_id=1, source_target_pairs={{0,2},{2,0},{4,6},{6,4},{1,3},{3,1},{5,7},{7,5},{8,10},{10,8},{12,... | collective-permute-start | bytes 2359304 | tf_op jit(solution)/shard_map/ppermute | solution.py:107
  193.5 126.8 %collective-permute-start.4 = (bf16[256,1536]{1,0:T(8,128)(2,1)}, bf16[256,1536]{1,0:T(8,128)(2,1)}, u32[]{:S(2)}, u32[]{:S(2)}) collective-permute-start(bf16[256,1536]{1,0:T(8,128)(2,1)} %get-tuple-element.27), channel_id=1, source_target_pairs={{0,4},{2,6},{4,0},{6,2},{1,5},{3,7},{5,1},{7,3},{8,12},{10,14},{12... | collective-permute-start | bytes 2359304 | tf_op jit(solution)/shard_map/ppermute | solution.py:107
  195.9 124.4 %collective-permute-start.5 = (bf16[256,1536]{1,0:T(8,128)(2,1)}, bf16[256,1536]{1,0:T(8,128)(2,1)}, u32[]{:S(2)}, u32[]{:S(2)}) collective-permute-start(bf16[256,1536]{1,0:T(8,128)(2,1)} %get-tuple-element.26), channel_id=1, source_target_pairs={{0,6},{2,4},{4,2},{6,0},{1,7},{3,5},{5,3},{7,1},{8,14},{10,12},{12... | collective-permute-start | bytes 2359304 | tf_op jit(solution)/shard_map/ppermute | solution.py:107
  315.9 43.3 %collective-permute-start.7 = (bf16[256,1536]{1,0:T(8,128)(2,1)}, bf16[256,1536]{1,0:T(8,128)(2,1)}, u32[]{:S(2)}, u32[]{:S(2)}) collective-permute-start(bf16[256,1536]{1,0:T(8,128)(2,1)} %get-tuple-element.22), channel_id=1, source_target_pairs={{0,2},{2,0},{4,6},{6,4},{1,3},{3,1},{5,7},{7,5},{8,10},{10,8},{12,... | collective-permute-start | bytes 2359304 | tf_op jit(solution)/shard_map/ppermute | solution.py:107
  317.4 62.5 %collective-permute-start.8 = (bf16[256,1536]{1,0:T(8,128)(2,1)}, bf16[256,1536]{1,0:T(8,128)(2,1)}, u32[]{:S(2)}, u32[]{:S(2)}) collective-permute-start(bf16[256,1536]{1,0:T(8,128)(2,1)} %get-tuple-element.24), channel_id=1, source_target_pairs={{0,4},{2,6},{4,0},{6,2},{1,5},{3,7},{5,1},{7,3},{8,12},{10,14},{12... | collective-permute-start | bytes 2359304 | tf_op jit(solution)/shard_map/ppermute | solution.py:107
  319.8 60.1 %collective-permute-start.9 = (bf16[256,1536]{1,0:T(8,128)(2,1)}, bf16[256,1536]{1,0:T(8,128)(2,1)}, u32[]{:S(2)}, u32[]{:S(2)}) collective-permute-start(bf16[256,1536]{1,0:T(8,128)(2,1)} %get-tuple-element.23), channel_id=1, source_target_pairs={{0,6},{2,4},{4,2},{6,0},{1,7},{3,5},{5,3},{7,1},{8,14},{10,12},{12... | collective-permute-start | bytes 2359304 | tf_op jit(solution)/shard_map/ppermute | solution.py:107
  332.5 113.3 %all-gather.8.cloned.1.call-start = ((), (), s32[]{:S(2)}) async-start(), calls=%async_computation.7 | async-start | bytes 1310720 | tf_op jit(solution)/shard_map/all_gather | solution.py:115
  392.2 168.8 %reduce-scatter.8.cloned.1.call-start = ((), (), s32[]{:S(2)}) async-start(), calls=%async_computation.8 | async-start | bytes 14155776 | tf_op jit(solution)/shard_map/reduce_scatter | solution.py:124
  470.1 0.7 copy-start.2
Sparse Core Ops, SparseCore 0:
  8.9 12.4 all-gather.3
  67.8 121.0 reduce-scatter.3
  192.0 120.7 reduce-scatter.5
  332.6 64.2 all-gather.5
  398.3 47.4 all-gather.7
  470.2 90.6 reduce-scatter.7

commit v18 on v14

--- a/solution.py
+++ b/solution.py
@@ -115,8 +115,10 @@
         )
         terms = term if terms is None else terms + term
     terms = terms.reshape(n_tok * n_out, tokens // n_tok, -1)
+    mine = lax.broadcasted_iota(jnp.int32, (n_tok * n_out, 1, 1), 0) == t * n_out + lax.axis_index("out")
+    terms = terms + jnp.where(mine, b_out.astype(jnp.float32)[None, None, :], 0.0)
     summed = lax.psum_scatter(terms, ("tok", "out"), scatter_dimension=0, tiled=True)
-    return summed[0] + b_out.astype(jnp.float32)
+    return summed[0]
 
 
 def solution(mesh):

time: 551 us -> 559 us (1.015)
  other arithmetic: 9.85 us -> 18.4 us
    add x1, other arithmetic: 2.74 us -> 11.2 us  [shards(): terms + jnp.where(mine, b_out.astype(jnp.float32)[None, None, :], 0.0)]
  transfers between devices with their start and end apart: 16 -> 16, of which waited for: 8 -> 8; matrix products, arithmetic and copies ran while one was open for 13% -> 12% of each run, Pallas kernels for 0% -> 0%
where the time goes in v18:
time: 559 us
  waiting for transfers between devices  411 us (74%)
  matrix products  58.8 us (11%)
  local copies, waits for them, and re-layouts  40.7 us (7%)
  other arithmetic  18.4 us (3%)
  starting transfers between devices  15.9 us (3%)
  between operations  13.7 us (2%)
    reduce_scatter x2, waiting for transfers between devices, shards(): slab_sum = lax.psum_scatter(part, 'tok', scatter_dimension=1, tiled=True)  217 us
    reduce_scatter x1, waiting for transfers between devices, shards(): lax.psum_scatter(terms, ('tok', 'out'), scatter_dimension=0, tiled=True)  90.8 us
    ppermute x6, waiting for transfers between devices, shards(): got[s] = lax.ppermute(blocks[s], 'ka', [(i, i ^ s) for i in range(n_ka)])  56.1 us
    dot_general x2, matrix products, shards(): value = jnp.dot(panel, w_h, preferred_element_type=jnp.float32)  35 us
    all_gather x2, waiting for transfers between devices, shards(): head_group = lax.all_gather(context, 'ka', axis=0, tiled=True)  28.7 us
    dot_general x2, matrix products, shards(): jnp.einsum('tsd,doc->tosc', head_group.reshape(n_tok, tokens // n_tok, -1...  19.7 us
    ppermute x3, waiting for transfers between devices, shards(): pieces[s] = lax.ppermute(owed, 'tok', [(i, i ^ s) for i in range(n_tok)])  17.4 us
    slice x1, local copies, waits for them, and re-layouts, shards(): w_qkv[:, c * width + h * piece:c * width + (h + 1) * piece]  13.5 us
  transfers between devices with their start and end apart: 16, of which 8 were waited for; matrix products, arithmetic and copies ran while one was open for 12% of the time, Pallas kernels for 0%

profile of v18, /device:TPU:0, one launch (start us, length us, event | category | flops | bytes accessed | tf_op | source)
XLA Modules:
  0.0 558.8 jit_solution(1742946731880626699)
XLA Ops:
  8.2 13.5 %fusion.44 = (bf16[768,1536]{1,0:T(8,128)(2,1)}, bf16[768,1536]{1,0:T(8,128)(2,1)}, bf16[768,1536]{1,0:T(8,128)(2,1)}, bf16[768,1536]{1,0:T(8,128)(2,1)}, bf16[7...) fusion(bf16[768,12288]{1,0:T(8,128)(2,1)} %param.10), kind=kLoop, calls=%fused_computation.89 | loop fusion | bytes 37748736 | tf_op jit(solution)/shard_map/slice | solution.py:91
  21.7 1.5 dynamic-slice_bitcast_fusion
  23.2 3.0 collective-permute-start
  26.2 1.5 collective-permute-start.1
  27.8 8.4 %collective-permute-done = bf16[256,768]{1,0:T(8,128)(2,1)S(1)} collective-permute-done((bf16[256,768]{1,0:T(8,128)(2,1)S(1)}, bf16[256,768]{1,0:T(8,128)(2,1)S(1)}, u32[]{:S(2)}, u32[]{:S(2)}) %collective-permute-start) | collective-permute-done | bytes 393248 | tf_op jit(solution)/shard_map/ppermute | solution.py:53
  36.2 9.0 %collective-permute-done.1 = bf16[256,768]{1,0:T(8,128)(2,1)S(1)} collective-permute-done((bf16[256,768]{1,0:T(8,128)(2,1)S(1)}, bf16[256,768]{1,0:T(8,128)(2,1)S(1)}, u32[]{:S(2)}, u32[]{:S(2)}) %collective-permute-start.1) | collective-permute-done | bytes 393248 | tf_op jit(solution)/shard_map/ppermute | solution.py:53
  47.4 2.1 gather_fusion.1
  49.7 17.9 %fusion.3 = bf16[1024,6144]{1,0:T(8,128)(2,1)} fusion(bf16[1024,768]{1,0:T(8,128)(2,1)S(1)} %bitcast.99, f32[6144]{0:T(1024)S(1)} %broadcast_in_dim.84, pred[6144]{0:T(1024)(128)(4,1)S(1)} %fusion.27, pred[1024]{0:T(1024)(128)(4,1)S(1)} %fusion.32, bf16[768,1536]{1,0:T(8,128)(2,1)} %get-tuple-element.8, bf16[768,1536]{1,0:T(8,128)(2,1)} %get-tuple-element.9, ...), kind=kOutput, calls=%fused_computation.7 | convolution fusion | flops 9726590976 | bytes 23624704 | tf_op jit(solution)/shard_map/dot_general | solution.py:93
  69.3 17.1 %fusion.5 = bf16[1024,6144]{1,0:T(8,128)(2,1)} fusion(bf16[1024,768]{1,0:T(8,128)(2,1)} %bitcast.100, f32[6144]{0:T(1024)S(1)} %broadcast_in_dim.89, pred[6144]{0:T(1024)(128)(4,1)S(1)} %fusion.27, pred[1024]{0:T(1024)(128)(4,1)S(1)} %fusion.32, bf16[768,1536]{1,0:T(8,128)(2,1)} %get-tuple-element.12, bf16[768,1536]{1,0:T(8,128)(2,1)} %get-tuple-element.13, ...), kind=kOutput, calls=%fused_computation.9 | convolution fusion | flops 9726590976 | bytes 23624704 | tf_op jit(solution)/shard_map/dot_general | solution.py:93
  86.5 1.9 collective-permute-start.6
  88.4 100.6 %reduce-scatter.4.cloned.1.call-done = bf16[1024,1536]{1,0:T(8,128)(2,1)} async-done(((bf16[1024,6144]{1,0:T(8,128)(2,1)}), bf16[1024,1536]{1,0:T(8,128)(2,1)}) %reduce-scatter.4.cloned.1.call-update) | async-done | bytes 3145744 | tf_op jit(solution)/shard_map/reduce_scatter | solution.py:96
  188.9 1.8 fusion.47
  190.7 1.5 collective-permute-start.3
  192.2 2.4 collective-permute-start.4
  196.0 116.8 %reduce-scatter.6.cloned.1.call-done = bf16[1024,1536]{1,0:T(8,128)(2,1)} async-done(((bf16[1024,6144]{1,0:T(8,128)(2,1)}), bf16[1024,1536]{1,0:T(8,128)(2,1)}) %reduce-scatter.6.cloned.1.call-update) | async-done | bytes 3145744 | tf_op jit(solution)/shard_map/reduce_scatter | solution.py:96
  312.8 3.0 fusion.46
  315.8 1.5 collective-permute-start.7
  317.2 2.4 collective-permute-start.8
  320.2 2.2 add_convert_fusion.1
  324.8 38.2 %collective-permute-done.7 = bf16[256,1536]{1,0:T(8,128)(2,1)} collective-permute-done((bf16[256,1536]{1,0:T(8,128)(2,1)}, bf16[256,1536]{1,0:T(8,128)(2,1)}, u32[]{:S(2)}, u32[]{:S(2)}) %collective-permute-start.7) | collective-permute-done | bytes 786464 | tf_op jit(solution)/shard_map/ppermute | solution.py:101
  362.9 18.0 %collective-permute-done.8 = bf16[256,1536]{1,0:T(8,128)(2,1)} collective-permute-done((bf16[256,1536]{1,0:T(8,128)(2,1)}, bf16[256,1536]{1,0:T(8,128)(2,1)}, u32[]{:S(2)}, u32[]{:S(2)}) %collective-permute-start.8) | collective-permute-done | bytes 786464 | tf_op jit(solution)/shard_map/ppermute | solution.py:101
  380.9 2.3 add_convert_fusion
  385.8 4.9 fusion.45
  390.7 2.8 copy.44
  393.5 3.2 copy.48
  396.8 2.3 copy.22
  399.1 10.2 %fusion.51 = f32[4,256,2,1536]{3,1,2,0:T(8,128)} fusion(bf16[4,256,512,1]{2,1,3,0:T(8,128)(2,1)} %bitcast.101, bf16[512,2,1536,1]{0,2,1,3:T(8,128)(2,1)} %bitcast.92), kind=kOutput, calls=%fused_computation.96 | convolution fusion | flops 3221225472 | bytes 16777216 | tf_op jit(solution)/shard_map/tsd,doc->tosc/dot_general | solution.py:110
  409.3 28.7 %all-gather.8.cloned.1.call-done = bf16[1024,512]{0,1:T(8,128)(2,1)} async-done(((bf16[256,512]{0,1:T(8,128)(2,1)}), bf16[1024,512]{0,1:T(8,128)(2,1)}) %all-gather.8.cloned.1.call-update) | async-done | bytes 1048592 | tf_op jit(solution)/shard_map/all_gather | solution.py:109
  438.0 2.3 copy.30
  440.3 9.5 %convolution_add_fusion = f32[4,256,2,1536]{3,1,2,0:T(8,128)} fusion(f32[4,256,2,1536]{3,1,2,0:T(8,128)} %fusion.51, bf16[4,256,512,1]{2,1,3,0:T(8,128)(2,1)} %bitcast.91, bf16[512,2,1536,1]{0,2,1,3:T(8,128)(2,1)S(1)} %bitcast.90), kind=kOutput, calls=%fused_computation.25 | convolution fusion | flops 3224371200 | bytes 29360128 | tf_op jit(solution)/shard_map/tsd,doc->tosc/dot_general | solution.py:110
  449.8 11.2 %bitcast_add_fusion = f32[8,256,1536]{2,1,0:T(8,128)} fusion(f32[4,256,2,1536]{3,1,2,0:T(8,128)} %convolution_add_fusion, f32[8,1536]{1,0:T(8,128)S(1)} %broadcast_select_fusion.2), kind=kLoop, calls=%fused_computation.10 | loop fusion | flops 3145728 | bytes 25214976 | tf_op jit(solution)/shard_map/add | solution.py:119
  461.1 90.8 %reduce-scatter.8.cloned.1.call-done = f32[1,256,1536]{2,1,0:T(8,128)} async-done(((f32[8,256,1536]{2,1,0:T(8,128)}), f32[1,256,1536]{2,1,0:T(8,128)}) %reduce-scatter.8.cloned.1.call-update) | async-done | bytes 1572880 | tf_op jit(solution)/shard_map/reduce_scatter | solution.py:120
  (58 shorter events, 12.5 us)
Async XLA Ops:
  6.5 15.2 %all-gather.4.cloned.1.call-start = ((), (), s32[]{:S(2)}) async-start(), calls=%async_computation.3 | async-start | bytes 2359296 | tf_op jit(solution)/shard_map/all_gather | solution.py:46
  7.3 181.7 %reduce-scatter.4.cloned.1.call-start = ((), (), s32[]{:S(2)}) async-start(), calls=%async_computation.4 | async-start | bytes 15728640 | tf_op jit(solution)/shard_map/reduce_scatter | solution.py:96
  23.2 13.0 %collective-permute-start = (bf16[256,768]{1,0:T(8,128)(2,1)S(1)}, bf16[256,768]{1,0:T(8,128)(2,1)S(1)}, u32[]{:S(2)}, u32[]{:S(2)}) collective-permute-start(bf16[256,768]{1,0:T(8,128)(2,1)S(1)} %get-tuple-element.25), channel_id=1, source_target_pairs={{0,8},{8,0},{16,24},{24,16},{1,9},{9,1},{17,25},{25,17},{2,10},{10... | collective-permute-start | bytes 1179656 | tf_op jit(solution)/shard_map/ppermute | solution.py:53
  26.2 19.0 %collective-permute-start.1 = (bf16[256,768]{1,0:T(8,128)(2,1)S(1)}, bf16[256,768]{1,0:T(8,128)(2,1)S(1)}, u32[]{:S(2)}, u32[]{:S(2)}) collective-permute-start(bf16[256,768]{1,0:T(8,128)(2,1)S(1)} %get-tuple-element.24), channel_id=1, source_target_pairs={{0,16},{8,24},{16,0},{24,8},{1,17},{9,25},{17,1},{25,9},{2,18},{10... | collective-permute-start | bytes 1179656 | tf_op jit(solution)/shard_map/ppermute | solution.py:53
  27.8 17.5 %collective-permute-start.2 = (bf16[256,768]{1,0:T(8,128)(2,1)S(1)}, bf16[256,768]{1,0:T(8,128)(2,1)S(1)}, u32[]{:S(2)}, u32[]{:S(2)}) collective-permute-start(bf16[256,768]{1,0:T(8,128)(2,1)S(1)} %get-tuple-element.23), channel_id=1, source_target_pairs={{0,24},{8,16},{16,8},{24,0},{1,25},{9,17},{17,9},{25,1},{2,26},{10... | collective-permute-start | bytes 1179656 | tf_op jit(solution)/shard_map/ppermute | solution.py:53
  49.7 17.9 %copy-start.1 = (bf16[4,256,768]{2,1,0:T(8,128)(2,1)}, bf16[4,256,768]{2,1,0:T(8,128)(2,1)S(1)}, u32[]{:S(2)}) copy-start(bf16[4,256,768]{2,1,0:T(8,128)(2,1)S(1)} %broadcast_select_fusion) | copy-start | bytes 4718596
  67.7 1.7 copy-start
  67.7 245.1 %reduce-scatter.6.cloned.1.call-start = ((), (), s32[]{:S(2)}) async-start(), calls=%async_computation.6 | async-start | bytes 15728640 | tf_op jit(solution)/shard_map/reduce_scatter | solution.py:96
  86.4 310.4 %all-gather.6.cloned.1.call-start = ((), (), s32[]{:S(2)}) async-start(), calls=%async_computation.5 | async-start | bytes 1310720 | tf_op jit(solution)/shard_map/all_gather | solution.py:109
  86.5 108.7 %collective-permute-start.6 = (s32[1]{0:T(128)}, s32[1]{0:T(128)}, u32[]{:S(2)}, u32[]{:S(2)}) collective-permute-start(s32[1]{0:T(128)} %param.9), channel_id=1, source_target_pairs={{0,0},{2,8},{4,16},{6,24},{8,2},{10,10},{12,18},{14,26},{16,4},{18... | collective-permute-start | bytes 20 | tf_op jit(solution)/shard_map/ppermute | solution.py:73
  190.7 129.0 %collective-permute-start.3 = (bf16[256,1536]{1,0:T(8,128)(2,1)S(1)}, bf16[256,1536]{1,0:T(8,128)(2,1)}, u32[]{:S(2)}, u32[]{:S(2)}) collective-permute-start(bf16[256,1536]{1,0:T(8,128)(2,1)S(1)} %get-tuple-element.19), channel_id=1, source_target_pairs={{0,2},{2,0},{4,6},{6,4},{1,3},{3,1},{5,7},{7,5},{8,10},{10,8},{12,... | collective-permute-start | bytes 2359304 | tf_op jit(solution)/shard_map/ppermute | solution.py:101
  192.2 127.9 %collective-permute-start.4 = (bf16[256,1536]{1,0:T(8,128)(2,1)S(1)}, bf16[256,1536]{1,0:T(8,128)(2,1)}, u32[]{:S(2)}, u32[]{:S(2)}) collective-permute-start(bf16[256,1536]{1,0:T(8,128)(2,1)S(1)} %get-tuple-element.21), channel_id=1, source_target_pairs={{0,4},{2,6},{4,0},{6,2},{1,5},{3,7},{5,1},{7,3},{8,12},{10,14},{12... | collective-permute-start | bytes 2359304 | tf_op jit(solution)/shard_map/ppermute | solution.py:101
  194.7 125.5 %collective-permute-start.5 = (bf16[256,1536]{1,0:T(8,128)(2,1)S(1)}, bf16[256,1536]{1,0:T(8,128)(2,1)}, u32[]{:S(2)}, u32[]{:S(2)}) collective-permute-start(bf16[256,1536]{1,0:T(8,128)(2,1)S(1)} %get-tuple-element.20), channel_id=1, source_target_pairs={{0,6},{2,4},{4,2},{6,0},{1,7},{3,5},{5,3},{7,1},{8,14},{10,12},{12... | collective-permute-start | bytes 2359304 | tf_op jit(solution)/shard_map/ppermute | solution.py:101
  315.8 47.2 %collective-permute-start.7 = (bf16[256,1536]{1,0:T(8,128)(2,1)}, bf16[256,1536]{1,0:T(8,128)(2,1)}, u32[]{:S(2)}, u32[]{:S(2)}) collective-permute-start(bf16[256,1536]{1,0:T(8,128)(2,1)} %get-tuple-element.16), channel_id=1, source_target_pairs={{0,2},{2,0},{4,6},{6,4},{1,3},{3,1},{5,7},{7,5},{8,10},{10,8},{12,... | collective-permute-start | bytes 2359304 | tf_op jit(solution)/shard_map/ppermute | solution.py:101
  317.2 63.7 %collective-permute-start.8 = (bf16[256,1536]{1,0:T(8,128)(2,1)}, bf16[256,1536]{1,0:T(8,128)(2,1)}, u32[]{:S(2)}, u32[]{:S(2)}) collective-permute-start(bf16[256,1536]{1,0:T(8,128)(2,1)} %get-tuple-element.18), channel_id=1, source_target_pairs={{0,4},{2,6},{4,0},{6,2},{1,5},{3,7},{5,1},{7,3},{8,12},{10,14},{12... | collective-permute-start | bytes 2359304 | tf_op jit(solution)/shard_map/ppermute | solution.py:101
  319.7 61.2 %collective-permute-start.9 = (bf16[256,1536]{1,0:T(8,128)(2,1)S(1)}, bf16[256,1536]{1,0:T(8,128)(2,1)}, u32[]{:S(2)}, u32[]{:S(2)}) collective-permute-start(bf16[256,1536]{1,0:T(8,128)(2,1)S(1)} %get-tuple-element.17), channel_id=1, source_target_pairs={{0,6},{2,4},{4,2},{6,0},{1,7},{3,5},{5,3},{7,1},{8,14},{10,12},{12... | collective-permute-start | bytes 2359304 | tf_op jit(solution)/shard_map/ppermute | solution.py:101
  324.7 113.3 %all-gather.8.cloned.1.call-start = ((), (), s32[]{:S(2)}) async-start(), calls=%async_computation.7 | async-start | bytes 1310720 | tf_op jit(solution)/shard_map/all_gather | solution.py:109
  385.5 166.4 %reduce-scatter.8.cloned.1.call-start = ((), (), s32[]{:S(2)}) async-start(), calls=%async_computation.8 | async-start | bytes 14155776 | tf_op jit(solution)/shard_map/reduce_scatter | solution.py:120
  393.5 3.2 copy-start.2
Sparse Core Ops, SparseCore 0:
  8.9 12.4 all-gather.3
  67.8 121.0 reduce-scatter.3
  192.0 120.7 reduce-scatter.5
  324.8 70.7 all-gather.5
  397.0 40.9 all-gather.7
  461.2 90.6 reduce-scatter.7
